TPU v7x, 128 devices: a whole 4x4x4 slice. The times are simulated.
128 devices in a mesh: ord: 16 (over x, y_lo, core), lat: 8 (over z, y_hi).
Axes of the slice: x: 4, y: 4 (y_hi: 2, y_lo: 2; y = y_hi * 2 + y_lo), z: 4, core: 2. Of those that a mesh axis runs over, the one named last changes fastest.
Arguments:
- grad_coef: bfloat16 [768, 768, 256], P(('ord', 'lat')), may hold values from -6 to 6
- legendre: bfloat16 [768, 256, 768], P('ord', 'lat'), may hold values from -0.0078125 to 0.0078125
- quad_weight: float32 [256], P('lat'), may hold values from 0.3 to 1
- slot_order: int32 [768], replicated, may hold values from 0 to 767, as said below
- slot_count: int32 [768], P('ord'), may hold values from 0 to 721, as said below
- conv_input: bfloat16 [256, 128, 1440], P(('lat', 'ord')), may hold values from -6 to 6
- depth_kernel: float32 [128, 25], replicated, may hold values from -1.25 to 1.25
- point_weight: bfloat16 [128, 128], replicated, may hold values from -0.5 to 0.5
Outputs:
- grad_input: bfloat16 [256, 128, 1440], P(('lat', 'ord'))
- grad_point: float32 [128, 128], replicated
- grad_depth: float32 [128, 25], replicated
Inputs may be any that keep to these rules, and one draw needn't show every extreme that they name: `slot_order`: a permutation of 0 to 767; slots g*48 to (g+1)*48 - 1 hold the orders of one aligned block of 48 orders, in some order. `slot_count`: 721 minus the slot's order in slot_order, or 0 where that is negative.
All inputs are finite; a program needn't handle non-finite values.
Results may differ from a plain program's by a relative error of at most 0.0068.
Values may be sent and summed in bfloat16 or wider, within the bound.
No kernel may reach another device: no remote copies, remote signals or barrier semaphores. Data moves between devices by JAX's collectives and lax.ppermute only.
A program may use at most 192 MiB of HBM per device.

v0:
```python
import math

import jax
import jax.numpy as jnp
from jax import lax
from jax.sharding import PartitionSpec as P


def padded(block, sides, width):
    for axis, dim in sides:
        count = lax.axis_size(axis)
        forward = [(i, i + 1) for i in range(count - 1)]
        forward.append((count - 1, 0))
        backward = [(target, source) for source, target in forward]
        low = lax.ppermute(
            lax.slice_in_dim(block, block.shape[dim] - width, None, axis=dim), axis, forward
        )
        high = lax.ppermute(lax.slice_in_dim(block, 0, width, axis=dim), axis, backward)
        block = jnp.concatenate([low, block, high], axis=dim)
    return block


def passed_along(value, axis, steps):
    count = lax.axis_size(axis)
    leading, last = (max(0, -steps), min(count, count - steps))
    return lax.ppermute(value, axis, [(source, source + steps) for source in range(leading, last)])


def make_table(orders, length):
    lon_ids = jnp.arange(length, dtype=jnp.int32)
    residue = orders[:, None] * lon_ids[None, :] % length
    angles = residue.astype(jnp.float32) * (2.0 * math.pi / length)
    factor = jnp.where((orders == 0) | (2 * orders == length), 1.0, 2.0).astype(jnp.float32)[
        :, None
    ]
    return jnp.stack([factor * jnp.cos(angles), -factor * jnp.sin(angles)], axis=1).astype(
        jnp.bfloat16
    )


def inverse_lon(spec_rows, dft_table):
    slots_here, rows_here, doubled = spec_rows.shape
    paired = spec_rows.reshape(slots_here, rows_here, doubled // 2, 2)
    return jnp.einsum("srcp,spf->rcf", paired, dft_table, preferred_element_type=jnp.float32)


def with_rims(field):
    extended = padded(field, (("ord", 0),), 2)
    upper_rim = extended[:2]
    lower_rim = extended[-2:]
    upper_band = passed_along(upper_rim, "lat", 1)
    lower_band = passed_along(lower_rim, "lat", -1)
    position = lax.axis_index("ord")
    upper_rim = jnp.where(position == 0, upper_band, upper_rim)
    lower_rim = jnp.where(position == lax.axis_size("ord") - 1, lower_band, lower_rim)
    return jnp.concatenate([upper_rim, field, lower_rim], axis=0)


def shards(
    grad_coef, legendre, quad_weight, slot_order, slot_count, conv_input, depth_kernel, point_weight
):
    group_slots, band_rows, degrees = legendre.shape
    row_count, channels, longitudes = conv_input.shape
    portion = lax.all_gather(grad_coef, "lat", axis=0, tiled=True)
    is_valid = jnp.arange(degrees, dtype=jnp.int32)[None, :] < slot_count[:, None]
    masked = portion * is_valid[:, :, None].astype(portion.dtype)
    summed = jnp.einsum("slj,sjk->slk", legendre, masked, preferred_element_type=jnp.float32)
    spectral = (summed * quad_weight[None, :, None]).astype(jnp.bfloat16)
    own_start = lax.axis_index("ord") * row_count
    own_rows = lax.dynamic_slice_in_dim(
        lax.all_gather(spectral, "ord", axis=0, tiled=True), own_start, row_count, 1
    )
    grad_grid = inverse_lon(own_rows, make_table(slot_order, longitudes))
    grad_grid = grad_grid.astype(jnp.bfloat16)
    x_wide = with_rims(conv_input).astype(jnp.float32)
    hidden = jnp.zeros((row_count, channels, longitudes), jnp.float32)
    for tap_row in range(5):
        for tap_col in range(5):
            weight_tap = depth_kernel[:, 5 * tap_row + tap_col][None, :, None]
            hidden = hidden + weight_tap * jnp.roll(
                x_wide[tap_row : tap_row + row_count], 2 - tap_col, axis=2
            )
    hidden = hidden.astype(jnp.bfloat16)
    grad_hidden = jnp.einsum(
        "cd,rdf->rcf", point_weight, grad_grid, preferred_element_type=jnp.float32
    ).astype(jnp.bfloat16)
    point_part = jnp.einsum("rcf,rdf->cd", hidden, grad_grid, preferred_element_type=jnp.float32)
    padded_grad = with_rims(grad_hidden).astype(jnp.float32)
    hidden_wide = grad_hidden.astype(jnp.float32)
    grad_input = jnp.zeros((row_count, channels, longitudes), jnp.float32)
    depth_terms = []
    for tap_row in range(5):
        for tap_col in range(5):
            weight_tap = depth_kernel[:, 5 * tap_row + tap_col][None, :, None]
            grad_input = grad_input + weight_tap * jnp.roll(
                padded_grad[4 - tap_row : 4 - tap_row + row_count], tap_col - 2, axis=2
            )
            shifted_x = jnp.roll(x_wide[tap_row : tap_row + row_count], 2 - tap_col, axis=2)
            depth_terms.append(jnp.sum(hidden_wide * shifted_x, axis=(0, 2)))
    depth_part = jnp.stack(depth_terms, axis=1)
    point_sum, depth_sum = lax.psum((point_part, depth_part), ("ord", "lat"))
    total_rows = row_count * lax.axis_size("ord") * lax.axis_size("lat")
    grad_scale = 1.0 / math.sqrt(total_rows * longitudes)
    return (grad_input.astype(jnp.bfloat16), point_sum * grad_scale, depth_sum * grad_scale)


def solution(mesh):
    return jax.shard_map(
        shards,
        mesh=mesh,
        in_specs=(
            P(("ord", "lat"), None, None),
            P("ord", "lat", None),
            P("lat"),
            P(),
            P("ord"),
            P(("lat", "ord"), None, None),
            P(),
            P(),
        ),
        out_specs=(P(("lat", "ord"), None, None), P(), P()),
        check_vma=False,
    )
```

profile of v0, /device:TPU:1, one launch (start us, length us, event | category | flops | bytes accessed | tf_op | source)
XLA Modules:
  0.0 568.1 jit_solution(15556947004917034212)
XLA Ops:
  7.2 0.0 all-gather.3.cloned.1.call-start
  7.2 0.7 all-gather.3.cloned.1.call-update
  7.9 0.0 all-gather.5.cloned.1.call-start
  8.0 0.1 fusion.70
  8.1 206.0 %all-gather.3.cloned.1.call-done = bf16[48,768,256]{2,1,0:T(8,128)(2,1)} async-done(((bf16[6,768,256]{2,1,0:T(8,128)(2,1)}), bf16[48,768,256]{2,1,0:T(8,128)(2,1)}) %all-gather.3.cloned.1.call-update) | async-done | bytes 18874384 | tf_op jit(solution)/shard_map/all_gather | solution.py:64
  214.2 11.0 %fusion.66 = bf16[48,32,256]{2,1,0:T(8,128)(2,1)} fusion(bf16[48,32,768]{2,1,0:T(8,128)(2,1)S(1)} %copy-done, bf16[48,768,256]{2,1,0:T(8,128)(2,1)} %all-gather.3.cloned.1.call-done, bf16[48,768]{1,0:T(8,128)(2,1)S(1)} %fusion.70, f32[32]{0:T(128)S(1)} %copy-done.24), kind=kOutput, calls=%fused_computation.144 | convolution fusion | flops 642514944 | bytes 22093952 | tf_op jit(solution)/shard_map/slj,sjk->slk/dot_general | solution.py:67
  225.2 0.0 all-gather.5.cloned.1.call-update
  225.2 0.0 all-reduce.2.cloned.1.call-start
  225.3 1.7 collective-permute-start.4
  227.0 27.1 %collective-permute-done.4 = bf16[2,128,1440]{1,2,0:T(8,128)(2,1)S(1)} collective-permute-done((bf16[2,128,1440]{1,2,0:T(8,128)(2,1)S(1)}, bf16[2,128,1440]{1,2,0:T(8,128)(2,1)S(1)}, u32[]{:S(2)}, u32[]{:S(2)}) %collective-permute-start.4) | collective-permute-done | bytes 737312 | tf_op jit(solution)/shard_map/ppermute | solution.py:15
  254.1 8.1 %collective-permute-start.5 = (bf16[2,128,1440]{1,2,0:T(8,128)(2,1)S(1)}, bf16[2,128,1440]{1,2,0:T(8,128)(2,1)S(1)}, u32[]{:S(2)}, u32[]{:S(2)}) collective-permute-start(bf16[2,128,1440]{1,2,0:T(8,128)(2,1)S(1)} %collective-permute-done.4), channel_id=1, source_target_pairs={{0,1},{1,2},{2,3},{3,4},{4,5},{5,6},{6,7},{8,9},{9,10},{10,11},{11... | collective-permute-start | bytes 2211848 | tf_op jit(solution)/shard_map/ppermute | solution.py:26
  262.2 20.0 %multiply_convert_fusion.1 = (bf16[768,1,1440]{0,2,1:T(8,128)(2,1)}, bf16[768,1,1440]{0,2,1:T(8,128)(2,1)}) fusion(s32[768]{0:T(1024)S(1)} %copy-done.20, f32[768]{0:T(1024)S(1)} %get-tuple-element.135, f32[768]{0:T(1024)S(1)} %get-tuple-element.136), kind=kLoop, calls=%fused_computation.36 | loop fusion | flops 14376960 | bytes 4432896 | tf_op jit(solution)/shard_map/convert
  282.2 1.3 collective-permute-start.7
  283.5 5.6 collective-permute-done.5
  289.1 0.1 broadcast_select_fusion.2
  289.1 32.6 %collective-permute-done.7 = bf16[2,128,1440]{1,2,0:T(8,128)(2,1)S(1)} collective-permute-done((bf16[2,128,1440]{1,2,0:T(8,128)(2,1)S(1)}, bf16[2,128,1440]{1,2,0:T(8,128)(2,1)S(1)}, u32[]{:S(2)}, u32[]{:S(2)}) %collective-permute-start.7) | collective-permute-done | bytes 737312 | tf_op jit(solution)/shard_map/ppermute | solution.py:26
  321.8 0.1 broadcast_select_fusion
  321.9 2.3 maximum_convert_fusion.1
  324.2 10.3 %fusion.78 = (f32[2,128,1439]{1,2,0:T(8,128)S(1)}, f32[2,128,1439]{1,2,0:T(8,128)}, f32[2,128,1439]{1,2,0:T(8,128)}, f32[2,128,1439]{1,2,0:T(8,128)}, f32[2,128,...) fusion(f32[6,128,1440]{1,2,0:T(8,128)} %maximum_convert_fusion.1), kind=kLoop, calls=%fused_computation.229 | loop fusion | bytes 29470720 | tf_op jit(solution)/shard_map/jit(_roll_static)/slice | solution.py:80
  334.6 10.8 %fusion.77 = (f32[2,128,1438]{1,2,0:T(8,128)}, f32[2,128,1438]{1,2,0:T(8,128)}, f32[2,128,1438]{1,2,0:T(8,128)}, f32[2,128,1438]{1,2,0:T(8,128)}, f32[2,128,1438...) fusion(f32[6,128,1440]{1,2,0:T(8,128)} %maximum_convert_fusion.1), kind=kLoop, calls=%fused_computation.228 | loop fusion | bytes 29450240 | tf_op jit(solution)/shard_map/jit(_roll_static)/slice | solution.py:80
  345.4 2.7 constant_dynamic-slice_fusion
  348.1 2.4 copy.13
  350.5 4.0 fusion.12
  354.5 0.2 copy-done.18
  354.7 0.4 copy-done.19
  355.1 1.5 fusion.36
  356.6 0.1 collective-permute-start.2
  356.7 4.5 collective-permute-start
  361.2 13.0 %convolution_bitcast_fusion = f32[128,128]{1,0:T(8,128)} fusion(bf16[2,128,1440]{1,2,0:T(8,128)(2,1)S(1)} %fusion.12, f32[6,128,1440]{1,2,0:T(8,128)S(1)} %bitcast.103, f32[2,128,1]{1,2,0:T(1,128)S(1)} %get-tuple-element.79, f32[2,128,1439]{1,2,0:T(8,128)} %get-tuple-element.45, f32[2,128,1439]{1,2,0:T(8,128)} %get-tuple-element.44, ...), kind=kOutput, calls=%fused_computation.145 | convolution fusion | flops 120176640 | bytes 37689856 | tf_op jit(solution)/shard_map/rcf,rdf->cd/dot_general | solution.py:87
  374.2 0.0 all-reduce.2.cloned.1.call-update
  374.3 5.3 fusion.38
  379.7 1.6 collective-permute-start.3
  381.3 0.4 copy-done.15
  381.7 0.4 copy-done.16
  382.1 0.4 copy-done.17
  382.5 1.8 fusion.37
  384.3 0.1 stack.110
  384.4 74.2 %psum.15 = f32[128,25]{0,1:T(8,128)S(1)} all-reduce(f32[128,25]{0,1:T(8,128)S(1)} %stack.110), channel_id=1, replica_groups=mesh['ord'=16,'lat'=8] {'ord','lat'}, use_global_device_ids=true, to_apply=%region_26.27 | all-reduce | flops 3200 | bytes 25600 | tf_op jit(solution)/shard_map/psum | solution.py:101
  458.6 0.6 broadcast_multiply_fusion.1
  459.2 3.8 collective-permute-start.1
  463.0 56.5 %all-reduce.2.cloned.1.call-done = f32[128,128]{1,0:T(8,128)} async-done(((f32[128,128]{1,0:T(8,128)}), f32[128,128]{1,0:T(8,128)}) %all-reduce.2.cloned.1.call-update) | async-done | bytes 65552 | tf_op jit(solution)/shard_map/psum | solution.py:101
  519.6 1.5 broadcast_multiply_fusion
  521.0 1.2 broadcast_select_fusion.1
  522.2 0.1 broadcast_select_fusion.3
  522.4 2.4 maximum_convert_fusion
  524.8 10.6 %fusion.80 = (f32[2,128,1439]{1,2,0:T(8,128)}, f32[2,128,1439]{1,2,0:T(8,128)}, f32[2,128,1439]{1,2,0:T(8,128)}, f32[2,128,1439]{1,2,0:T(8,128)}, f32[2,128,1439...) fusion(f32[6,128,1440]{1,2,0:T(8,128)} %maximum_convert_fusion), kind=kLoop, calls=%fused_computation.231 | loop fusion | bytes 29470720 | tf_op jit(solution)/shard_map/jit(_roll_static)/slice | solution.py:95
  535.3 10.7 %fusion.79 = (f32[2,128,1438]{1,2,0:T(8,128)}, f32[2,128,1438]{1,2,0:T(8,128)}, f32[2,128,1438]{1,2,0:T(8,128)}, f32[2,128,1438]{1,2,0:T(8,128)}, f32[2,128,1438...) fusion(f32[6,128,1440]{1,2,0:T(8,128)} %maximum_convert_fusion), kind=kLoop, calls=%fused_computation.230 | loop fusion | bytes 29450240 | tf_op jit(solution)/shard_map/jit(_roll_static)/slice | solution.py:95
  546.1 15.5 %fusion.42 = bf16[2,128,1440]{1,2,0:T(8,128)(2,1)} fusion(f32[6,128,1440]{1,2,0:T(8,128)} %maximum_convert_fusion, f32[2,128,2]{1,2,0:T(2,128)S(1)} %get-tuple-element.103, f32[2,128,1438]{1,2,0:T(8,128)} %get-tuple-element.57, f32[2,128,1]{1,2,0:T(1,128)S(1)} %get-tuple-element.107, f32[2,128,1439]{1,2,0:T(8,128)} %get-tuple-element.67, ...), kind=kLoop, calls=%fused_computation.77 | loop fusion | flops 25804800 | bytes 37614080 | tf_op jit(solution)/shard_map/convert_element_type | solution.py:104
  (68 shorter events, 0.2 us)
Async XLA Ops:
  7.2 207.0 %copy-start = (bf16[48,32,768]{2,1,0:T(8,128)(2,1)S(1)}, bf16[48,32,768]{2,1,0:T(8,128)(2,1)}, u32[]{:S(2)}) copy-start(bf16[48,32,768]{2,1,0:T(8,128)(2,1)} %param.9) | copy-start | bytes 7077892
  7.2 0.8 copy-start.22
  7.2 207.0 %copy-start.24 = (f32[32]{0:T(128)S(1)}, f32[32]{0:T(128)}, u32[]{:S(2)}) copy-start(f32[32]{0:T(128)} %param.10) | copy-start | bytes 388
  7.2 207.0 %all-gather.3.cloned.1.call-start = ((), (), s32[]{:S(2)}) async-start(), calls=%async_computation | async-start | bytes 21233664 | tf_op jit(solution)/shard_map/all_gather | solution.py:64
  7.9 337.4 %all-gather.5.cloned.1.call-start = ((), (), s32[]{:S(2)}) async-start(), calls=%async_computation.1 | async-start | bytes 13369344 | tf_op jit(solution)/shard_map/all_gather | solution.py:71
  8.1 217.2 %copy-start.2 = (bf16[2,128,1440]{1,2,0:T(8,128)(2,1)S(1)}, bf16[2,128,1440]{1,2,0:T(8,128)(2,1)}, u32[]{:S(2)}) copy-start(bf16[2,128,1440]{1,2,0:T(8,128)(2,1)} %param.13) | copy-start | bytes 2211844
  8.1 218.9 %copy-start.21 = (f32[128,25]{0,1:T(8,128)S(1)}, f32[128,25]{0,1:T(8,128)}, u32[]{:S(2)}) copy-start(f32[128,25]{0,1:T(8,128)} %param.14) | copy-start | bytes 38404
  8.1 218.9 %copy-start.20 = (s32[768]{0:T(1024)S(1)}, s32[768]{0:T(1024)}, u32[]{:S(2)}) copy-start(s32[768]{0:T(1024)} %param.11) | copy-start | bytes 9220
  225.2 294.3 %all-reduce.2.cloned.1.call-start = ((), (), s32[]{:S(2)}) async-start(), calls=%async_computation.2 | async-start | bytes 131072 | tf_op jit(solution)/shard_map/psum | solution.py:101
  225.3 28.8 %collective-permute-start.4 = (bf16[2,128,1440]{1,2,0:T(8,128)(2,1)S(1)}, bf16[2,128,1440]{1,2,0:T(8,128)(2,1)S(1)}, u32[]{:S(2)}, u32[]{:S(2)}) collective-permute-start(bf16[2,128,1440]{1,2,0:T(8,128)(2,1)S(1)} %copy-done.2), channel_id=1, source_target_pairs={{0,8},{8,16},{16,24},{24,32},{32,40},{40,48},{48,56},{56,64},{64,7... | collective-permute-start | bytes 2211848 | tf_op jit(solution)/shard_map/ppermute | solution.py:15
  226.9 55.2 %collective-permute-start.6 = (bf16[2,128,1440]{1,2,0:T(8,128)(2,1)S(1)}, bf16[2,128,1440]{1,2,0:T(8,128)(2,1)S(1)}, u32[]{:S(2)}, u32[]{:S(2)}) collective-permute-start(bf16[2,128,1440]{1,2,0:T(8,128)(2,1)S(1)} %copy-done.2), channel_id=1, source_target_pairs={{8,0},{16,8},{24,16},{32,24},{40,32},{48,40},{56,48},{64,56},{72,6... | collective-permute-start | bytes 2211848 | tf_op jit(solution)/shard_map/ppermute | solution.py:18
  254.1 35.0 %collective-permute-start.5 = (bf16[2,128,1440]{1,2,0:T(8,128)(2,1)S(1)}, bf16[2,128,1440]{1,2,0:T(8,128)(2,1)S(1)}, u32[]{:S(2)}, u32[]{:S(2)}) collective-permute-start(bf16[2,128,1440]{1,2,0:T(8,128)(2,1)S(1)} %collective-permute-done.4), channel_id=1, source_target_pairs={{0,1},{1,2},{2,3},{3,4},{4,5},{5,6},{6,7},{8,9},{9,10},{10,11},{11... | collective-permute-start | bytes 2211848 | tf_op jit(solution)/shard_map/ppermute | solution.py:26
  282.2 39.6 %collective-permute-start.7 = (bf16[2,128,1440]{1,2,0:T(8,128)(2,1)S(1)}, bf16[2,128,1440]{1,2,0:T(8,128)(2,1)S(1)}, u32[]{:S(2)}, u32[]{:S(2)}) collective-permute-start(bf16[2,128,1440]{1,2,0:T(8,128)(2,1)S(1)} %collective-permute-done.6), channel_id=1, source_target_pairs={{1,0},{2,1},{3,2},{4,3},{5,4},{6,5},{7,6},{9,8},{10,9},{11,10},{12... | collective-permute-start | bytes 2211848 | tf_op jit(solution)/shard_map/ppermute | solution.py:26
  348.1 6.3 %slice-start = ((s8[4423680]{0:T(1024)(128)(4,1)}), s8[229376]{0:T(1024)(128)(4,1)S(1)}, s32[]{:S(2)}) async-start(s8[4423680]{0:T(1024)(128)(4,1)} %bitcast.102), calls=%async_computation.3 | async-start | bytes 458752
  350.5 4.0 slice-start.1
  350.5 4.2 copy-start.18
  350.5 4.6 copy-start.19
  350.5 4.6 copy-start.23
  355.1 6.1 %copy-start.3 = (f32[2,128,1439]{1,2,0:T(8,128)S(1)}, f32[2,128,1439]{1,2,0:T(8,128)}, u32[]{:S(2)}) copy-start(f32[2,128,1439]{1,2,0:T(8,128)} %get-tuple-element.42) | copy-start | bytes 4420612
  355.1 6.1 %copy-start.4 = (f32[2,128,1439]{1,2,0:T(8,128)S(1)}, f32[2,128,1439]{1,2,0:T(8,128)}, u32[]{:S(2)}) copy-start(f32[2,128,1439]{1,2,0:T(8,128)} %get-tuple-element.43) | copy-start | bytes 4420612
  355.1 6.1 %copy-start.5 = (f32[2,128,1439]{1,2,0:T(8,128)S(1)}, f32[2,128,1439]{1,2,0:T(8,128)}, u32[]{:S(2)}) copy-start(f32[2,128,1439]{1,2,0:T(8,128)} %get-tuple-element.47) | copy-start | bytes 4420612
  355.1 6.1 %copy-start.6 = (f32[2,128,1438]{1,2,0:T(8,128)S(1)}, f32[2,128,1438]{1,2,0:T(8,128)}, u32[]{:S(2)}) copy-start(f32[2,128,1438]{1,2,0:T(8,128)} %get-tuple-element.29) | copy-start | bytes 4417540
  355.1 6.1 %copy-start.7 = (f32[2,128,1438]{1,2,0:T(8,128)S(1)}, f32[2,128,1438]{1,2,0:T(8,128)}, u32[]{:S(2)}) copy-start(f32[2,128,1438]{1,2,0:T(8,128)} %get-tuple-element.32) | copy-start | bytes 4417540
  355.1 6.1 %copy-start.8 = (f32[2,128,1438]{1,2,0:T(8,128)S(1)}, f32[2,128,1438]{1,2,0:T(8,128)}, u32[]{:S(2)}) copy-start(f32[2,128,1438]{1,2,0:T(8,128)} %get-tuple-element.34) | copy-start | bytes 4417540
  356.6 23.0 %collective-permute-start.2 = (bf16[2,128,1440]{1,2,0:T(8,128)(2,1)S(1)}, bf16[2,128,1440]{1,2,0:T(8,128)(2,1)}, u32[]{:S(2)}, u32[]{:S(2)}) collective-permute-start(bf16[2,128,1440]{1,2,0:T(8,128)(2,1)S(1)} %get-tuple-element.137), channel_id=1, source_target_pairs={{8,0},{16,8},{24,16},{32,24},{40,32},{48,40},{56,48},{64,56},{72,6... | collective-permute-start | bytes 2211848 | tf_op jit(solution)/shard_map/ppermute | solution.py:18
  356.7 102.5 %collective-permute-start = (bf16[2,128,1440]{1,2,0:T(8,128)(2,1)S(1)}, bf16[2,128,1440]{1,2,0:T(8,128)(2,1)S(1)}, u32[]{:S(2)}, u32[]{:S(2)}) collective-permute-start(bf16[2,128,1440]{1,2,0:T(8,128)(2,1)S(1)} %get-tuple-element.137), channel_id=1, source_target_pairs={{0,8},{8,16},{16,24},{24,32},{32,40},{40,48},{48,56},{56,64},{64,7... | collective-permute-start | bytes 2211848 | tf_op jit(solution)/shard_map/ppermute | solution.py:15
  374.2 7.0 %copy-start.9 = (f32[2,128,1439]{1,2,0:T(8,128)S(1)}, f32[2,128,1439]{1,2,0:T(8,128)}, u32[]{:S(2)}) copy-start(f32[2,128,1439]{1,2,0:T(8,128)} %get-tuple-element.39) | copy-start | bytes 4420612
  374.3 7.0 %copy-start.10 = (f32[2,128,1439]{1,2,0:T(8,128)S(1)}, f32[2,128,1439]{1,2,0:T(8,128)}, u32[]{:S(2)}) copy-start(f32[2,128,1439]{1,2,0:T(8,128)} %get-tuple-element.40) | copy-start | bytes 4420612
  374.3 7.0 %copy-start.11 = (f32[2,128,1439]{1,2,0:T(8,128)S(1)}, f32[2,128,1439]{1,2,0:T(8,128)}, u32[]{:S(2)}) copy-start(f32[2,128,1439]{1,2,0:T(8,128)} %get-tuple-element.41) | copy-start | bytes 4420612
  374.3 7.0 %copy-start.12 = (f32[2,128,1439]{1,2,0:T(8,128)S(1)}, f32[2,128,1439]{1,2,0:T(8,128)}, u32[]{:S(2)}) copy-start(f32[2,128,1439]{1,2,0:T(8,128)} %get-tuple-element.45) | copy-start | bytes 4420612
  374.3 7.0 %copy-start.13 = (f32[2,128,1439]{1,2,0:T(8,128)S(1)}, f32[2,128,1439]{1,2,0:T(8,128)}, u32[]{:S(2)}) copy-start(f32[2,128,1439]{1,2,0:T(8,128)} %get-tuple-element.46) | copy-start | bytes 4420612
  374.3 7.0 %copy-start.14 = (f32[2,128,1438]{1,2,0:T(8,128)S(1)}, f32[2,128,1438]{1,2,0:T(8,128)}, u32[]{:S(2)}) copy-start(f32[2,128,1438]{1,2,0:T(8,128)} %get-tuple-element.30) | copy-start | bytes 4417540
  374.3 7.4 %copy-start.15 = (f32[2,128,1438]{1,2,0:T(8,128)S(1)}, f32[2,128,1438]{1,2,0:T(8,128)}, u32[]{:S(2)}) copy-start(f32[2,128,1438]{1,2,0:T(8,128)} %get-tuple-element.31) | copy-start | bytes 4417540
  374.3 7.8 %copy-start.16 = (f32[2,128,1438]{1,2,0:T(8,128)S(1)}, f32[2,128,1438]{1,2,0:T(8,128)}, u32[]{:S(2)}) copy-start(f32[2,128,1438]{1,2,0:T(8,128)} %get-tuple-element.33) | copy-start | bytes 4417540
  374.3 8.2 %copy-start.17 = (f32[2,128,1438]{1,2,0:T(8,128)S(1)}, f32[2,128,1438]{1,2,0:T(8,128)}, u32[]{:S(2)}) copy-start(f32[2,128,1438]{1,2,0:T(8,128)} %get-tuple-element.37) | copy-start | bytes 4417540
  379.7 141.4 %collective-permute-start.3 = (bf16[2,128,1440]{1,2,0:T(8,128)(2,1)}, bf16[2,128,1440]{1,2,0:T(8,128)(2,1)S(1)}, u32[]{:S(2)}, u32[]{:S(2)}) collective-permute-start(bf16[2,128,1440]{1,2,0:T(8,128)(2,1)} %collective-permute-done.2), channel_id=1, source_target_pairs={{1,0},{2,1},{3,2},{4,3},{5,4},{6,5},{7,6},{9,8},{10,9},{11,10},{12... | collective-permute-start | bytes 2211848 | tf_op jit(solution)/shard_map/ppermute | solution.py:26
  459.2 63.0 %collective-permute-start.1 = (bf16[2,128,1440]{1,2,0:T(8,128)(2,1)S(1)}, bf16[2,128,1440]{1,2,0:T(8,128)(2,1)}, u32[]{:S(2)}, u32[]{:S(2)}) collective-permute-start(bf16[2,128,1440]{1,2,0:T(8,128)(2,1)S(1)} %collective-permute-done), channel_id=1, source_target_pairs={{0,1},{1,2},{2,3},{3,4},{4,5},{5,6},{6,7},{8,9},{9,10},{10,11},{11... | collective-permute-start | bytes 2211848 | tf_op jit(solution)/shard_map/ppermute | solution.py:26
  546.0 15.5 %copy-start.1 = (bf16[48,32,768]{2,1,0:T(8,128)(2,1)S(1)}, bf16[48,32,768]{2,1,0:T(8,128)(2,1)}, u32[]{:S(2)}) copy-start(bf16[48,32,768]{2,1,0:T(8,128)(2,1)} %param.9) | copy-start | bytes 7077892
Sparse Core Ops, SparseCore 0:
  10.3 203.8 all-gather.2
  225.3 97.3 all-gather.4
  374.4 145.1 all-reduce.1
where the time goes:
time: 569 us; the launch traced here: 568 us
  waiting for transfers between devices  329 us (58%)
  blocking collectives  74.2 us (13%)
  other arithmetic  50.9 us (9%)
  local copies, waits for them, and re-layouts  49.6 us (9%)
  matrix products  29.5 us (5%)
  starting transfers between devices  21.1 us (4%)
  between operations  14.2 us (2%)
    all_gather x1, waiting for transfers between devices, shards(): portion = lax.all_gather(grad_coef, 'lat', axis=0, tiled=True)  206 us
    psum x1, blocking collectives, shards(): point_sum, depth_sum = lax.psum((point_part, depth_part), ('ord', 'lat'))  74.2 us
    psum x1, waiting for transfers between devices, shards(): point_sum, depth_sum = lax.psum((point_part, depth_part), ('ord', 'lat'))  56.5 us
    ppermute x4, waiting for transfers between devices, passed_along(): lax.ppermute(value, axis, [(source, source + steps) for source in range(l...  38.2 us
    ppermute x2, waiting for transfers between devices, padded(): lax.ppermute(lax.slice_in_dim(block, block.shape[dim] - width, None, axis...  27.1 us
    slice x2, local copies, waits for them, and re-layouts, shards(): jnp.roll(padded_grad[4 - tap_row:4 - tap_row + row_count], tap_col - 2, a...  21.3 us
    slice x2, local copies, waits for them, and re-layouts, shards(): jnp.roll(x_wide[tap_row:tap_row + row_count], 2 - tap_col, axis=2)  21.1 us
    another operation x1, other arithmetic  20 us
  transfers between devices with their start and end apart: 11, of which 5 were waited for; matrix products, arithmetic and copies ran while one was open for 12% of the time, Pallas kernels for 0%

commit v1 on v0

v1 whole, which is shorter than its diff:
```python
import math

import jax
import jax.numpy as jnp
from jax import lax
from jax.sharding import PartitionSpec as P

MESH_AXES = ("ord", "lat")


def device_of_block(k):
    n_ord, n_lat = lax.axis_size("ord"), lax.axis_size("lat")
    l, o = divmod(k, n_ord)
    return o * n_lat + l


def with_rims(field, width=2):
    count = lax.axis_size("ord") * lax.axis_size("lat")
    down_pairs = [(device_of_block(k), device_of_block(k + 1)) for k in range(count - 1)]
    up_pairs = [(device_of_block(k + 1), device_of_block(k)) for k in range(count - 1)]
    upper = lax.ppermute(field[field.shape[0] - width :], MESH_AXES, down_pairs)
    lower = lax.ppermute(field[:width], MESH_AXES, up_pairs)
    return jnp.concatenate([upper, field, lower], axis=0)


def make_table(orders, length):
    lon_ids = jnp.arange(length, dtype=jnp.int32)
    residue = orders[:, None] * lon_ids[None, :] % length
    angles = residue.astype(jnp.float32) * (2.0 * math.pi / length)
    factor = jnp.where((orders == 0) | (2 * orders == length), 1.0, 2.0).astype(jnp.float32)[
        :, None
    ]
    return jnp.stack([factor * jnp.cos(angles), -factor * jnp.sin(angles)], axis=1).astype(
        jnp.bfloat16
    )


def inverse_lon(spec_rows, dft_table):
    slots_here, rows_here, doubled = spec_rows.shape
    paired = spec_rows.reshape(slots_here, rows_here, doubled // 2, 2)
    return jnp.einsum("srcp,spf->rcf", paired, dft_table, preferred_element_type=jnp.float32)


def shards(
    grad_coef, legendre, quad_weight, slot_order, slot_count, conv_input, depth_kernel, point_weight
):
    n_ord = lax.axis_size("ord")
    n_lat = lax.axis_size("lat")
    own_slots, degrees, doubled = grad_coef.shape
    row_count, channels, longitudes = conv_input.shape
    lat_index = lax.axis_index("lat")

    x_wide = with_rims(conv_input).astype(jnp.float32)

    leg_rows = lax.all_to_all(legendre, "lat", 0, 1, tiled=True)
    weights = lax.all_gather(quad_weight, "lat", axis=0, tiled=True)
    counts = lax.dynamic_slice_in_dim(slot_count, lat_index * own_slots, own_slots)
    is_valid = jnp.arange(degrees, dtype=jnp.int32)[None, :] < counts[:, None]
    masked = grad_coef * is_valid[:, :, None].astype(grad_coef.dtype)
    summed = jnp.einsum("slj,sjk->slk", leg_rows, masked, preferred_element_type=jnp.float32)
    spectral = (summed * weights[None, :, None]).astype(jnp.bfloat16)
    by_device = spectral.reshape(own_slots, n_lat, n_ord, row_count, doubled)
    by_device = by_device.transpose(0, 2, 1, 3, 4).reshape(own_slots, -1, doubled)
    own_rows = lax.all_to_all(by_device, MESH_AXES, 1, 0, tiled=True)

    grad_grid = inverse_lon(own_rows, make_table(slot_order, longitudes))
    grad_grid = grad_grid.astype(jnp.bfloat16)

    hidden = jnp.zeros((row_count, channels, longitudes), jnp.float32)
    for tap_row in range(5):
        for tap_col in range(5):
            weight_tap = depth_kernel[:, 5 * tap_row + tap_col][None, :, None]
            hidden = hidden + weight_tap * jnp.roll(
                x_wide[tap_row : tap_row + row_count], 2 - tap_col, axis=2
            )
    hidden = hidden.astype(jnp.bfloat16)
    grad_hidden = jnp.einsum(
        "cd,rdf->rcf", point_weight, grad_grid, preferred_element_type=jnp.float32
    ).astype(jnp.bfloat16)
    point_part = jnp.einsum("rcf,rdf->cd", hidden, grad_grid, preferred_element_type=jnp.float32)
    hidden_wide = grad_hidden.astype(jnp.float32)
    depth_terms = []
    for tap_row in range(5):
        for tap_col in range(5):
            shifted_x = jnp.roll(x_wide[tap_row : tap_row + row_count], 2 - tap_col, axis=2)
            depth_terms.append(jnp.sum(hidden_wide * shifted_x, axis=(0, 2)))
    depth_part = jnp.stack(depth_terms, axis=1)
    sums = lax.psum(jnp.concatenate([point_part, depth_part], axis=1), MESH_AXES)

    padded_grad = with_rims(grad_hidden).astype(jnp.float32)
    grad_input = jnp.zeros((row_count, channels, longitudes), jnp.float32)
    for tap_row in range(5):
        for tap_col in range(5):
            weight_tap = depth_kernel[:, 5 * tap_row + tap_col][None, :, None]
            grad_input = grad_input + weight_tap * jnp.roll(
                padded_grad[4 - tap_row : 4 - tap_row + row_count], tap_col - 2, axis=2
            )
    total_rows = row_count * n_ord * n_lat
    grad_scale = 1.0 / math.sqrt(total_rows * longitudes)
    sums = sums * grad_scale
    return (grad_input.astype(jnp.bfloat16), sums[:, :channels], sums[:, channels:])


def solution(mesh):
    return jax.shard_map(
        shards,
        mesh=mesh,
        in_specs=(
            P(("ord", "lat"), None, None),
            P("ord", "lat", None),
            P("lat"),
            P(),
            P("ord"),
            P(("lat", "ord"), None, None),
            P(),
            P(),
        ),
        out_specs=(P(("lat", "ord"), None, None), P(), P()),
        check_vma=False,
    )
```

time: 569 us -> 413 us (0.73)
  waiting for transfers between devices: 329 us -> 149 us
  local copies, waits for them, and re-layouts: 49.6 us -> 111 us
  blocking collectives: 74.2 us -> 46 us
  matrix products: 29.5 us -> 17.9 us
  starting transfers between devices: 21.1 us -> 29.4 us
  other arithmetic: 50.9 us -> 43.9 us
    all_gather x2 -> x0, waiting for transfers between devices: 206 us -> none  [the longest x1 206 us: shards(): portion = lax.all_gather(grad_coef, 'lat', axis=0, tiled=True)]
    psum x1, waiting for transfers between devices: 56.5 us -> 140 us  [shards(): lax.psum(jnp.concatenate([point_part, depth_part], axis=1), MESH_AXES)]
    psum x1 -> x0, blocking collectives: 74.2 us -> none  [shards(): point_sum, depth_sum = lax.psum((point_part, depth_part), ('ord', 'lat'))]
    ppermute x8 -> x4, waiting for transfers between devices: 65.3 us -> 0.01 us  [the longest x2 0.01 us: with_rims(): upper = lax.ppermute(field[field.shape[0] - width:], MESH_AXES, down_pairs)]
    unnamed x0 -> x1, blocking collectives: none -> 46 us
    all_to_all x0 -> x2, local copies, waits for them, and re-layouts: none -> 28.6 us  [the longest x1 26.6 us: shards(): own_rows = lax.all_to_all(by_device, MESH_AXES, 1, 0, tiled=True)]
    reshape x0 -> x3, local copies, waits for them, and re-layouts: none -> 28.2 us  [the longest x1 26 us: inverse_lon(): paired = spec_rows.reshape(slots_here, rows_here, doubled // 2, 2)]
    all_to_all x0 -> x2, starting transfers between devices: none -> 17.7 us  [the longest x1 10.3 us: shards(): own_rows = lax.all_to_all(by_device, MESH_AXES, 1, 0, tiled=True)]
  transfers between devices with their start and end apart: 11 -> 7, of which waited for: 5 -> 2; matrix products, arithmetic and copies ran while one was open for 12% -> 16% of each run, Pallas kernels for 0% -> 0%
where the time goes in v1:
time: 413 us
  waiting for transfers between devices  149 us (36%)
  local copies, waits for them, and re-layouts  111 us (27%)
  blocking collectives  46 us (11%)
  other arithmetic  43.9 us (11%)
  starting transfers between devices  29.4 us (7%)
  matrix products  17.9 us (4%)
  between operations  15.3 us (4%)
    psum x1, waiting for transfers between devices, shards(): lax.psum(jnp.concatenate([point_part, depth_part], axis=1), MESH_AXES)  140 us
    unnamed x1, blocking collectives  46 us
    all_to_all x1, local copies, waits for them, and re-layouts, shards(): own_rows = lax.all_to_all(by_device, MESH_AXES, 1, 0, tiled=True)  26.6 us
    reshape x1, local copies, waits for them, and re-layouts, inverse_lon(): paired = spec_rows.reshape(slots_here, rows_here, doubled // 2, 2)  26 us
    slice x2, local copies, waits for them, and re-layouts, shards(): jnp.roll(padded_grad[4 - tap_row:4 - tap_row + row_count], tap_col - 2, a...  21.5 us
    slice x2, local copies, waits for them, and re-layouts, shards(): jnp.roll(x_wide[tap_row:tap_row + row_count], 2 - tap_col, axis=2)  21.5 us
    another operation x1, other arithmetic  20 us
    convert_element_type x1, other arithmetic, shards(): grad_input.astype(jnp.bfloat16)  13.1 us
  transfers between devices with their start and end apart: 7, of which 2 were waited for; matrix products, arithmetic and copies ran while one was open for 16% of the time, Pallas kernels for 0%

profile of v1, /device:TPU:1, one launch (start us, length us, event | category | flops | bytes accessed | tf_op | source)
XLA Modules:
  0.0 412.7 jit_solution(17577364740879625948)
XLA Ops:
  7.2 4.7 %collective-permute-start.2 = (bf16[2,128,1440]{1,2,0:T(8,128)(2,1)}, bf16[2,128,1440]{1,2,0:T(8,128)(2,1)S(1)}, u32[]{:S(2)}, u32[]{:S(2)}) collective-permute-start(bf16[2,128,1440]{1,2,0:T(8,128)(2,1)} %param.13), channel_id=1, source_target_pairs={{0,8},{8,16},{16,24},{24,32},{32,40},{40,48},{48,56},{56,64},{64,7... | collective-permute-start | bytes 2211848 | tf_op jit(solution)/shard_map/ppermute | solution.py:21
  12.0 1.9 collective-permute-start.3
  13.9 7.4 %all-to-all-start = ((bf16[48,32,768]{2,1,0:T(8,128)(2,1)}), bf16[48,32,768]{2,1,0:T(8,128)(2,1)}, u32[]{:S(2)}, u32[]{:S(2)}) async-start(bf16[48,32,768]{2,1,0:T(8,128)(2,1)} %param.9), calls=%async_computation | async-start | bytes 4718592 | tf_op jit(solution)/shard_map/all_to_all | solution.py:55
  21.3 0.1 dynamic_slice.3
  21.4 0.1 fusion.71
  21.4 0.6 dynamic-slice
  22.7 0.2 dynamic-update-slice
  22.9 46.0 %all-reduce = f32[256]{0:T(256)S(1)} all-reduce(f32[256]{0:T(256)S(1)} %dynamic-update-slice), channel_id=1, replica_groups=mesh['ord'=16,'lat'=8] {'lat'}, use_global_device_ids=true, to_apply=%add | all-reduce | flops 256 | bytes 2048
  69.0 20.0 %multiply_convert_fusion.1 = (bf16[768,1,1440]{0,2,1:T(8,128)(2,1)}, bf16[768,1,1440]{0,2,1:T(8,128)(2,1)}) fusion(s32[768]{0:T(1024)S(1)} %copy-done.25, f32[768]{0:T(1024)S(1)} %get-tuple-element.144, f32[768]{0:T(1024)S(1)} %get-tuple-element.145), kind=kLoop, calls=%fused_computation.33 | loop fusion | flops 14376960 | bytes 4432896 | tf_op jit(solution)/shard_map/convert
  89.1 2.3 maximum_convert_fusion.1
  91.4 10.8 %fusion.77 = (f32[2,128,1438]{1,2,0:T(8,128)}, f32[2,128,1438]{1,2,0:T(8,128)}, f32[2,128,1438]{1,2,0:T(8,128)}, f32[2,128,1438]{1,2,0:T(8,128)}, f32[2,128,1438...) fusion(f32[6,128,1440]{1,2,0:T(8,128)} %maximum_convert_fusion.1), kind=kLoop, calls=%fused_computation.222 | loop fusion | bytes 29450240 | tf_op jit(solution)/shard_map/jit(_roll_static)/slice | solution.py:73
  102.3 2.0 copy.18
  104.3 0.4 copy-done.27
  104.7 1.2 fusion.65
  105.9 0.3 reshape.184
  106.2 1.8 copy.25
  108.0 10.3 %all-to-all-start.1 = ((bf16[6,256,256]{2,0,1:T(8,128)(2,1)}), bf16[6,256,256]{2,0,1:T(8,128)(2,1)S(1)}, u32[]{:S(2)}, u32[]{:S(2)}) async-start(bf16[6,256,256]{2,0,1:T(8,128)(2,1)} %bitcast.7), calls=%async_computation.1 | async-start | bytes 2097152 | tf_op jit(solution)/shard_map/all_to_all | solution.py:64
  118.3 0.2 all-reduce.3.cloned.1.call-start
  118.6 10.6 %fusion.78 = (f32[2,128,1439]{1,2,0:T(8,128)}, f32[2,128,1439]{1,2,0:T(8,128)}, f32[2,128,1439]{1,2,0:T(8,128)}, f32[2,128,1439]{1,2,0:T(8,128)}, f32[2,128,1439...) fusion(f32[6,128,1440]{1,2,0:T(8,128)} %maximum_convert_fusion.1), kind=kLoop, calls=%fused_computation.223 | loop fusion | bytes 29470720 | tf_op jit(solution)/shard_map/jit(_roll_static)/slice | solution.py:73
  129.2 8.6 %all-to-all-done.1 = bf16[6,256,256]{2,0,1:T(8,128)(2,1)S(1)} async-done(((bf16[6,256,256]{2,0,1:T(8,128)(2,1)}), bf16[6,256,256]{2,0,1:T(8,128)(2,1)S(1)}, u32[]{:S(2)}, u32[]{:S(2)}) %all-to-all-start.1) | async-done | bytes 786464 | tf_op jit(solution)/shard_map/all_to_all | solution.py:64
  137.8 26.6 %copy.21 = bf16[6,128,2,256]{0,1,3,2:T(8,128)(2,1)} copy(bf16[6,128,2,256]{3,0,2,1:T(8,128)(2,1)S(1)} %bitcast.118) | data formatting | bytes 1572864 | tf_op jit(solution)/shard_map/all_to_all | solution.py:64
  164.5 26.0 %reshape.186 = bf16[768,2,128,2]{0,3,2,1:T(2,128)(2,1)S(1)} reshape(bf16[128,6,2,256]{1,0,3,2:T(8,128)(2,1)} %bitcast.117) | data formatting | bytes 1572864 | tf_op jit(solution)/shard_map/reshape | solution.py:40
  190.6 3.1 fusion.9
  193.7 0.1 copy-done.23
  193.8 0.4 copy-done.24
  194.3 1.5 fusion.35
  195.8 2.2 collective-permute-start
  198.0 2.7 collective-permute-start.1
  200.8 1.8 fusion.36
  202.6 0.4 copy-done.6
  203.0 0.4 copy-done.7
  203.5 0.4 copy-done.8
  203.9 0.4 copy-done.9
  204.3 12.1 %convolution_bitcast_fusion = f32[128,128]{0,1:T(8,128)S(1)} fusion(bf16[2,128,1440]{1,2,0:T(8,128)(2,1)S(1)} %fusion.9, f32[6,128,1440]{1,2,0:T(8,128)S(1)} %bitcast.116, f32[2,128,1]{1,2,0:T(1,128)S(1)} %get-tuple-element.88, f32[2,128,1439]{1,2,0:T(8,128)} %get-tuple-element.54, f32[2,128,1439]{1,2,0:T(8,128)} %get-tuple-element.53, ...), kind=kOutput, calls=%fused_computation.145 | convolution fusion | flops 120176640 | bytes 37690880 | tf_op jit(solution)/shard_map/rcf,rdf->cd/dot_general | solution.py:80
  216.4 3.4 fusion.37
  219.7 3.1 concatenate.195
  222.8 140.2 %all-reduce.3.cloned.1.call-done = f32[128,153]{0,1:T(8,128)} async-done(((f32[128,153]{0,1:T(8,128)}), f32[128,153]{0,1:T(8,128)}) %all-reduce.3.cloned.1.call-update) | async-done | bytes 78352 | tf_op jit(solution)/shard_map/psum | solution.py:88
  363.0 0.9 broadcast_multiply_fusion
  363.9 0.6 slice.737
  364.5 0.7 copy.23
  365.3 2.4 maximum_convert_fusion
  367.6 10.9 %fusion.79 = (f32[2,128,1438]{1,2,0:T(8,128)}, f32[2,128,1438]{1,2,0:T(8,128)}, f32[2,128,1438]{1,2,0:T(8,128)}, f32[2,128,1438]{1,2,0:T(8,128)}, f32[2,128,1438...) fusion(f32[6,128,1440]{1,2,0:T(8,128)} %maximum_convert_fusion), kind=kLoop, calls=%fused_computation.224 | loop fusion | bytes 29450240 | tf_op jit(solution)/shard_map/jit(_roll_static)/slice | solution.py:95
  378.5 10.7 %fusion.80 = (f32[2,128,1439]{1,2,0:T(8,128)}, f32[2,128,1439]{1,2,0:T(8,128)}, f32[2,128,1439]{1,2,0:T(8,128)}, f32[2,128,1439]{1,2,0:T(8,128)}, f32[2,128,1439...) fusion(f32[6,128,1440]{1,2,0:T(8,128)} %maximum_convert_fusion), kind=kLoop, calls=%fused_computation.225 | loop fusion | bytes 29470720 | tf_op jit(solution)/shard_map/jit(_roll_static)/slice | solution.py:95
  389.3 1.3 copy-done.20
  390.5 0.4 copy-done.21
  391.0 0.4 copy-done.19
  391.4 1.3 copy-done.2
  392.8 13.1 %fusion.41 = bf16[2,128,1440]{1,2,0:T(8,128)(2,1)} fusion(f32[6,128,1440]{1,2,0:T(8,128)S(1)} %copy-done.2, f32[2,128,2]{1,2,0:T(2,128)S(1)} %get-tuple-element.112, f32[2,128,1438]{1,2,0:T(8,128)} %get-tuple-element.66, f32[2,128,1]{1,2,0:T(1,128)S(1)} %get-tuple-element.116, f32[2,128,1439]{1,2,0:T(8,128)} %get-tuple-element.76, ...), kind=kLoop, calls=%fused_computation.76 | loop fusion | flops 25804800 | bytes 37614080 | tf_op jit(solution)/shard_map/convert_element_type | solution.py:101
  (75 shorter events, 0.3 us)
Async XLA Ops:
  7.2 186.5 %copy-start = (bf16[128,128]{1,0:T(8,128)(2,1)S(1)}, bf16[128,128]{1,0:T(8,128)(2,1)}, u32[]{:S(2)}) copy-start(bf16[128,128]{1,0:T(8,128)(2,1)} %param.15) | copy-start | bytes 98308
  7.2 14.3 %copy-start.30 = (u32[128]{0:T(128)S(1)}, u32[128]{0:T(128)}, u32[]{:S(2)}) copy-start(u32[128]{0:T(128)} %constant.39) | copy-start | bytes 1540
  7.2 14.1 %copy-start.28 = (s32[48]{0:T(128)S(1)}, s32[48]{0:T(128)}, u32[]{:S(2)}) copy-start(s32[48]{0:T(128)} %param.12) | copy-start | bytes 580
  7.2 15.5 %copy-start.29 = (f32[32]{0:T(128)S(1)}, f32[32]{0:T(128)}, u32[]{:S(2)}) copy-start(f32[32]{0:T(128)} %param.10) | copy-start | bytes 388
  7.2 61.8 %copy-start.25 = (s32[768]{0:T(1024)S(1)}, s32[768]{0:T(1024)}, u32[]{:S(2)}) copy-start(s32[768]{0:T(1024)} %param.11) | copy-start | bytes 9220
  7.2 61.8 %copy-start.26 = (f32[128,25]{0,1:T(8,128)S(1)}, f32[128,25]{0,1:T(8,128)}, u32[]{:S(2)}) copy-start(f32[128,25]{0,1:T(8,128)} %param.14) | copy-start | bytes 38404
  7.2 81.8 %collective-permute-start.2 = (bf16[2,128,1440]{1,2,0:T(8,128)(2,1)}, bf16[2,128,1440]{1,2,0:T(8,128)(2,1)S(1)}, u32[]{:S(2)}, u32[]{:S(2)}) collective-permute-start(bf16[2,128,1440]{1,2,0:T(8,128)(2,1)} %param.13), channel_id=1, source_target_pairs={{0,8},{8,16},{16,24},{24,32},{32,40},{40,48},{48,56},{56,64},{64,7... | collective-permute-start | bytes 2211848 | tf_op jit(solution)/shard_map/ppermute | solution.py:21
  12.0 77.0 %collective-permute-start.3 = (bf16[2,128,1440]{1,2,0:T(8,128)(2,1)}, bf16[2,128,1440]{1,2,0:T(8,128)(2,1)S(1)}, u32[]{:S(2)}, u32[]{:S(2)}) collective-permute-start(bf16[2,128,1440]{1,2,0:T(8,128)(2,1)} %param.13), channel_id=1, source_target_pairs={{8,0},{16,8},{24,16},{32,24},{40,32},{48,40},{56,48},{64,56},{72,6... | collective-permute-start | bytes 2211848 | tf_op jit(solution)/shard_map/ppermute | solution.py:22
  13.9 88.4 %all-to-all-start = ((bf16[48,32,768]{2,1,0:T(8,128)(2,1)}), bf16[48,32,768]{2,1,0:T(8,128)(2,1)}, u32[]{:S(2)}, u32[]{:S(2)}) async-start(bf16[48,32,768]{2,1,0:T(8,128)(2,1)} %param.9), calls=%async_computation | async-start | bytes 4718592 | tf_op jit(solution)/shard_map/all_to_all | solution.py:55
  69.0 20.0 %copy-start.3 = (bf16[2,128,1440]{1,2,0:T(8,128)(2,1)S(1)}, bf16[2,128,1440]{1,2,0:T(8,128)(2,1)}, u32[]{:S(2)}) copy-start(bf16[2,128,1440]{1,2,0:T(8,128)(2,1)} %param.13) | copy-start | bytes 2211844
  102.3 2.4 copy-start.27
  108.0 29.8 %all-to-all-start.1 = ((bf16[6,256,256]{2,0,1:T(8,128)(2,1)}), bf16[6,256,256]{2,0,1:T(8,128)(2,1)S(1)}, u32[]{:S(2)}, u32[]{:S(2)}) async-start(bf16[6,256,256]{2,0,1:T(8,128)(2,1)} %bitcast.7), calls=%async_computation.1 | async-start | bytes 2097152 | tf_op jit(solution)/shard_map/all_to_all | solution.py:64
  118.3 244.7 %all-reduce.3.cloned.1.call-start = ((), (), s32[]{:S(2)}) async-start(), calls=%async_computation.2 | async-start | bytes 163840 | tf_op jit(solution)/shard_map/psum | solution.py:88
  164.5 26.1 %copy-start.22 = (bf16[768,1,1440]{0,2,1:T(8,128)(2,1)S(1)}, bf16[768,1,1440]{0,2,1:T(8,128)(2,1)}, u32[]{:S(2)}) copy-start(bf16[768,1,1440]{0,2,1:T(8,128)(2,1)} %get-tuple-element.142) | copy-start | bytes 6635524
  164.5 29.3 %slice-start = ((s8[4423680]{0:T(1024)(128)(4,1)}), s8[229376]{0:T(1024)(128)(4,1)S(1)}, s32[]{:S(2)}) async-start(s8[4423680]{0:T(1024)(128)(4,1)} %bitcast.115), calls=%async_computation.3 | async-start | bytes 458752
  190.5 3.2 slice-start.1
  190.5 3.3 copy-start.23
  190.5 3.7 copy-start.24
  190.6 10.1 %copy-start.16 = (f32[2,128,1439]{1,2,0:T(8,128)S(1)}, f32[2,128,1439]{1,2,0:T(8,128)}, u32[]{:S(2)}) copy-start(f32[2,128,1439]{1,2,0:T(8,128)} %get-tuple-element.50) | copy-start | bytes 4420612
  190.6 10.1 %copy-start.17 = (f32[2,128,1439]{1,2,0:T(8,128)S(1)}, f32[2,128,1439]{1,2,0:T(8,128)}, u32[]{:S(2)}) copy-start(f32[2,128,1439]{1,2,0:T(8,128)} %get-tuple-element.54) | copy-start | bytes 4420612
  190.6 10.1 %copy-start.18 = (f32[2,128,1439]{1,2,0:T(8,128)S(1)}, f32[2,128,1439]{1,2,0:T(8,128)}, u32[]{:S(2)}) copy-start(f32[2,128,1439]{1,2,0:T(8,128)} %get-tuple-element.55) | copy-start | bytes 4420612
  194.3 6.4 %copy-start.10 = (f32[2,128,1438]{1,2,0:T(8,128)S(1)}, f32[2,128,1438]{1,2,0:T(8,128)}, u32[]{:S(2)}) copy-start(f32[2,128,1438]{1,2,0:T(8,128)} %get-tuple-element.39) | copy-start | bytes 4417540
  194.3 6.4 %copy-start.11 = (f32[2,128,1438]{1,2,0:T(8,128)S(1)}, f32[2,128,1438]{1,2,0:T(8,128)}, u32[]{:S(2)}) copy-start(f32[2,128,1438]{1,2,0:T(8,128)} %get-tuple-element.40) | copy-start | bytes 4417540
  194.3 6.4 %copy-start.12 = (f32[2,128,1438]{1,2,0:T(8,128)S(1)}, f32[2,128,1438]{1,2,0:T(8,128)}, u32[]{:S(2)}) copy-start(f32[2,128,1438]{1,2,0:T(8,128)} %get-tuple-element.42) | copy-start | bytes 4417540
  194.3 6.4 %copy-start.13 = (f32[2,128,1438]{1,2,0:T(8,128)S(1)}, f32[2,128,1438]{1,2,0:T(8,128)}, u32[]{:S(2)}) copy-start(f32[2,128,1438]{1,2,0:T(8,128)} %get-tuple-element.46) | copy-start | bytes 4417540
  194.3 6.4 %copy-start.14 = (f32[2,128,1439]{1,2,0:T(8,128)S(1)}, f32[2,128,1439]{1,2,0:T(8,128)}, u32[]{:S(2)}) copy-start(f32[2,128,1439]{1,2,0:T(8,128)} %get-tuple-element.48) | copy-start | bytes 4420612
  194.3 6.4 %copy-start.15 = (f32[2,128,1439]{1,2,0:T(8,128)S(1)}, f32[2,128,1439]{1,2,0:T(8,128)}, u32[]{:S(2)}) copy-start(f32[2,128,1439]{1,2,0:T(8,128)} %get-tuple-element.49) | copy-start | bytes 4420612
  195.8 169.5 %collective-permute-start = (bf16[2,128,1440]{1,2,0:T(8,128)(2,1)S(1)}, bf16[2,128,1440]{1,2,0:T(8,128)(2,1)S(1)}, u32[]{:S(2)}, u32[]{:S(2)}) collective-permute-start(bf16[2,128,1440]{1,2,0:T(8,128)(2,1)S(1)} %get-tuple-element.146), channel_id=1, source_target_pairs={{0,8},{8,16},{16,24},{24,32},{32,40},{40,48},{48,56},{56,64},{64,7... | collective-permute-start | bytes 2211848 | tf_op jit(solution)/shard_map/ppermute | solution.py:21
  198.0 167.3 %collective-permute-start.1 = (bf16[2,128,1440]{1,2,0:T(8,128)(2,1)S(1)}, bf16[2,128,1440]{1,2,0:T(8,128)(2,1)S(1)}, u32[]{:S(2)}, u32[]{:S(2)}) collective-permute-start(bf16[2,128,1440]{1,2,0:T(8,128)(2,1)S(1)} %get-tuple-element.146), channel_id=1, source_target_pairs={{8,0},{16,8},{24,16},{32,24},{40,32},{48,40},{56,48},{64,56},{72,6... | collective-permute-start | bytes 2211848 | tf_op jit(solution)/shard_map/ppermute | solution.py:22
  200.7 1.9 copy-start.4
  200.8 1.9 copy-start.5
  200.8 2.2 copy-start.6
  200.8 2.7 copy-start.7
  200.8 3.1 copy-start.8
  200.8 3.5 copy-start.9
  389.2 1.4 copy-start.20
  389.2 1.8 copy-start.21
  389.2 2.2 copy-start.19
  389.2 3.6 copy-start.2
  392.8 13.1 %copy-start.1 = (bf16[128,128]{1,0:T(8,128)(2,1)S(1)}, bf16[128,128]{1,0:T(8,128)(2,1)}, u32[]{:S(2)}) copy-start(bf16[128,128]{1,0:T(8,128)(2,1)} %param.15) | copy-start | bytes 98308
Sparse Core Ops, SparseCore 0:
  223.0 139.9 all-reduce.2

commit v2 on v1

--- a/solution.py
+++ b/solution.py
@@ -23,6 +23,16 @@
     return jnp.concatenate([upper, field, lower], axis=0)
 
 
+def butterfly_sum(value):
+    count = lax.axis_size("ord") * lax.axis_size("lat")
+    bits = count.bit_length() - 1
+    order = sorted(range(bits), key=lambda b: (b != 3, b))
+    for bit in order:
+        pairs = [(d, d ^ (1 << bit)) for d in range(count)]
+        value = value + lax.ppermute(value, MESH_AXES, pairs)
+    return value
+
+
 def make_table(orders, length):
     lon_ids = jnp.arange(length, dtype=jnp.int32)
     residue = orders[:, None] * lon_ids[None, :] % length
@@ -30,15 +40,8 @@
     factor = jnp.where((orders == 0) | (2 * orders == length), 1.0, 2.0).astype(jnp.float32)[
         :, None
     ]
-    return jnp.stack([factor * jnp.cos(angles), -factor * jnp.sin(angles)], axis=1).astype(
-        jnp.bfloat16
-    )
-
-
-def inverse_lon(spec_rows, dft_table):
-    slots_here, rows_here, doubled = spec_rows.shape
-    paired = spec_rows.reshape(slots_here, rows_here, doubled // 2, 2)
-    return jnp.einsum("srcp,spf->rcf", paired, dft_table, preferred_element_type=jnp.float32)
+    parts = [factor * jnp.cos(angles), -factor * jnp.sin(angles)]
+    return jnp.concatenate(parts, axis=1).astype(jnp.bfloat16)
 
 
 def shards(
@@ -53,18 +56,28 @@
     x_wide = with_rims(conv_input).astype(jnp.float32)
 
     leg_rows = lax.all_to_all(legendre, "lat", 0, 1, tiled=True)
-    weights = lax.all_gather(quad_weight, "lat", axis=0, tiled=True)
+    spread = jnp.broadcast_to(quad_weight[None], (n_lat,) + quad_weight.shape)
+    weights = lax.all_to_all(spread, "lat", 0, 0, tiled=True).reshape(-1)
     counts = lax.dynamic_slice_in_dim(slot_count, lat_index * own_slots, own_slots)
     is_valid = jnp.arange(degrees, dtype=jnp.int32)[None, :] < counts[:, None]
     masked = grad_coef * is_valid[:, :, None].astype(grad_coef.dtype)
+    source = jnp.arange(doubled, dtype=jnp.int32)
+    target = (source % 2) * channels + source // 2
+    permute = (target[:, None] == source[None, :]).astype(grad_coef.dtype)
+    masked = jnp.einsum("sjk,kt->sjt", masked, permute, preferred_element_type=jnp.float32)
+    masked = masked.astype(grad_coef.dtype)
     summed = jnp.einsum("slj,sjk->slk", leg_rows, masked, preferred_element_type=jnp.float32)
     spectral = (summed * weights[None, :, None]).astype(jnp.bfloat16)
-    by_device = spectral.reshape(own_slots, n_lat, n_ord, row_count, doubled)
-    by_device = by_device.transpose(0, 2, 1, 3, 4).reshape(own_slots, -1, doubled)
+    by_device = spectral.reshape(own_slots, n_lat, n_ord, row_count * doubled)
+    by_device = by_device.transpose(0, 2, 1, 3).reshape(own_slots, n_ord * n_lat, -1)
     own_rows = lax.all_to_all(by_device, MESH_AXES, 1, 0, tiled=True)
+    own_rows = own_rows.reshape(-1, row_count * doubled)
 
-    grad_grid = inverse_lon(own_rows, make_table(slot_order, longitudes))
-    grad_grid = grad_grid.astype(jnp.bfloat16)
+    table = make_table(slot_order, longitudes)
+    both = jnp.einsum("sn,sq->nq", own_rows, table, preferred_element_type=jnp.float32)
+    both = both.reshape(row_count, 2, channels, 2 * longitudes)
+    grad_grid = both[:, 0, :, :longitudes] + both[:, 1, :, longitudes:]
+    grad_grid = grad_grid.reshape(row_count, channels, longitudes).astype(jnp.bfloat16)
 
     hidden = jnp.zeros((row_count, channels, longitudes), jnp.float32)
     for tap_row in range(5):
@@ -85,7 +98,7 @@
             shifted_x = jnp.roll(x_wide[tap_row : tap_row + row_count], 2 - tap_col, axis=2)
             depth_terms.append(jnp.sum(hidden_wide * shifted_x, axis=(0, 2)))
     depth_part = jnp.stack(depth_terms, axis=1)
-    sums = lax.psum(jnp.concatenate([point_part, depth_part], axis=1), MESH_AXES)
+    sums = butterfly_sum(jnp.concatenate([point_part, depth_part], axis=1))
 
     padded_grad = with_rims(grad_hidden).astype(jnp.float32)
     grad_input = jnp.zeros((row_count, channels, longitudes), jnp.float32)

time: 413 us -> 234 us (0.57)
  waiting for transfers between devices: 149 us -> 54.8 us
  blocking collectives: 46 us -> 0 us
  local copies, waits for them, and re-layouts: 111 us -> 66.2 us
  between operations: 15.3 us -> 1.82 us
  starting transfers between devices: 29.4 us -> 40.3 us
  matrix products: 17.9 us -> 23 us
    psum x1 -> x0, waiting for transfers between devices: 140 us -> none  [shards(): lax.psum(jnp.concatenate([point_part, depth_part], axis=1), MESH_AXES)]
    unnamed x1 -> x0, blocking collectives: 46 us -> none
    ppermute x0 -> x7, waiting for transfers between devices: none -> 35.7 us  [butterfly_sum(): value = value + lax.ppermute(value, MESH_AXES, pairs)]
    all_to_all x1, local copies, waits for them, and re-layouts: 26.6 us -> 0.51 us  [shards(): weights = lax.all_to_all(spread, 'lat', 0, 0, tiled=True).reshape(-1)]
    reshape x3, local copies, waits for them, and re-layouts: 28.2 us -> 2.82 us  [the longest x1 1.43 us: shards(): by_device.transpose(0, 2, 1, 3).reshape(own_slots, n_ord * n_lat, -1)]
    all_to_all x1, waiting for transfers between devices: 0.01 us -> 10.9 us  [shards(): leg_rows = lax.all_to_all(legendre, 'lat', 0, 1, tiled=True)]
    all_to_all x0 -> x1, starting transfers between devices: none -> 7.37 us  [shards(): weights = lax.all_to_all(spread, 'lat', 0, 0, tiled=True).reshape(-1)]
    unnamed x70 -> x133, local copies, waits for them, and re-layouts: 7.78 us -> 10 us
  transfers between devices with their start and end apart: 7 -> 14, of which waited for: 2 -> 8; matrix products, arithmetic and copies ran while one was open for 16% -> 23% of each run, Pallas kernels for 0% -> 0%
where the time goes in v2:
time: 234 us; the launch traced here: 232 us
  local copies, waits for them, and re-layouts  66.2 us (28%)
  waiting for transfers between devices  54.8 us (23%)
  other arithmetic  45.7 us (20%)
  starting transfers between devices  40.3 us (17%)
  matrix products  23 us (10%)
    ppermute x7, waiting for transfers between devices, butterfly_sum(): value = value + lax.ppermute(value, MESH_AXES, pairs)  35.7 us
    slice x2, local copies, waits for them, and re-layouts, shards(): jnp.roll(x_wide[tap_row:tap_row + row_count], 2 - tap_col, axis=2)  21.7 us
    slice x2, local copies, waits for them, and re-layouts, shards(): jnp.roll(padded_grad[4 - tap_row:4 - tap_row + row_count], tap_col - 2, a...  21.6 us
    another operation x1, other arithmetic  20.8 us
    convert_element_type x1, other arithmetic, shards(): grad_input.astype(jnp.bfloat16)  13.1 us
    dot_general x1, matrix products, shards(): jnp.einsum('rcf,rdf->cd', hidden, grad_grid, preferred_element_type=jnp.f...  12.1 us
    all_to_all x1, waiting for transfers between devices, shards(): leg_rows = lax.all_to_all(legendre, 'lat', 0, 1, tiled=True)  10.9 us
    unnamed x133, local copies, waits for them, and re-layouts  10 us
  transfers between devices with their start and end apart: 14, of which 8 were waited for; matrix products, arithmetic and copies ran while one was open for 23% of the time, Pallas kernels for 0%

profile of v2, /device:TPU:1, one launch (start us, length us, event | category | flops | bytes accessed | tf_op | source)
XLA Modules:
  0.0 231.7 jit_solution(2990645944846890115)
XLA Ops:
  0.6 4.6 %collective-permute-start.2 = (bf16[2,128,1440]{1,2,0:T(8,128)(2,1)}, bf16[2,128,1440]{1,2,0:T(8,128)(2,1)S(1)}, u32[]{:S(2)}, u32[]{:S(2)}) collective-permute-start(bf16[2,128,1440]{1,2,0:T(8,128)(2,1)} %param.13), channel_id=1, source_target_pairs={{0,8},{8,16},{16,24},{24,32},{32,40},{40,48},{48,56},{56,64},{64,7... | collective-permute-start | bytes 2211848 | tf_op jit(solution)/shard_map/ppermute | solution.py:21
  5.2 1.9 collective-permute-start.3
  7.2 1.3 broadcast_in_dim.8
  8.4 7.4 %all-to-all-start.1 = ((f32[8,1,32]{2,1,0:T(1,128)}), f32[8,1,32]{2,1,0:T(1,128)S(1)}, u32[]{:S(2)}, u32[]{:S(2)}) async-start(f32[8,1,32]{2,1,0:T(1,128)} %broadcast_in_dim.8), calls=%async_computation.1 | async-start | bytes 8192 | tf_op jit(solution)/shard_map/all_to_all | solution.py:60
  15.8 0.7 fusion.88
  16.5 0.7 dynamic_slice.3
  17.2 20.8 %multiply_convert_fusion.1 = (bf16[768,1440]{0,1:T(8,128)(2,1)}, bf16[768,1440]{0,1:T(8,128)(2,1)}) fusion(s32[768]{0:T(1024)} %param.11, f32[768]{0:T(1024)S(1)} %get-tuple-element.147, f32[768]{0:T(1024)S(1)} %get-tuple-element.148), kind=kLoop, calls=%fused_computation.33 | loop fusion | flops 14376960 | bytes 4432896 | tf_op jit(solution)/shard_map/convert
  38.1 0.6 slice_bitcast_fusion.24
  38.8 6.8 %all-to-all-start = ((bf16[48,32,768]{2,1,0:T(8,128)(2,1)}), bf16[48,32,768]{2,1,0:T(8,128)(2,1)}, u32[]{:S(2)}, u32[]{:S(2)}) async-start(bf16[48,32,768]{2,1,0:T(8,128)(2,1)} %param.9), calls=%async_computation | async-start | bytes 4718592 | tf_op jit(solution)/shard_map/all_to_all | solution.py:58
  45.5 0.6 slice_bitcast_fusion.23
  46.7 0.7 reduce.3
  47.4 0.6 maximum_convert_fusion.19
  48.0 0.6 maximum_convert_fusion.20
  49.2 2.3 %maximum_convert_fusion.1 = f32[6,128,1440]{1,2,0:T(8,128)} fusion(bf16[2,128,1440]{1,2,0:T(8,128)(2,1)S(1)} %collective-permute-done.3, bf16[2,128,1440]{1,2,0:T(8,128)(2,1)S(1)} %copy-done.3, bf16[2,128,1440]{1,2,0:T(8,128)(2,1)S(1)} %collective-permute-done.2), kind=kLoop, calls=%fused_computation.45 | loop fusion | flops 3317760 | bytes 6635520 | tf_op jit(solution)/shard_map/convert_element_type | solution.py:56
  51.5 10.4 %fusion.97 = (f32[2,128,1439]{1,2,0:T(8,128)S(1)}, f32[2,128,1439]{1,2,0:T(8,128)}, f32[2,128,1439]{1,2,0:T(8,128)}, f32[2,128,1439]{1,2,0:T(8,128)}, f32[2,128,...) fusion(f32[6,128,1440]{1,2,0:T(8,128)} %maximum_convert_fusion.1), kind=kLoop, calls=%fused_computation.238 | loop fusion | bytes 29470720 | tf_op jit(solution)/shard_map/jit(_roll_static)/slice | solution.py:86
  62.0 10.9 %all-to-all-done = bf16[48,32,768]{2,1,0:T(8,128)(2,1)} async-done(((bf16[48,32,768]{2,1,0:T(8,128)(2,1)}), bf16[48,32,768]{2,1,0:T(8,128)(2,1)}, u32[]{:S(2)}, u32[]{:S(2)}) %all-to-all-start) | async-done | bytes 2359328 | tf_op jit(solution)/shard_map/all_to_all | solution.py:58
  72.9 3.3 %copy.24 = bf16[8,6,32,768]{3,2,0,1:T(8,128)(2,1)} copy(bf16[8,6,32,768]{3,2,1,0:T(8,128)(2,1)} %bitcast.2) | data formatting | bytes 4718592 | tf_op jit(solution)/shard_map/all_to_all | solution.py:58
  76.2 4.4 %fusion.72 = bf16[6,256,256]{1,2,0:T(8,128)(2,1)S(1)} fusion(bf16[6,256,768]{2,1,0:T(8,128)(2,1)} %bitcast.122, bf16[6,768,256]{2,1,0:T(8,128)(2,1)} %param.8, bf16[6,768]{1,0:T(8,128)(2,1)S(1)} %fusion.86, f32[256]{0:T(256)S(1)} %mul.561, s32[256]{0:T(256)S(1)} %fusion.92), kind=kOutput, calls=%fused_computation.145 | convolution fusion | flops 1211170816 | bytes 5516288 | tf_op jit(solution)/shard_map/slj,sjk->slk/dot_general | solution.py:69
  81.6 1.4 copy.28
  83.0 10.0 %all-to-all-start.2 = ((bf16[6,128,512]{2,0,1:T(8,128)(2,1)}), bf16[6,128,512]{2,0,1:T(8,128)(2,1)S(1)}, u32[]{:S(2)}, u32[]{:S(2)}) async-start(bf16[6,128,512]{2,0,1:T(8,128)(2,1)} %copy.28), calls=%async_computation.2 | async-start | bytes 2097152 | tf_op jit(solution)/shard_map/all_to_all | solution.py:73
  93.0 11.2 %fusion.96 = (f32[2,128,1438]{1,2,0:T(8,128)}, f32[2,128,1438]{1,2,0:T(8,128)}, f32[2,128,1438]{1,2,0:T(8,128)}, f32[2,128,1438]{1,2,0:T(8,128)}, f32[2,128,1438...) fusion(f32[6,128,1440]{1,2,0:T(8,128)} %maximum_convert_fusion.1), kind=kLoop, calls=%fused_computation.237 | loop fusion | bytes 29450240 | tf_op jit(solution)/shard_map/jit(_roll_static)/slice | solution.py:86
  104.2 8.2 %all-to-all-done.2 = bf16[6,128,512]{2,0,1:T(8,128)(2,1)S(1)} async-done(((bf16[6,128,512]{2,0,1:T(8,128)(2,1)}), bf16[6,128,512]{2,0,1:T(8,128)(2,1)S(1)}, u32[]{:S(2)}, u32[]{:S(2)}) %all-to-all-start.2) | async-done | bytes 786464 | tf_op jit(solution)/shard_map/all_to_all | solution.py:73
  112.5 1.1 reshape.104
  113.6 1.4 copy.29
  115.1 4.9 %fusion.2 = f32[2,2,128,2880]{2,3,1,0:T(8,128)S(1)} fusion(bf16[2,2,128,768]{3,2,1,0:T(8,128)(2,1)S(1)} %bitcast.123, bf16[768,1440]{0,1:T(8,128)(2,1)} %get-tuple-element.146, bf16[768,1440]{0,1:T(8,128)(2,1)} %get-tuple-element.145), kind=kOutput, calls=%fused_computation.29 | convolution fusion | flops 2273771520 | bytes 11108352 | tf_op jit(solution)/shard_map/sn,sq->nq/dot_general | solution.py:77
  120.8 1.5 fusion.39
  124.8 1.8 fusion.41
  129.7 1.8 fusion.40
  131.8 12.1 %convolution_bitcast_fusion = f32[128,128]{0,1:T(8,128)S(1)} fusion(bf16[2,128,1440]{1,2,0:T(8,128)(2,1)S(1)} %fusion.79, f32[6,128,1440]{1,2,0:T(8,128)S(1)} %bitcast.117, f32[2,128,1]{1,2,0:T(1,128)S(1)} %copy-done.29, f32[2,128,1439]{1,2,0:T(8,128)} %get-tuple-element.57, f32[2,128,1439]{1,2,0:T(8,128)} %get-tuple-element.56, ...), kind=kOutput, calls=%fused_computation.147 | convolution fusion | flops 120176640 | bytes 37689856 | tf_op jit(solution)/shard_map/rcf,rdf->cd/dot_general | solution.py:93
  144.4 2.1 collective-permute-start.1
  146.5 3.4 %collective-permute-start = (bf16[2,128,1440]{1,2,0:T(8,128)(2,1)S(1)}, bf16[2,128,1440]{1,2,0:T(8,128)(2,1)S(1)}, u32[]{:S(2)}, u32[]{:S(2)}) collective-permute-start(bf16[2,128,1440]{1,2,0:T(8,128)(2,1)S(1)} %get-tuple-element.149), channel_id=1, source_target_pairs={{0,8},{8,16},{16,24},{24,32},{32,40},{40,48},{48,56},{56,64},{64,7... | collective-permute-start | bytes 2211848 | tf_op jit(solution)/shard_map/ppermute | solution.py:21
  150.0 1.7 collective-permute-start.5
  151.7 16.7 %collective-permute-done.5 = f32[128,153]{0,1:T(8,128)S(1)} collective-permute-done((f32[128,153]{0,1:T(8,128)S(1)}, f32[128,153]{0,1:T(8,128)S(1)}, u32[]{:S(2)}, u32[]{:S(2)}) %collective-permute-start.5) | collective-permute-done | bytes 78368 | tf_op jit(solution)/shard_map/ppermute | solution.py:32
  168.4 0.6 collective-permute-start.6
  169.0 3.0 %collective-permute-done.6 = f32[128,153]{0,1:T(8,128)S(1)} collective-permute-done((f32[128,153]{0,1:T(8,128)S(1)}, f32[128,153]{0,1:T(8,128)S(1)}, u32[]{:S(2)}, u32[]{:S(2)}) %collective-permute-start.6) | collective-permute-done | bytes 78368 | tf_op jit(solution)/shard_map/ppermute | solution.py:32
  172.6 4.3 %collective-permute-done.7 = f32[128,153]{0,1:T(8,128)S(1)} collective-permute-done((f32[128,153]{0,1:T(8,128)S(1)}, f32[128,153]{0,1:T(8,128)S(1)}, u32[]{:S(2)}, u32[]{:S(2)}) %collective-permute-start.7) | collective-permute-done | bytes 78368 | tf_op jit(solution)/shard_map/ppermute | solution.py:32
  177.0 3.3 %collective-permute-done.8 = f32[128,153]{0,1:T(8,128)S(1)} collective-permute-done((f32[128,153]{0,1:T(8,128)S(1)}, f32[128,153]{0,1:T(8,128)S(1)}, u32[]{:S(2)}, u32[]{:S(2)}) %collective-permute-start.8) | collective-permute-done | bytes 78368 | tf_op jit(solution)/shard_map/ppermute | solution.py:32
  180.4 3.9 %collective-permute-done.9 = f32[128,153]{0,1:T(8,128)S(1)} collective-permute-done((f32[128,153]{0,1:T(8,128)S(1)}, f32[128,153]{0,1:T(8,128)S(1)}, u32[]{:S(2)}, u32[]{:S(2)}) %collective-permute-start.9) | collective-permute-done | bytes 78368 | tf_op jit(solution)/shard_map/ppermute | solution.py:32
  184.3 0.7 collective-permute-start.10
  185.0 4.4 %collective-permute-done.10 = f32[128,153]{0,1:T(8,128)S(1)} collective-permute-done((f32[128,153]{0,1:T(8,128)S(1)}, f32[128,153]{0,1:T(8,128)S(1)}, u32[]{:S(2)}, u32[]{:S(2)}) %collective-permute-start.10) | collective-permute-done | bytes 78368 | tf_op jit(solution)/shard_map/ppermute | solution.py:32
  189.5 0.6 slice.747
  190.1 0.7 copy.30
  190.8 2.4 %maximum_convert_fusion = f32[6,128,1440]{1,2,0:T(8,128)} fusion(bf16[2,128,1440]{1,2,0:T(8,128)(2,1)S(1)} %collective-permute-done.1, bf16[2,128,1440]{1,2,0:T(8,128)(2,1)S(1)} %get-tuple-element.149, bf16[2,128,1440]{1,2,0:T(8,128)(2,1)S(1)} %collective-permute-done), kind=kLoop, calls=%fused_computation.44 | loop fusion | flops 3317760 | bytes 6635520 | tf_op jit(solution)/shard_map/convert_element_type | solution.py:103
  193.2 10.8 %fusion.99 = (f32[2,128,1439]{1,2,0:T(8,128)}, f32[2,128,1439]{1,2,0:T(8,128)}, f32[2,128,1439]{1,2,0:T(8,128)}, f32[2,128,1439]{1,2,0:T(8,128)}, f32[2,128,1439...) fusion(f32[6,128,1440]{1,2,0:T(8,128)} %maximum_convert_fusion), kind=kLoop, calls=%fused_computation.240 | loop fusion | bytes 29470720 | tf_op jit(solution)/shard_map/jit(_roll_static)/slice | solution.py:108
  204.0 10.8 %fusion.98 = (f32[2,128,1438]{1,2,0:T(8,128)}, f32[2,128,1438]{1,2,0:T(8,128)}, f32[2,128,1438]{1,2,0:T(8,128)}, f32[2,128,1438]{1,2,0:T(8,128)}, f32[2,128,1438...) fusion(f32[6,128,1440]{1,2,0:T(8,128)} %maximum_convert_fusion), kind=kLoop, calls=%fused_computation.239 | loop fusion | bytes 29450240 | tf_op jit(solution)/shard_map/jit(_roll_static)/slice | solution.py:108
  214.9 1.3 copy-done.22
  217.1 1.3 copy-done.2
  218.5 13.1 %fusion.45 = bf16[2,128,1440]{1,2,0:T(8,128)(2,1)} fusion(f32[6,128,1440]{1,2,0:T(8,128)S(1)} %copy-done.2, f32[2,128,2]{1,2,0:T(2,128)S(1)} %get-tuple-element.115, f32[2,128,1438]{1,2,0:T(8,128)} %get-tuple-element.69, f32[2,128,1]{1,2,0:T(1,128)S(1)} %get-tuple-element.119, f32[2,128,1439]{1,2,0:T(8,128)} %get-tuple-element.79, ...), kind=kLoop, calls=%fused_computation.76 | loop fusion | flops 25804800 | bytes 37614080 | tf_op jit(solution)/shard_map/convert_element_type | solution.py:114
  (164 shorter events, 10.4 us)
Async XLA Ops:
  0.6 119.6 %copy-start = (bf16[128,128]{1,0:T(8,128)(2,1)S(1)}, bf16[128,128]{1,0:T(8,128)(2,1)}, u32[]{:S(2)}) copy-start(bf16[128,128]{1,0:T(8,128)(2,1)} %param.15) | copy-start | bytes 98308
  0.6 46.8 %collective-permute-start.2 = (bf16[2,128,1440]{1,2,0:T(8,128)(2,1)}, bf16[2,128,1440]{1,2,0:T(8,128)(2,1)S(1)}, u32[]{:S(2)}, u32[]{:S(2)}) collective-permute-start(bf16[2,128,1440]{1,2,0:T(8,128)(2,1)} %param.13), channel_id=1, source_target_pairs={{0,8},{8,16},{16,24},{24,32},{32,40},{40,48},{48,56},{56,64},{64,7... | collective-permute-start | bytes 2211848 | tf_op jit(solution)/shard_map/ppermute | solution.py:21
  5.2 42.2 %collective-permute-start.3 = (bf16[2,128,1440]{1,2,0:T(8,128)(2,1)}, bf16[2,128,1440]{1,2,0:T(8,128)(2,1)S(1)}, u32[]{:S(2)}, u32[]{:S(2)}) collective-permute-start(bf16[2,128,1440]{1,2,0:T(8,128)(2,1)} %param.13), channel_id=1, source_target_pairs={{8,0},{16,8},{24,16},{32,24},{40,32},{48,40},{56,48},{64,56},{72,6... | collective-permute-start | bytes 2211848 | tf_op jit(solution)/shard_map/ppermute | solution.py:22
  8.4 30.3 %all-to-all-start.1 = ((f32[8,1,32]{2,1,0:T(1,128)}), f32[8,1,32]{2,1,0:T(1,128)S(1)}, u32[]{:S(2)}, u32[]{:S(2)}) async-start(f32[8,1,32]{2,1,0:T(1,128)} %broadcast_in_dim.8), calls=%async_computation.1 | async-start | bytes 8192 | tf_op jit(solution)/shard_map/all_to_all | solution.py:60
  17.2 20.9 %copy-start.26 = (f32[128,25]{0,1:T(8,128)S(1)}, f32[128,25]{0,1:T(8,128)}, u32[]{:S(2)}) copy-start(f32[128,25]{0,1:T(8,128)} %param.14) | copy-start | bytes 38404
  38.7 8.7 %copy-start.3 = (bf16[2,128,1440]{1,2,0:T(8,128)(2,1)S(1)}, bf16[2,128,1440]{1,2,0:T(8,128)(2,1)}, u32[]{:S(2)}) copy-start(bf16[2,128,1440]{1,2,0:T(8,128)(2,1)} %param.13) | copy-start | bytes 2211844
  38.8 34.2 %all-to-all-start = ((bf16[48,32,768]{2,1,0:T(8,128)(2,1)}), bf16[48,32,768]{2,1,0:T(8,128)(2,1)}, u32[]{:S(2)}, u32[]{:S(2)}) async-start(bf16[48,32,768]{2,1,0:T(8,128)(2,1)} %param.9), calls=%async_computation | async-start | bytes 4718592 | tf_op jit(solution)/shard_map/all_to_all | solution.py:58
  83.0 29.5 %all-to-all-start.2 = ((bf16[6,128,512]{2,0,1:T(8,128)(2,1)}), bf16[6,128,512]{2,0,1:T(8,128)(2,1)S(1)}, u32[]{:S(2)}, u32[]{:S(2)}) async-start(bf16[6,128,512]{2,0,1:T(8,128)(2,1)} %copy.28), calls=%async_computation.2 | async-start | bytes 2097152 | tf_op jit(solution)/shard_map/all_to_all | solution.py:73
  113.6 6.6 %slice-start = ((s8[4423680]{0:T(1024)(128)(4,1)}), s8[229376]{0:T(1024)(128)(4,1)S(1)}, s32[]{:S(2)}) async-start(s8[4423680]{0:T(1024)(128)(4,1)} %bitcast.116), calls=%async_computation.3 | async-start | bytes 458752
  115.1 5.2 %slice-start.1 = ((s8[4423680]{0:T(1024)(128)(4,1)}), s8[4194304]{0:T(1024)(128)(4,1)S(1)}, s32[]{:S(2)}) async-start(s8[4423680]{0:T(1024)(128)(4,1)} %bitcast.116), calls=%async_computation.4 | async-start | bytes 8388608
  115.1 5.2 %copy-start.24 = (f32[2,128,1439]{1,2,0:T(8,128)S(1)}, f32[2,128,1439]{1,2,0:T(8,128)}, u32[]{:S(2)}) copy-start(f32[2,128,1439]{1,2,0:T(8,128)} %get-tuple-element.56) | copy-start | bytes 4420612
  115.1 5.2 %copy-start.25 = (f32[2,128,1438]{1,2,0:T(8,128)S(1)}, f32[2,128,1438]{1,2,0:T(8,128)}, u32[]{:S(2)}) copy-start(f32[2,128,1438]{1,2,0:T(8,128)} %get-tuple-element.40) | copy-start | bytes 4417540
  120.0 2.3 copy-start.10
  120.0 2.3 copy-start.11
  120.7 2.2 copy-start.5
  120.7 2.6 %copy-start.6 = (f32[2,128,1439]{1,2,0:T(8,128)S(1)}, f32[2,128,1439]{1,2,0:T(8,128)}, u32[]{:S(2)}) copy-start(f32[2,128,1439]{1,2,0:T(8,128)} %get-tuple-element.59) | copy-start | bytes 4420612
  120.7 3.1 %copy-start.7 = (f32[2,128,1438]{1,2,0:T(8,128)S(1)}, f32[2,128,1438]{1,2,0:T(8,128)}, u32[]{:S(2)}) copy-start(f32[2,128,1438]{1,2,0:T(8,128)} %get-tuple-element.41) | copy-start | bytes 4417540
  120.7 3.5 %copy-start.8 = (f32[2,128,1438]{1,2,0:T(8,128)S(1)}, f32[2,128,1438]{1,2,0:T(8,128)}, u32[]{:S(2)}) copy-start(f32[2,128,1438]{1,2,0:T(8,128)} %get-tuple-element.44) | copy-start | bytes 4417540
  120.7 3.9 %copy-start.9 = (f32[2,128,1438]{1,2,0:T(8,128)S(1)}, f32[2,128,1438]{1,2,0:T(8,128)}, u32[]{:S(2)}) copy-start(f32[2,128,1438]{1,2,0:T(8,128)} %get-tuple-element.46) | copy-start | bytes 4417540
  120.7 3.9 %copy-start.28 = (f32[2,128,1]{1,2,0:T(1,128)S(1)}, f32[2,128,1]{1,2,0:T(1,128)}, u32[]{:S(2)}) copy-start(f32[2,128,1]{1,2,0:T(1,128)} %get-tuple-element.90) | copy-start | bytes 3076
  120.8 3.9 %copy-start.33 = (f32[2,128,1]{1,2,0:T(1,128)S(1)}, f32[2,128,1]{1,2,0:T(1,128)}, u32[]{:S(2)}) copy-start(f32[2,128,1]{1,2,0:T(1,128)} %get-tuple-element.96) | copy-start | bytes 3076
  120.8 3.9 %copy-start.35 = (f32[2,128,1]{1,2,0:T(1,128)S(1)}, f32[2,128,1]{1,2,0:T(1,128)}, u32[]{:S(2)}) copy-start(f32[2,128,1]{1,2,0:T(1,128)} %get-tuple-element.98) | copy-start | bytes 3076
  120.8 3.8 %copy-start.36 = (f32[2,128,1]{1,2,0:T(1,128)S(1)}, f32[2,128,1]{1,2,0:T(1,128)}, u32[]{:S(2)}) copy-start(f32[2,128,1]{1,2,0:T(1,128)} %get-tuple-element.99) | copy-start | bytes 3076
  124.6 2.2 copy-start.14
  124.7 2.7 %copy-start.15 = (f32[2,128,1439]{1,2,0:T(8,128)S(1)}, f32[2,128,1439]{1,2,0:T(8,128)}, u32[]{:S(2)}) copy-start(f32[2,128,1439]{1,2,0:T(8,128)} %get-tuple-element.57) | copy-start | bytes 4420612
  124.7 3.1 %copy-start.16 = (f32[2,128,1439]{1,2,0:T(8,128)S(1)}, f32[2,128,1439]{1,2,0:T(8,128)}, u32[]{:S(2)}) copy-start(f32[2,128,1439]{1,2,0:T(8,128)} %get-tuple-element.58) | copy-start | bytes 4420612
  124.7 3.5 %copy-start.17 = (f32[2,128,1438]{1,2,0:T(8,128)S(1)}, f32[2,128,1438]{1,2,0:T(8,128)}, u32[]{:S(2)}) copy-start(f32[2,128,1438]{1,2,0:T(8,128)} %get-tuple-element.42) | copy-start | bytes 4417540
  124.7 3.9 %copy-start.18 = (f32[2,128,1438]{1,2,0:T(8,128)S(1)}, f32[2,128,1438]{1,2,0:T(8,128)}, u32[]{:S(2)}) copy-start(f32[2,128,1438]{1,2,0:T(8,128)} %get-tuple-element.43) | copy-start | bytes 4417540
  124.7 4.3 %copy-start.19 = (f32[2,128,1438]{1,2,0:T(8,128)S(1)}, f32[2,128,1438]{1,2,0:T(8,128)}, u32[]{:S(2)}) copy-start(f32[2,128,1438]{1,2,0:T(8,128)} %get-tuple-element.45) | copy-start | bytes 4417540
  124.7 4.8 %copy-start.20 = (f32[2,128,1438]{1,2,0:T(8,128)S(1)}, f32[2,128,1438]{1,2,0:T(8,128)}, u32[]{:S(2)}) copy-start(f32[2,128,1438]{1,2,0:T(8,128)} %get-tuple-element.49) | copy-start | bytes 4417540
  124.7 4.7 %copy-start.27 = (f32[2,128,2]{1,2,0:T(2,128)S(1)}, f32[2,128,2]{1,2,0:T(2,128)}, u32[]{:S(2)}) copy-start(f32[2,128,2]{1,2,0:T(2,128)} %get-tuple-element.85) | copy-start | bytes 6148
  124.7 4.7 %copy-start.29 = (f32[2,128,1]{1,2,0:T(1,128)S(1)}, f32[2,128,1]{1,2,0:T(1,128)}, u32[]{:S(2)}) copy-start(f32[2,128,1]{1,2,0:T(1,128)} %get-tuple-element.91) | copy-start | bytes 3076
  124.7 4.7 %copy-start.30 = (f32[2,128,1]{1,2,0:T(1,128)S(1)}, f32[2,128,1]{1,2,0:T(1,128)}, u32[]{:S(2)}) copy-start(f32[2,128,1]{1,2,0:T(1,128)} %get-tuple-element.93) | copy-start | bytes 3076
  124.7 4.7 %copy-start.31 = (f32[2,128,1]{1,2,0:T(1,128)S(1)}, f32[2,128,1]{1,2,0:T(1,128)}, u32[]{:S(2)}) copy-start(f32[2,128,1]{1,2,0:T(1,128)} %get-tuple-element.94) | copy-start | bytes 3076
  124.8 4.7 %copy-start.32 = (f32[2,128,1]{1,2,0:T(1,128)S(1)}, f32[2,128,1]{1,2,0:T(1,128)}, u32[]{:S(2)}) copy-start(f32[2,128,1]{1,2,0:T(1,128)} %get-tuple-element.95) | copy-start | bytes 3076
  124.8 4.7 %copy-start.34 = (f32[2,128,1]{1,2,0:T(1,128)S(1)}, f32[2,128,1]{1,2,0:T(1,128)}, u32[]{:S(2)}) copy-start(f32[2,128,1]{1,2,0:T(1,128)} %get-tuple-element.97) | copy-start | bytes 3076
  144.0 5.9 %collective-permute-start.4 = (f32[128,153]{0,1:T(8,128)S(1)}, f32[128,153]{0,1:T(8,128)S(1)}, u32[]{:S(2)}, u32[]{:S(2)}) collective-permute-start(f32[128,153]{0,1:T(8,128)S(1)} %concatenate.200), channel_id=1, source_target_pairs={{0,8},{1,9},{2,10},{3,11},{4,12},{5,13},{6,14},{7,15},{8,0},{9,1},... | collective-permute-start | bytes 235016 | tf_op jit(solution)/shard_map/ppermute | solution.py:32
  144.4 46.4 %collective-permute-start.1 = (bf16[2,128,1440]{1,2,0:T(8,128)(2,1)S(1)}, bf16[2,128,1440]{1,2,0:T(8,128)(2,1)S(1)}, u32[]{:S(2)}, u32[]{:S(2)}) collective-permute-start(bf16[2,128,1440]{1,2,0:T(8,128)(2,1)S(1)} %get-tuple-element.149), channel_id=1, source_target_pairs={{8,0},{16,8},{24,16},{32,24},{40,32},{48,40},{56,48},{64,56},{72,6... | collective-permute-start | bytes 2211848 | tf_op jit(solution)/shard_map/ppermute | solution.py:22
  146.5 44.3 %collective-permute-start = (bf16[2,128,1440]{1,2,0:T(8,128)(2,1)S(1)}, bf16[2,128,1440]{1,2,0:T(8,128)(2,1)S(1)}, u32[]{:S(2)}, u32[]{:S(2)}) collective-permute-start(bf16[2,128,1440]{1,2,0:T(8,128)(2,1)S(1)} %get-tuple-element.149), channel_id=1, source_target_pairs={{0,8},{8,16},{16,24},{24,32},{32,40},{40,48},{48,56},{56,64},{64,7... | collective-permute-start | bytes 2211848 | tf_op jit(solution)/shard_map/ppermute | solution.py:21
  150.0 18.4 %collective-permute-start.5 = (f32[128,153]{0,1:T(8,128)S(1)}, f32[128,153]{0,1:T(8,128)S(1)}, u32[]{:S(2)}, u32[]{:S(2)}) collective-permute-start(f32[128,153]{0,1:T(8,128)S(1)} %add.253), channel_id=1, source_target_pairs={{0,1},{1,0},{2,3},{3,2},{4,5},{5,4},{6,7},{7,6},{8,9},{9,8},{10,11... | collective-permute-start | bytes 235016 | tf_op jit(solution)/shard_map/ppermute | solution.py:32
  168.4 3.7 %collective-permute-start.6 = (f32[128,153]{0,1:T(8,128)S(1)}, f32[128,153]{0,1:T(8,128)S(1)}, u32[]{:S(2)}, u32[]{:S(2)}) collective-permute-start(f32[128,153]{0,1:T(8,128)S(1)} %add.254), channel_id=1, source_target_pairs={{0,2},{1,3},{2,0},{3,1},{4,6},{5,7},{6,4},{7,5},{8,10},{9,11},{10,... | collective-permute-start | bytes 235016 | tf_op jit(solution)/shard_map/ppermute | solution.py:32
  172.1 4.9 %collective-permute-start.7 = (f32[128,153]{0,1:T(8,128)S(1)}, f32[128,153]{0,1:T(8,128)S(1)}, u32[]{:S(2)}, u32[]{:S(2)}) collective-permute-start(f32[128,153]{0,1:T(8,128)S(1)} %add.255), channel_id=1, source_target_pairs={{0,4},{1,5},{2,6},{3,7},{4,0},{5,1},{6,2},{7,3},{8,12},{9,13},{10,... | collective-permute-start | bytes 235016 | tf_op jit(solution)/shard_map/ppermute | solution.py:32
  177.0 3.4 %collective-permute-start.8 = (f32[128,153]{0,1:T(8,128)S(1)}, f32[128,153]{0,1:T(8,128)S(1)}, u32[]{:S(2)}, u32[]{:S(2)}) collective-permute-start(f32[128,153]{0,1:T(8,128)S(1)} %add.256), channel_id=1, source_target_pairs={{0,16},{1,17},{2,18},{3,19},{4,20},{5,21},{6,22},{7,23},{8,24},{9,... | collective-permute-start | bytes 235016 | tf_op jit(solution)/shard_map/ppermute | solution.py:32
  180.3 4.0 %collective-permute-start.9 = (f32[128,153]{0,1:T(8,128)S(1)}, f32[128,153]{0,1:T(8,128)S(1)}, u32[]{:S(2)}, u32[]{:S(2)}) collective-permute-start(f32[128,153]{0,1:T(8,128)S(1)} %add.257), channel_id=1, source_target_pairs={{0,32},{1,33},{2,34},{3,35},{4,36},{5,37},{6,38},{7,39},{8,40},{9,... | collective-permute-start | bytes 235016 | tf_op jit(solution)/shard_map/ppermute | solution.py:32
  184.3 5.1 %collective-permute-start.10 = (f32[128,153]{0,1:T(8,128)S(1)}, f32[128,153]{0,1:T(8,128)S(1)}, u32[]{:S(2)}, u32[]{:S(2)}) collective-permute-start(f32[128,153]{0,1:T(8,128)S(1)} %add.258), channel_id=1, source_target_pairs={{0,64},{1,65},{2,66},{3,67},{4,68},{5,69},{6,70},{7,71},{8,72},{9,... | collective-permute-start | bytes 235016 | tf_op jit(solution)/shard_map/ppermute | solution.py:32
  214.9 2.2 copy-start.21
  214.9 3.6 %copy-start.2 = (f32[6,128,1440]{1,2,0:T(8,128)S(1)}, f32[6,128,1440]{1,2,0:T(8,128)}, u32[]{:S(2)}) copy-start(f32[6,128,1440]{1,2,0:T(8,128)} %maximum_convert_fusion) | copy-start | bytes 13271044
  218.4 13.1 %copy-start.1 = (bf16[128,128]{1,0:T(8,128)(2,1)S(1)}, bf16[128,128]{1,0:T(8,128)(2,1)}, u32[]{:S(2)}) copy-start(bf16[128,128]{1,0:T(8,128)(2,1)} %param.15) | copy-start | bytes 98308
  (32 other events, 61.6 us)

commit v3 on v2

--- a/solution.py
+++ b/solution.py
@@ -4,6 +4,7 @@
 import jax.numpy as jnp
 from jax import lax
 from jax.sharding import PartitionSpec as P
+
 
 MESH_AXES = ("ord", "lat")
 
@@ -23,14 +24,19 @@
     return jnp.concatenate([upper, field, lower], axis=0)
 
 
-def butterfly_sum(value):
+def butterfly_sum(value, carry, steps):
     count = lax.axis_size("ord") * lax.axis_size("lat")
     bits = count.bit_length() - 1
     order = sorted(range(bits), key=lambda b: (b != 3, b))
-    for bit in order:
+    for round_index, bit in enumerate(order):
         pairs = [(d, d ^ (1 << bit)) for d in range(count)]
-        value = value + lax.ppermute(value, MESH_AXES, pairs)
-    return value
+        received = lax.ppermute(value, MESH_AXES, pairs)
+        if round_index < len(steps):
+            carry = steps[round_index](carry)
+        value, carry = lax.optimization_barrier((value + received, carry))
+    for step in steps[len(order):]:
+        carry = step(carry)
+    return value, carry
 
 
 def make_table(orders, length):
@@ -44,7 +50,7 @@
     return jnp.concatenate(parts, axis=1).astype(jnp.bfloat16)
 
 
-def shards(
+def layer(
     grad_coef, legendre, quad_weight, slot_order, slot_count, conv_input, depth_kernel, point_weight
 ):
     n_ord = lax.axis_size("ord")
@@ -98,16 +104,28 @@
             shifted_x = jnp.roll(x_wide[tap_row : tap_row + row_count], 2 - tap_col, axis=2)
             depth_terms.append(jnp.sum(hidden_wide * shifted_x, axis=(0, 2)))
     depth_part = jnp.stack(depth_terms, axis=1)
-    sums = butterfly_sum(jnp.concatenate([point_part, depth_part], axis=1))
+    padded_grad = with_rims(grad_hidden).astype(jnp.float32)
+    taps = [(tap_row, tap_col) for tap_row in range(5) for tap_col in range(5)]
+    rounds = (n_ord * n_lat).bit_length() - 1
+    groups = [taps[i * len(taps) // rounds : (i + 1) * len(taps) // rounds] for i in range(rounds)]
 
-    padded_grad = with_rims(grad_hidden).astype(jnp.float32)
+    def tap_group(group):
+        def step(grad_input):
+            for tap_row, tap_col in group:
+                weight_tap = depth_kernel[:, 5 * tap_row + tap_col][None, :, None]
+                grad_input = grad_input + weight_tap * jnp.roll(
+                    padded_grad[4 - tap_row : 4 - tap_row + row_count], tap_col - 2, axis=2
+                )
+            return grad_input
+
+        return step
+
     grad_input = jnp.zeros((row_count, channels, longitudes), jnp.float32)
-    for tap_row in range(5):
-        for tap_col in range(5):
-            weight_tap = depth_kernel[:, 5 * tap_row + tap_col][None, :, None]
-            grad_input = grad_input + weight_tap * jnp.roll(
-                padded_grad[4 - tap_row : 4 - tap_row + row_count], tap_col - 2, axis=2
-            )
+    sums, grad_input = butterfly_sum(
+        jnp.concatenate([point_part, depth_part], axis=1),
+        grad_input,
+        [tap_group(group) for group in groups],
+    )
     total_rows = row_count * n_ord * n_lat
     grad_scale = 1.0 / math.sqrt(total_rows * longitudes)
     sums = sums * grad_scale
@@ -116,7 +134,7 @@
 
 def solution(mesh):
     return jax.shard_map(
-        shards,
+        layer,
         mesh=mesh,
         in_specs=(
             P(("ord", "lat"), None, None),

time: 234 us -> 208 us (0.89)
  the two profiles are of different devices: /device:TPU:1 before, /device:TPU:30 now
where the time goes in v3:
time: 208 us
  local copies, waits for them, and re-layouts  58.3 us (28%)
  waiting for transfers between devices  46.4 us (22%)
  starting transfers between devices  40.4 us (19%)
  other arithmetic  38.8 us (19%)
  matrix products  22.3 us (11%)
    ppermute x7, waiting for transfers between devices, butterfly_sum(): received = lax.ppermute(value, MESH_AXES, pairs)  27.2 us
    slice x2, local copies, waits for them, and re-layouts, step(): jnp.roll(padded_grad[4 - tap_row:4 - tap_row + row_count], tap_col - 2, a...  21.7 us
    slice x2, local copies, waits for them, and re-layouts, layer(): jnp.roll(x_wide[tap_row:tap_row + row_count], 2 - tap_col, axis=2)  20.8 us
    another operation x1, other arithmetic  20.8 us
    all_to_all x1, waiting for transfers between devices, layer(): leg_rows = lax.all_to_all(legendre, 'lat', 0, 1, tiled=True)  13.4 us
    dot_general x1, matrix products, layer(): jnp.einsum('rcf,rdf->cd', hidden, grad_grid, preferred_element_type=jnp.f...  12.2 us
    all_to_all x1, starting transfers between devices, layer(): weights = lax.all_to_all(spread, 'lat', 0, 0, tiled=True).reshape(-1)  8.28 us
    all_to_all x1, starting transfers between devices, layer(): own_rows = lax.all_to_all(by_device, MESH_AXES, 1, 0, tiled=True)  7.87 us
  transfers between devices with their start and end apart: 14, of which 9 were waited for; matrix products, arithmetic and copies ran while one was open for 34% of the time, Pallas kernels for 0%

profile of v3, /device:TPU:30, one launch (start us, length us, event | category | flops | bytes accessed | tf_op | source)
XLA Modules:
  0.0 207.6 jit_solution(11686143864726456235)
XLA Ops:
  0.6 1.9 collective-permute-start
  2.6 3.6 %collective-permute-start.1 = (bf16[2,128,1440]{1,2,0:T(8,128)(2,1)}, bf16[2,128,1440]{1,2,0:T(8,128)(2,1)S(1)}, u32[]{:S(2)}, u32[]{:S(2)}) collective-permute-start(bf16[2,128,1440]{1,2,0:T(8,128)(2,1)} %param.13), channel_id=1, source_target_pairs={{8,0},{16,8},{24,16},{32,24},{40,32},{48,40},{56,48},{64,56},{72,6... | collective-permute-start | bytes 2211848 | tf_op jit(solution)/shard_map/ppermute | solution.py:23
  6.2 1.3 broadcast_in_dim.8
  7.5 8.3 %all-to-all-start.1 = ((f32[8,1,32]{2,1,0:T(1,128)}), f32[8,1,32]{2,1,0:T(1,128)S(1)}, u32[]{:S(2)}, u32[]{:S(2)}) async-start(f32[8,1,32]{2,1,0:T(1,128)} %broadcast_in_dim.8), calls=%async_computation.1 | async-start | bytes 8192 | tf_op jit(solution)/shard_map/all_to_all | solution.py:66
  15.8 0.7 fusion.87
  16.4 0.7 dynamic_slice.3
  17.2 20.8 %multiply_convert_fusion.1 = (bf16[768,1440]{0,1:T(8,128)(2,1)}, bf16[768,1440]{0,1:T(8,128)(2,1)}) fusion(s32[768]{0:T(1024)} %param.11, f32[768]{0:T(1024)S(1)} %get-tuple-element.175, f32[768]{0:T(1024)S(1)} %get-tuple-element.176), kind=kLoop, calls=%fused_computation.33 | loop fusion | flops 14376960 | bytes 4432896 | tf_op jit(solution)/shard_map/convert
  38.1 7.4 %all-to-all-start = ((bf16[48,32,768]{2,1,0:T(8,128)(2,1)}), bf16[48,32,768]{2,1,0:T(8,128)(2,1)}, u32[]{:S(2)}, u32[]{:S(2)}) async-start(bf16[48,32,768]{2,1,0:T(8,128)(2,1)} %param.9), calls=%async_computation | async-start | bytes 4718592 | tf_op jit(solution)/shard_map/all_to_all | solution.py:64
  45.4 0.5 broadcast.80
  45.9 0.7 reduce.3
  46.8 2.3 %maximum_convert_fusion = f32[6,128,1440]{1,2,0:T(8,128)} fusion(bf16[2,128,1440]{1,2,0:T(8,128)(2,1)S(1)} %collective-permute-done.1, bf16[2,128,1440]{1,2,0:T(8,128)(2,1)S(1)} %copy-done.3, bf16[2,128,1440]{1,2,0:T(8,128)(2,1)S(1)} %collective-permute-done), kind=kLoop, calls=%fused_computation.44 | loop fusion | flops 3317760 | bytes 6635520 | tf_op jit(solution)/shard_map/convert_element_type | solution.py:62
  49.1 10.6 %fusion.98 = (f32[2,128,1439]{1,2,0:T(8,128)}, f32[2,128,1439]{1,2,0:T(8,128)}, f32[2,128,1439]{1,2,0:T(8,128)}, f32[2,128,1439]{1,2,0:T(8,128)}, f32[2,128,1439...) fusion(f32[6,128,1440]{1,2,0:T(8,128)} %maximum_convert_fusion), kind=kLoop, calls=%fused_computation.239 | loop fusion | bytes 29470720 | tf_op jit(solution)/shard_map/jit(_roll_static)/slice | solution.py:92
  59.7 13.4 %all-to-all-done = bf16[48,32,768]{2,1,0:T(8,128)(2,1)} async-done(((bf16[48,32,768]{2,1,0:T(8,128)(2,1)}), bf16[48,32,768]{2,1,0:T(8,128)(2,1)}, u32[]{:S(2)}, u32[]{:S(2)}) %all-to-all-start) | async-done | bytes 2359328 | tf_op jit(solution)/shard_map/all_to_all | solution.py:64
  73.1 1.9 copy.24
  75.0 3.7 %fusion.71 = bf16[6,256,256]{1,2,0:T(8,128)(2,1)S(1)} fusion(bf16[6,256,768]{2,1,0:T(8,128)(2,1)S(1)} %bitcast.122, bf16[6,768,256]{2,1,0:T(8,128)(2,1)} %param.8, bf16[6,768]{1,0:T(8,128)(2,1)S(1)} %fusion.85, f32[256]{0:T(256)S(1)} %mul.634, s32[256]{0:T(256)S(1)} %fusion.91), kind=kOutput, calls=%fused_computation.144 | convolution fusion | flops 1211170816 | bytes 5516288 | tf_op jit(solution)/shard_map/slj,sjk->slk/dot_general | solution.py:75
  79.7 1.4 copy.28
  81.1 7.9 %all-to-all-start.2 = ((bf16[6,128,512]{2,0,1:T(8,128)(2,1)}), bf16[6,128,512]{2,0,1:T(8,128)(2,1)S(1)}, u32[]{:S(2)}, u32[]{:S(2)}) async-start(bf16[6,128,512]{2,0,1:T(8,128)(2,1)} %copy.28), calls=%async_computation.2 | async-start | bytes 2097152 | tf_op jit(solution)/shard_map/all_to_all | solution.py:79
  89.0 10.2 %fusion.97 = (f32[2,128,1438]{1,2,0:T(8,128)S(1)}, f32[2,128,1438]{1,2,0:T(8,128)}, f32[2,128,1438]{1,2,0:T(8,128)}, f32[2,128,1438]{1,2,0:T(8,128)}, f32[2,128,...) fusion(f32[6,128,1440]{1,2,0:T(8,128)} %maximum_convert_fusion), kind=kLoop, calls=%fused_computation.238 | loop fusion | bytes 29450240 | tf_op jit(solution)/shard_map/jit(_roll_static)/slice | solution.py:92
  99.2 5.8 %all-to-all-done.2 = bf16[6,128,512]{2,0,1:T(8,128)(2,1)S(1)} async-done(((bf16[6,128,512]{2,0,1:T(8,128)(2,1)}), bf16[6,128,512]{2,0,1:T(8,128)(2,1)S(1)}, u32[]{:S(2)}, u32[]{:S(2)}) %all-to-all-start.2) | async-done | bytes 786464 | tf_op jit(solution)/shard_map/all_to_all | solution.py:79
  105.6 4.9 %fusion.2 = f32[2,2,128,2880]{2,3,1,0:T(8,128)S(1)} fusion(bf16[2,2,128,768]{3,2,1,0:T(8,128)(2,1)S(1)} %bitcast.123, bf16[768,1440]{0,1:T(8,128)(2,1)} %get-tuple-element.174, bf16[768,1440]{0,1:T(8,128)(2,1)} %get-tuple-element.173), kind=kOutput, calls=%fused_computation.29 | convolution fusion | flops 2273771520 | bytes 11108352 | tf_op jit(solution)/shard_map/sn,sq->nq/dot_general | solution.py:83
  110.7 1.2 copy-done.37
  111.9 1.5 fusion.39
  113.4 2.3 %collective-permute-start.4 = (bf16[2,128,1440]{1,2,0:T(8,128)(2,1)S(1)}, bf16[2,128,1440]{1,2,0:T(8,128)(2,1)S(1)}, u32[]{:S(2)}, u32[]{:S(2)}) collective-permute-start(bf16[2,128,1440]{1,2,0:T(8,128)(2,1)S(1)} %get-tuple-element.177), channel_id=1, source_target_pairs={{8,0},{16,8},{24,16},{32,24},{40,32},{48,40},{56,48},{64,56},{72,6... | collective-permute-start | bytes 2211848 | tf_op jit(solution)/shard_map/ppermute | solution.py:23
  115.8 2.2 %collective-permute-start.3 = (bf16[2,128,1440]{1,2,0:T(8,128)(2,1)S(1)}, bf16[2,128,1440]{1,2,0:T(8,128)(2,1)S(1)}, u32[]{:S(2)}, u32[]{:S(2)}) collective-permute-start(bf16[2,128,1440]{1,2,0:T(8,128)(2,1)S(1)} %get-tuple-element.177), channel_id=1, source_target_pairs={{0,8},{8,16},{16,24},{24,32},{32,40},{40,48},{48,56},{56,64},{64,7... | collective-permute-start | bytes 2211848 | tf_op jit(solution)/shard_map/ppermute | solution.py:22
  118.1 12.2 %convolution_bitcast_fusion = f32[128,128]{0,1:T(8,128)S(1)} fusion(bf16[2,128,1440]{1,2,0:T(8,128)(2,1)S(1)} %fusion.78, f32[6,128,1440]{1,2,0:T(8,128)S(1)} %bitcast.117, f32[2,128,1]{1,2,0:T(1,128)S(1)} %get-tuple-element.139, f32[2,128,1439]{1,2,0:T(8,128)} %get-tuple-element.105, f32[2,128,1439]{1,2,0:T(8,128)} %get-tuple-element.104, ...), kind=kOutput, calls=%fused_computation.146 | convolution fusion | flops 120176640 | bytes 37687808 | tf_op jit(solution)/shard_map/rcf,rdf->cd/dot_general | solution.py:99
  130.4 3.5 %fusion.41 = (f32[128]{0:T(128)S(1)}, f32[128]{0:T(128)S(1)}, f32[128]{0:T(128)S(1)}, f32[128]{0:T(128)S(1)}, f32[128]{0:T(128)S(1)}, /*index=5*/f32[128]{0:T(12...) fusion(bf16[2,128,1440]{1,2,0:T(8,128)(2,1)S(1)} %get-tuple-element.177, f32[2,128,2]{1,2,0:T(2,128)S(1)} %get-tuple-element.129, ...), kind=kLoop, calls=%fused_computation.71 | loop fusion | flops 10320768 | bytes 14012928 | tf_op jit(solution)/shard_map/reduce_sum | solution.py:105
  136.5 1.8 fusion.40
  138.3 5.8 %collective-permute-start.2 = (f32[128,153]{0,1:T(8,128)S(1)}, f32[128,153]{0,1:T(8,128)S(1)}, u32[]{:S(2)}, u32[]{:S(2)}) collective-permute-start(f32[128,153]{0,1:T(8,128)S(1)} %concatenate.179), channel_id=1, source_target_pairs={{0,8},{1,9},{2,10},{3,11},{4,12},{5,13},{6,14},{7,15},{8,0},{9,1},... | collective-permute-start | bytes 235016 | tf_op jit(solution)/shard_map/ppermute | solution.py:33
  144.1 0.9 collective-permute-done.2
  145.1 2.3 %maximum_convert_fusion.1 = f32[6,128,1440]{1,2,0:T(8,128)} fusion(bf16[2,128,1440]{1,2,0:T(8,128)(2,1)S(1)} %collective-permute-done.4, bf16[2,128,1440]{1,2,0:T(8,128)(2,1)S(1)} %get-tuple-element.177, bf16[2,128,1440]{1,2,0:T(8,128)(2,1)S(1)} %collective-permute-done.3), kind=kLoop, calls=%fused_computation.45 | loop fusion | flops 3317760 | bytes 6635520 | tf_op jit(solution)/shard_map/convert_element_type | solution.py:107
  147.4 10.9 %fusion.96 = (f32[2,128,1439]{1,2,0:T(8,128)}, f32[2,128,1439]{1,2,0:T(8,128)}, f32[2,128,1439]{1,2,0:T(8,128)}, f32[2,128,1439]{1,2,0:T(8,128)}, f32[2,128,1439...) fusion(f32[6,128,1440]{1,2,0:T(8,128)} %maximum_convert_fusion.1), kind=kLoop, calls=%fused_computation.237 | loop fusion | bytes 29470720 | tf_op jit(solution)/shard_map/jit(_roll_static)/slice | solution.py:116
  158.3 10.7 %fusion.95 = (f32[2,128,1438]{1,2,0:T(8,128)}, f32[2,128,1438]{1,2,0:T(8,128)}, f32[2,128,1438]{1,2,0:T(8,128)}, f32[2,128,1438]{1,2,0:T(8,128)}, f32[2,128,1438...) fusion(f32[6,128,1440]{1,2,0:T(8,128)} %maximum_convert_fusion.1), kind=kLoop, calls=%fused_computation.236 | loop fusion | bytes 29450240 | tf_op jit(solution)/shard_map/jit(_roll_static)/slice | solution.py:116
  169.1 2.2 %copy-done.2 = f32[6,128,1440]{1,2,0:T(8,128)S(1)} copy-done((f32[6,128,1440]{1,2,0:T(8,128)S(1)}, f32[6,128,1440]{1,2,0:T(8,128)}, u32[]{:S(2)}) %copy-start.2) | copy-done | bytes 4423704
  171.3 2.2 %fusion.54 = f32[2,128,1440]{1,2,0:T(8,128)S(1)} fusion(f32[6,128,1440]{1,2,0:T(8,128)S(1)} %copy-done.2, f32[2,128,2]{1,2,0:T(2,128)S(1)} %get-tuple-element.123, f32[2,128,1438]{1,2,0:T(8,128)} %get-tuple-element.77, f32[2,128,1]{1,2,0:T(1,128)S(1)} %get-tuple-element.127, f32[2,128,1439]{1,2,0:T(8,128)} %get-tuple-element.87, ...), kind=kLoop, calls=%fused_computation.89 | loop fusion | flops 2580480 | bytes 5899776 | tf_op jit(solution)/shard_map/add | solution.py:116
  173.6 0.5 collective-permute-start.5
  174.9 0.6 fusion.60
  175.6 4.5 %collective-permute-done.5 = f32[128,153]{0,1:T(8,128)S(1)} collective-permute-done((f32[128,153]{0,1:T(8,128)S(1)}, f32[128,153]{0,1:T(8,128)S(1)}, u32[]{:S(2)}, u32[]{:S(2)}) %collective-permute-start.5) | collective-permute-done | bytes 78368 | tf_op jit(solution)/shard_map/ppermute | solution.py:33
  180.2 0.5 fusion.53
  180.7 4.3 %collective-permute-done.6 = f32[128,153]{0,1:T(8,128)S(1)} collective-permute-done((f32[128,153]{0,1:T(8,128)S(1)}, f32[128,153]{0,1:T(8,128)S(1)}, u32[]{:S(2)}, u32[]{:S(2)}) %collective-permute-start.6) | collective-permute-done | bytes 78368 | tf_op jit(solution)/shard_map/ppermute | solution.py:33
  185.2 0.5 fusion.50
  185.7 5.4 %collective-permute-done.7 = f32[128,153]{0,1:T(8,128)S(1)} collective-permute-done((f32[128,153]{0,1:T(8,128)S(1)}, f32[128,153]{0,1:T(8,128)S(1)}, u32[]{:S(2)}, u32[]{:S(2)}) %collective-permute-start.7) | collective-permute-done | bytes 78368 | tf_op jit(solution)/shard_map/ppermute | solution.py:33
  191.7 4.0 %collective-permute-done.8 = f32[128,153]{0,1:T(8,128)S(1)} collective-permute-done((f32[128,153]{0,1:T(8,128)S(1)}, f32[128,153]{0,1:T(8,128)S(1)}, u32[]{:S(2)}, u32[]{:S(2)}) %collective-permute-start.8) | collective-permute-done | bytes 78368 | tf_op jit(solution)/shard_map/ppermute | solution.py:33
  195.8 0.6 fusion.48
  196.4 3.8 %collective-permute-done.9 = f32[128,153]{0,1:T(8,128)S(1)} collective-permute-done((f32[128,153]{0,1:T(8,128)S(1)}, f32[128,153]{0,1:T(8,128)S(1)}, u32[]{:S(2)}, u32[]{:S(2)}) %collective-permute-start.9) | collective-permute-done | bytes 78368 | tf_op jit(solution)/shard_map/ppermute | solution.py:33
  200.3 1.5 fusion.44
  201.8 4.4 %collective-permute-done.10 = f32[128,153]{0,1:T(8,128)S(1)} collective-permute-done((f32[128,153]{0,1:T(8,128)S(1)}, f32[128,153]{0,1:T(8,128)S(1)}, u32[]{:S(2)}, u32[]{:S(2)}) %collective-permute-start.10) | collective-permute-done | bytes 78368 | tf_op jit(solution)/shard_map/ppermute | solution.py:33
  206.2 0.6 slice.747
  206.8 0.7 copy.30
  (123 shorter events, 6.5 us)
Async XLA Ops:
  0.6 110.0 %copy-start = (bf16[128,128]{1,0:T(8,128)(2,1)S(1)}, bf16[128,128]{1,0:T(8,128)(2,1)}, u32[]{:S(2)}) copy-start(bf16[128,128]{1,0:T(8,128)(2,1)} %param.15) | copy-start | bytes 98308
  0.6 46.0 %collective-permute-start = (bf16[2,128,1440]{1,2,0:T(8,128)(2,1)}, bf16[2,128,1440]{1,2,0:T(8,128)(2,1)S(1)}, u32[]{:S(2)}, u32[]{:S(2)}) collective-permute-start(bf16[2,128,1440]{1,2,0:T(8,128)(2,1)} %param.13), channel_id=1, source_target_pairs={{0,8},{8,16},{16,24},{24,32},{32,40},{40,48},{48,56},{56,64},{64,7... | collective-permute-start | bytes 2211848 | tf_op jit(solution)/shard_map/ppermute | solution.py:22
  2.6 44.1 %collective-permute-start.1 = (bf16[2,128,1440]{1,2,0:T(8,128)(2,1)}, bf16[2,128,1440]{1,2,0:T(8,128)(2,1)S(1)}, u32[]{:S(2)}, u32[]{:S(2)}) collective-permute-start(bf16[2,128,1440]{1,2,0:T(8,128)(2,1)} %param.13), channel_id=1, source_target_pairs={{8,0},{16,8},{24,16},{32,24},{40,32},{48,40},{56,48},{64,56},{72,6... | collective-permute-start | bytes 2211848 | tf_op jit(solution)/shard_map/ppermute | solution.py:23
  7.5 30.6 %all-to-all-start.1 = ((f32[8,1,32]{2,1,0:T(1,128)}), f32[8,1,32]{2,1,0:T(1,128)S(1)}, u32[]{:S(2)}, u32[]{:S(2)}) async-start(f32[8,1,32]{2,1,0:T(1,128)} %broadcast_in_dim.8), calls=%async_computation.1 | async-start | bytes 8192 | tf_op jit(solution)/shard_map/all_to_all | solution.py:66
  17.2 20.9 %copy-start.39 = (f32[128,25]{0,1:T(8,128)S(1)}, f32[128,25]{0,1:T(8,128)}, u32[]{:S(2)}) copy-start(f32[128,25]{0,1:T(8,128)} %param.14) | copy-start | bytes 38404
  38.1 8.6 %copy-start.3 = (bf16[2,128,1440]{1,2,0:T(8,128)(2,1)S(1)}, bf16[2,128,1440]{1,2,0:T(8,128)(2,1)}, u32[]{:S(2)}) copy-start(bf16[2,128,1440]{1,2,0:T(8,128)(2,1)} %param.13) | copy-start | bytes 2211844
  38.1 35.1 %all-to-all-start = ((bf16[48,32,768]{2,1,0:T(8,128)(2,1)}), bf16[48,32,768]{2,1,0:T(8,128)(2,1)}, u32[]{:S(2)}, u32[]{:S(2)}) async-start(bf16[48,32,768]{2,1,0:T(8,128)(2,1)} %param.9), calls=%async_computation | async-start | bytes 4718592 | tf_op jit(solution)/shard_map/all_to_all | solution.py:64
  81.1 23.9 %all-to-all-start.2 = ((bf16[6,128,512]{2,0,1:T(8,128)(2,1)}), bf16[6,128,512]{2,0,1:T(8,128)(2,1)S(1)}, u32[]{:S(2)}, u32[]{:S(2)}) async-start(bf16[6,128,512]{2,0,1:T(8,128)(2,1)} %copy.28), calls=%async_computation.2 | async-start | bytes 2097152 | tf_op jit(solution)/shard_map/all_to_all | solution.py:79
  99.2 11.4 %copy-start.38 = (f32[2,128,1438]{1,2,0:T(8,128)}, f32[2,128,1438]{1,2,0:T(8,128)S(1)}, u32[]{:S(2)}) copy-start(f32[2,128,1438]{1,2,0:T(8,128)S(1)} %get-tuple-element.88) | copy-start | bytes 4417540
  105.3 5.4 %slice-start = ((s8[4423680]{0:T(1024)(128)(4,1)}), s8[229376]{0:T(1024)(128)(4,1)S(1)}, s32[]{:S(2)}) async-start(s8[4423680]{0:T(1024)(128)(4,1)} %bitcast.116), calls=%async_computation.3 | async-start | bytes 458752
  105.6 5.1 %slice-start.1 = ((s8[4423680]{0:T(1024)(128)(4,1)}), s8[4194304]{0:T(1024)(128)(4,1)S(1)}, s32[]{:S(2)}) async-start(s8[4423680]{0:T(1024)(128)(4,1)} %bitcast.116), calls=%async_computation.4 | async-start | bytes 8388608
  111.9 6.2 %copy-start.7 = (f32[2,128,1439]{1,2,0:T(8,128)S(1)}, f32[2,128,1439]{1,2,0:T(8,128)}, u32[]{:S(2)}) copy-start(f32[2,128,1439]{1,2,0:T(8,128)} %get-tuple-element.98) | copy-start | bytes 4420612
  111.9 6.2 %copy-start.8 = (f32[2,128,1439]{1,2,0:T(8,128)S(1)}, f32[2,128,1439]{1,2,0:T(8,128)}, u32[]{:S(2)}) copy-start(f32[2,128,1439]{1,2,0:T(8,128)} %get-tuple-element.102) | copy-start | bytes 4420612
  111.9 6.2 %copy-start.9 = (f32[2,128,1439]{1,2,0:T(8,128)S(1)}, f32[2,128,1439]{1,2,0:T(8,128)}, u32[]{:S(2)}) copy-start(f32[2,128,1439]{1,2,0:T(8,128)} %get-tuple-element.103) | copy-start | bytes 4420612
  111.9 6.2 %copy-start.10 = (f32[2,128,1439]{1,2,0:T(8,128)S(1)}, f32[2,128,1439]{1,2,0:T(8,128)}, u32[]{:S(2)}) copy-start(f32[2,128,1439]{1,2,0:T(8,128)} %get-tuple-element.107) | copy-start | bytes 4420612
  111.9 6.2 %copy-start.14 = (f32[2,128,1438]{1,2,0:T(8,128)S(1)}, f32[2,128,1438]{1,2,0:T(8,128)}, u32[]{:S(2)}) copy-start(f32[2,128,1438]{1,2,0:T(8,128)} %get-tuple-element.89) | copy-start | bytes 4417540
  111.9 6.2 %copy-start.15 = (f32[2,128,1438]{1,2,0:T(8,128)S(1)}, f32[2,128,1438]{1,2,0:T(8,128)}, u32[]{:S(2)}) copy-start(f32[2,128,1438]{1,2,0:T(8,128)} %get-tuple-element.92) | copy-start | bytes 4417540
  113.4 31.6 %collective-permute-start.4 = (bf16[2,128,1440]{1,2,0:T(8,128)(2,1)S(1)}, bf16[2,128,1440]{1,2,0:T(8,128)(2,1)S(1)}, u32[]{:S(2)}, u32[]{:S(2)}) collective-permute-start(bf16[2,128,1440]{1,2,0:T(8,128)(2,1)S(1)} %get-tuple-element.177), channel_id=1, source_target_pairs={{8,0},{16,8},{24,16},{32,24},{40,32},{48,40},{56,48},{64,56},{72,6... | collective-permute-start | bytes 2211848 | tf_op jit(solution)/shard_map/ppermute | solution.py:23
  115.8 29.3 %collective-permute-start.3 = (bf16[2,128,1440]{1,2,0:T(8,128)(2,1)S(1)}, bf16[2,128,1440]{1,2,0:T(8,128)(2,1)S(1)}, u32[]{:S(2)}, u32[]{:S(2)}) collective-permute-start(bf16[2,128,1440]{1,2,0:T(8,128)(2,1)S(1)} %get-tuple-element.177), channel_id=1, source_target_pairs={{0,8},{8,16},{16,24},{24,32},{32,40},{40,48},{48,56},{56,64},{64,7... | collective-permute-start | bytes 2211848 | tf_op jit(solution)/shard_map/ppermute | solution.py:22
  130.3 3.6 %copy-start.25 = (f32[2,128,1439]{1,2,0:T(8,128)S(1)}, f32[2,128,1439]{1,2,0:T(8,128)}, u32[]{:S(2)}) copy-start(f32[2,128,1439]{1,2,0:T(8,128)} %get-tuple-element.99) | copy-start | bytes 4420612
  130.3 4.0 %copy-start.28 = (f32[2,128,1439]{1,2,0:T(8,128)S(1)}, f32[2,128,1439]{1,2,0:T(8,128)}, u32[]{:S(2)}) copy-start(f32[2,128,1439]{1,2,0:T(8,128)} %get-tuple-element.105) | copy-start | bytes 4420612
  130.3 4.4 %copy-start.29 = (f32[2,128,1439]{1,2,0:T(8,128)S(1)}, f32[2,128,1439]{1,2,0:T(8,128)}, u32[]{:S(2)}) copy-start(f32[2,128,1439]{1,2,0:T(8,128)} %get-tuple-element.106) | copy-start | bytes 4420612
  130.3 4.9 %copy-start.30 = (f32[2,128,1438]{1,2,0:T(8,128)S(1)}, f32[2,128,1438]{1,2,0:T(8,128)}, u32[]{:S(2)}) copy-start(f32[2,128,1438]{1,2,0:T(8,128)} %get-tuple-element.90) | copy-start | bytes 4417540
  130.4 5.3 %copy-start.31 = (f32[2,128,1438]{1,2,0:T(8,128)S(1)}, f32[2,128,1438]{1,2,0:T(8,128)}, u32[]{:S(2)}) copy-start(f32[2,128,1438]{1,2,0:T(8,128)} %get-tuple-element.91) | copy-start | bytes 4417540
  130.4 5.7 %copy-start.32 = (f32[2,128,1438]{1,2,0:T(8,128)S(1)}, f32[2,128,1438]{1,2,0:T(8,128)}, u32[]{:S(2)}) copy-start(f32[2,128,1438]{1,2,0:T(8,128)} %get-tuple-element.93) | copy-start | bytes 4417540
  130.4 6.1 %copy-start.33 = (f32[2,128,1438]{1,2,0:T(8,128)S(1)}, f32[2,128,1438]{1,2,0:T(8,128)}, u32[]{:S(2)}) copy-start(f32[2,128,1438]{1,2,0:T(8,128)} %get-tuple-element.97) | copy-start | bytes 4417540
  138.3 6.7 %collective-permute-start.2 = (f32[128,153]{0,1:T(8,128)S(1)}, f32[128,153]{0,1:T(8,128)S(1)}, u32[]{:S(2)}, u32[]{:S(2)}) collective-permute-start(f32[128,153]{0,1:T(8,128)S(1)} %concatenate.179), channel_id=1, source_target_pairs={{0,8},{1,9},{2,10},{3,11},{4,12},{5,13},{6,14},{7,15},{8,0},{9,1},... | collective-permute-start | bytes 235016 | tf_op jit(solution)/shard_map/ppermute | solution.py:33
  173.6 6.5 %collective-permute-start.5 = (f32[128,153]{0,1:T(8,128)S(1)}, f32[128,153]{0,1:T(8,128)S(1)}, u32[]{:S(2)}, u32[]{:S(2)}) collective-permute-start(f32[128,153]{0,1:T(8,128)S(1)} %add.229), channel_id=1, source_target_pairs={{0,1},{1,0},{2,3},{3,2},{4,5},{5,4},{6,7},{7,6},{8,9},{9,8},{10,11... | collective-permute-start | bytes 235016 | tf_op jit(solution)/shard_map/ppermute | solution.py:33
  175.5 4.7 %copy-start.21 = (f32[2,128,1438]{1,2,0:T(8,128)S(1)}, f32[2,128,1438]{1,2,0:T(8,128)}, u32[]{:S(2)}) copy-start(f32[2,128,1438]{1,2,0:T(8,128)} %get-tuple-element.72) | copy-start | bytes 4417540
  175.6 4.7 %copy-start.20 = (f32[2,128,1439]{1,2,0:T(8,128)S(1)}, f32[2,128,1439]{1,2,0:T(8,128)}, u32[]{:S(2)}) copy-start(f32[2,128,1439]{1,2,0:T(8,128)} %get-tuple-element.82) | copy-start | bytes 4420612
  180.1 4.9 %collective-permute-start.6 = (f32[128,153]{0,1:T(8,128)S(1)}, f32[128,153]{0,1:T(8,128)S(1)}, u32[]{:S(2)}, u32[]{:S(2)}) collective-permute-start(f32[128,153]{0,1:T(8,128)S(1)} %add.232), channel_id=1, source_target_pairs={{0,2},{1,3},{2,0},{3,1},{4,6},{5,7},{6,4},{7,5},{8,10},{9,11},{10,... | collective-permute-start | bytes 235016 | tf_op jit(solution)/shard_map/ppermute | solution.py:33
  180.2 5.0 %copy-start.11 = (f32[2,128,1439]{1,2,0:T(8,128)S(1)}, f32[2,128,1439]{1,2,0:T(8,128)}, u32[]{:S(2)}) copy-start(f32[2,128,1439]{1,2,0:T(8,128)} %get-tuple-element.79) | copy-start | bytes 4420612
  180.2 5.0 %copy-start.12 = (f32[2,128,1439]{1,2,0:T(8,128)S(1)}, f32[2,128,1439]{1,2,0:T(8,128)}, u32[]{:S(2)}) copy-start(f32[2,128,1439]{1,2,0:T(8,128)} %get-tuple-element.81) | copy-start | bytes 4420612
  180.2 5.0 %copy-start.13 = (f32[2,128,1438]{1,2,0:T(8,128)S(1)}, f32[2,128,1438]{1,2,0:T(8,128)}, u32[]{:S(2)}) copy-start(f32[2,128,1438]{1,2,0:T(8,128)} %get-tuple-element.71) | copy-start | bytes 4417540
  185.1 6.0 %collective-permute-start.7 = (f32[128,153]{0,1:T(8,128)S(1)}, f32[128,153]{0,1:T(8,128)S(1)}, u32[]{:S(2)}, u32[]{:S(2)}) collective-permute-start(f32[128,153]{0,1:T(8,128)S(1)} %add.237), channel_id=1, source_target_pairs={{0,4},{1,5},{2,6},{3,7},{4,0},{5,1},{6,2},{7,3},{8,12},{9,13},{10,... | collective-permute-start | bytes 235016 | tf_op jit(solution)/shard_map/ppermute | solution.py:33
  185.2 6.0 %copy-start.34 = (f32[2,128,1439]{1,2,0:T(8,128)S(1)}, f32[2,128,1439]{1,2,0:T(8,128)}, u32[]{:S(2)}) copy-start(f32[2,128,1439]{1,2,0:T(8,128)} %get-tuple-element.80) | copy-start | bytes 4420612
  185.2 6.0 %copy-start.35 = (f32[2,128,1438]{1,2,0:T(8,128)S(1)}, f32[2,128,1438]{1,2,0:T(8,128)}, u32[]{:S(2)}) copy-start(f32[2,128,1438]{1,2,0:T(8,128)} %get-tuple-element.73) | copy-start | bytes 4417540
  185.2 6.0 %copy-start.36 = (f32[2,128,1438]{1,2,0:T(8,128)S(1)}, f32[2,128,1438]{1,2,0:T(8,128)}, u32[]{:S(2)}) copy-start(f32[2,128,1438]{1,2,0:T(8,128)} %get-tuple-element.76) | copy-start | bytes 4417540
  191.1 4.5 %collective-permute-start.8 = (f32[128,153]{0,1:T(8,128)S(1)}, f32[128,153]{0,1:T(8,128)S(1)}, u32[]{:S(2)}, u32[]{:S(2)}) collective-permute-start(f32[128,153]{0,1:T(8,128)S(1)} %add.241), channel_id=1, source_target_pairs={{0,16},{1,17},{2,18},{3,19},{4,20},{5,21},{6,22},{7,23},{8,24},{9,... | collective-permute-start | bytes 235016 | tf_op jit(solution)/shard_map/ppermute | solution.py:33
  191.2 4.5 %copy-start.4 = (f32[2,128,1439]{1,2,0:T(8,128)S(1)}, f32[2,128,1439]{1,2,0:T(8,128)}, u32[]{:S(2)}) copy-start(f32[2,128,1439]{1,2,0:T(8,128)} %get-tuple-element.86) | copy-start | bytes 4420612
  191.2 4.5 %copy-start.5 = (f32[2,128,1438]{1,2,0:T(8,128)S(1)}, f32[2,128,1438]{1,2,0:T(8,128)}, u32[]{:S(2)}) copy-start(f32[2,128,1438]{1,2,0:T(8,128)} %get-tuple-element.69) | copy-start | bytes 4417540
  191.2 4.5 %copy-start.6 = (f32[2,128,1438]{1,2,0:T(8,128)S(1)}, f32[2,128,1438]{1,2,0:T(8,128)}, u32[]{:S(2)}) copy-start(f32[2,128,1438]{1,2,0:T(8,128)} %get-tuple-element.70) | copy-start | bytes 4417540
  195.6 4.5 %collective-permute-start.9 = (f32[128,153]{0,1:T(8,128)S(1)}, f32[128,153]{0,1:T(8,128)S(1)}, u32[]{:S(2)}, u32[]{:S(2)}) collective-permute-start(f32[128,153]{0,1:T(8,128)S(1)} %add.246), channel_id=1, source_target_pairs={{0,32},{1,33},{2,34},{3,35},{4,36},{5,37},{6,38},{7,39},{8,40},{9,... | collective-permute-start | bytes 235016 | tf_op jit(solution)/shard_map/ppermute | solution.py:33
  195.8 4.5 %copy-start.22 = (f32[2,128,1439]{1,2,0:T(8,128)S(1)}, f32[2,128,1439]{1,2,0:T(8,128)}, u32[]{:S(2)}) copy-start(f32[2,128,1439]{1,2,0:T(8,128)} %get-tuple-element.78) | copy-start | bytes 4420612
  195.8 4.5 %copy-start.23 = (f32[2,128,1439]{1,2,0:T(8,128)S(1)}, f32[2,128,1439]{1,2,0:T(8,128)}, u32[]{:S(2)}) copy-start(f32[2,128,1439]{1,2,0:T(8,128)} %get-tuple-element.83) | copy-start | bytes 4420612
  195.8 4.5 %copy-start.24 = (f32[2,128,1438]{1,2,0:T(8,128)S(1)}, f32[2,128,1438]{1,2,0:T(8,128)}, u32[]{:S(2)}) copy-start(f32[2,128,1438]{1,2,0:T(8,128)} %get-tuple-element.68) | copy-start | bytes 4417540
  200.2 6.0 %collective-permute-start.10 = (f32[128,153]{0,1:T(8,128)S(1)}, f32[128,153]{0,1:T(8,128)S(1)}, u32[]{:S(2)}, u32[]{:S(2)}) collective-permute-start(f32[128,153]{0,1:T(8,128)S(1)} %add.250), channel_id=1, source_target_pairs={{0,64},{1,65},{2,66},{3,67},{4,68},{5,69},{6,70},{7,71},{8,72},{9,... | collective-permute-start | bytes 235016 | tf_op jit(solution)/shard_map/ppermute | solution.py:33
  200.3 7.3 %copy-start.1 = (bf16[128,128]{1,0:T(8,128)(2,1)S(1)}, bf16[128,128]{1,0:T(8,128)(2,1)}, u32[]{:S(2)}) copy-start(bf16[128,128]{1,0:T(8,128)(2,1)} %param.15) | copy-start | bytes 98308
  (8 other events, 23.1 us)

commit v4 on v3

--- a/solution.py
+++ b/solution.py
@@ -39,6 +39,10 @@
     return value, carry
 
 
+def wrap_longitudes(field, width):
+    return jnp.concatenate([field[:, -width:], field, field[:, :width]], axis=1)
+
+
 def make_table(orders, length):
     lon_ids = jnp.arange(length, dtype=jnp.int32)
     residue = orders[:, None] * lon_ids[None, :] % length
@@ -59,7 +63,8 @@
     row_count, channels, longitudes = conv_input.shape
     lat_index = lax.axis_index("lat")
 
-    x_wide = with_rims(conv_input).astype(jnp.float32)
+    x_rows = with_rims(conv_input.transpose(0, 2, 1))
+    x_pad = wrap_longitudes(x_rows, 2).astype(jnp.float32)
 
     leg_rows = lax.all_to_all(legendre, "lat", 0, 1, tiled=True)
     spread = jnp.broadcast_to(quad_weight[None], (n_lat,) + quad_weight.shape)
@@ -80,31 +85,33 @@
     own_rows = own_rows.reshape(-1, row_count * doubled)
 
     table = make_table(slot_order, longitudes)
-    both = jnp.einsum("sn,sq->nq", own_rows, table, preferred_element_type=jnp.float32)
-    both = both.reshape(row_count, 2, channels, 2 * longitudes)
-    grad_grid = both[:, 0, :, :longitudes] + both[:, 1, :, longitudes:]
-    grad_grid = grad_grid.reshape(row_count, channels, longitudes).astype(jnp.bfloat16)
+    per_row = own_rows.reshape(-1, row_count, doubled)
+    grid_rows = []
+    for row in range(row_count):
+        both = jnp.einsum("sq,sn->qn", table, per_row[:, row], preferred_element_type=jnp.float32)
+        grid_rows.append(both[:longitudes, :channels] + both[longitudes:, channels:])
+    grad_grid = jnp.stack(grid_rows).astype(jnp.bfloat16)
 
-    hidden = jnp.zeros((row_count, channels, longitudes), jnp.float32)
+    hidden = jnp.zeros((row_count, longitudes, channels), jnp.float32)
     for tap_row in range(5):
         for tap_col in range(5):
-            weight_tap = depth_kernel[:, 5 * tap_row + tap_col][None, :, None]
-            hidden = hidden + weight_tap * jnp.roll(
-                x_wide[tap_row : tap_row + row_count], 2 - tap_col, axis=2
-            )
+            weight_tap = depth_kernel[:, 5 * tap_row + tap_col]
+            hidden = hidden + weight_tap * x_pad[
+                tap_row : tap_row + row_count, tap_col : tap_col + longitudes
+            ]
     hidden = hidden.astype(jnp.bfloat16)
     grad_hidden = jnp.einsum(
-        "cd,rdf->rcf", point_weight, grad_grid, preferred_element_type=jnp.float32
+        "rqd,cd->rqc", grad_grid, point_weight, preferred_element_type=jnp.float32
     ).astype(jnp.bfloat16)
-    point_part = jnp.einsum("rcf,rdf->cd", hidden, grad_grid, preferred_element_type=jnp.float32)
+    point_part = jnp.einsum("rqc,rqd->cd", hidden, grad_grid, preferred_element_type=jnp.float32)
     hidden_wide = grad_hidden.astype(jnp.float32)
     depth_terms = []
     for tap_row in range(5):
         for tap_col in range(5):
-            shifted_x = jnp.roll(x_wide[tap_row : tap_row + row_count], 2 - tap_col, axis=2)
-            depth_terms.append(jnp.sum(hidden_wide * shifted_x, axis=(0, 2)))
+            shifted_x = x_pad[tap_row : tap_row + row_count, tap_col : tap_col + longitudes]
+            depth_terms.append(jnp.sum(hidden_wide * shifted_x, axis=(0, 1)))
     depth_part = jnp.stack(depth_terms, axis=1)
-    padded_grad = with_rims(grad_hidden).astype(jnp.float32)
+    grad_pad = wrap_longitudes(with_rims(grad_hidden), 2).astype(jnp.float32)
     taps = [(tap_row, tap_col) for tap_row in range(5) for tap_col in range(5)]
     rounds = (n_ord * n_lat).bit_length() - 1
     groups = [taps[i * len(taps) // rounds : (i + 1) * len(taps) // rounds] for i in range(rounds)]
@@ -112,24 +119,25 @@
     def tap_group(group):
         def step(grad_input):
             for tap_row, tap_col in group:
-                weight_tap = depth_kernel[:, 5 * tap_row + tap_col][None, :, None]
-                grad_input = grad_input + weight_tap * jnp.roll(
-                    padded_grad[4 - tap_row : 4 - tap_row + row_count], tap_col - 2, axis=2
-                )
+                weight_tap = depth_kernel[:, 5 * tap_row + tap_col]
+                grad_input = grad_input + weight_tap * grad_pad[
+                    4 - tap_row : 4 - tap_row + row_count, 4 - tap_col : 4 - tap_col + longitudes
+                ]
             return grad_input
 
         return step
 
-    grad_input = jnp.zeros((row_count, channels, longitudes), jnp.float32)
+    grad_input = jnp.zeros((row_count, longitudes, channels), jnp.float32)
     sums, grad_input = butterfly_sum(
         jnp.concatenate([point_part, depth_part], axis=1),
         grad_input,
         [tap_group(group) for group in groups],
     )
+    grad_input = grad_input.astype(jnp.bfloat16).transpose(0, 2, 1)
     total_rows = row_count * n_ord * n_lat
     grad_scale = 1.0 / math.sqrt(total_rows * longitudes)
     sums = sums * grad_scale
-    return (grad_input.astype(jnp.bfloat16), sums[:, :channels], sums[:, channels:])
+    return (grad_input, sums[:, :channels], sums[:, channels:])
 
 
 def solution(mesh):

time: 208 us -> 174 us (0.84)
  the two profiles are of different devices: /device:TPU:30 before, /device:TPU:24 now
where the time goes in v4:
time: 174 us; the launch traced here: 173 us
  starting transfers between devices  43.5 us (25%)
  other arithmetic  36.4 us (21%)
  local copies, waits for them, and re-layouts  32.9 us (19%)
  waiting for transfers between devices  28.8 us (17%)
  matrix products  17.9 us (10%)
  blocking collectives  12.8 us (7%)
    another operation x1, other arithmetic  22.5 us
    ppermute x7, waiting for transfers between devices, butterfly_sum(): received = lax.ppermute(value, MESH_AXES, pairs)  22.2 us
    concatenate x2, local copies, waits for them, and re-layouts, wrap_longitudes(): return jnp.concatenate([field[:, -width:], field, field[:, :width]], axis=1)  21.3 us
    all_to_all x1, starting transfers between devices, layer(): own_rows = lax.all_to_all(by_device, MESH_AXES, 1, 0, tiled=True)  18.5 us
    all_to_all x1, blocking collectives, layer(): weights = lax.all_to_all(spread, 'lat', 0, 0, tiled=True).reshape(-1)  12.8 us
    ppermute x2, starting transfers between devices, with_rims(): lower = lax.ppermute(field[:width], MESH_AXES, up_pairs)  7.36 us
    ppermute x7, starting transfers between devices, butterfly_sum(): received = lax.ppermute(value, MESH_AXES, pairs)  7.05 us
    dot_general x2, matrix products, layer(): jnp.einsum('sq,sn->qn', table, per_row[:, row], preferred_element_type=jn...  6.65 us
  transfers between devices with their start and end apart: 13, of which 9 were waited for; matrix products, arithmetic and copies ran while one was open for 35% of the time, Pallas kernels for 0%

profile of v4, /device:TPU:24, one launch (start us, length us, event | category | flops | bytes accessed | tf_op | source)
XLA Modules:
  0.0 173.3 jit_solution(6006285585992249426)
XLA Ops:
  0.6 0.7 broadcast_in_dim.10
  1.3 12.8 %all_to_all.39 = f32[8,1,32]{2,1,0:T(1,128)S(1)} all-to-all(f32[8,1,32]{2,1,0:T(1,128)S(1)} %broadcast_in_dim.10), channel_id=1, replica_groups=mesh['ord'=16,'lat'=8] {'lat'}, dimensions={0} | all-to-all | bytes 2048 | tf_op jit(solution)/shard_map/all_to_all | solution.py:71
  14.1 6.6 %all-to-all-start = ((bf16[48,32,768]{2,1,0:T(8,128)(2,1)}), bf16[48,32,768]{2,1,0:T(8,128)(2,1)S(1)}, u32[]{:S(2)}, u32[]{:S(2)}) async-start(bf16[48,32,768]{2,1,0:T(8,128)(2,1)} %param.9), calls=%async_computation | async-start | bytes 4718592 | tf_op jit(solution)/shard_map/all_to_all | solution.py:69
  20.7 1.9 %collective-permute-start = (bf16[2,1440,128]{2,1,0:T(8,128)(2,1)S(1)}, bf16[2,1440,128]{2,1,0:T(8,128)(2,1)}, u32[]{:S(2)}, u32[]{:S(2)}) collective-permute-start(bf16[2,1440,128]{2,1,0:T(8,128)(2,1)S(1)} %bitcast.123), channel_id=1, source_target_pairs={{0,8},{8,16},{16,24},{24,32},{32,40},{40,48},{48,56},{56,64},{64,7... | collective-permute-start | bytes 2211848 | tf_op jit(solution)/shard_map/ppermute | solution.py:22
  22.6 3.6 %collective-permute-start.1 = (bf16[2,1440,128]{2,1,0:T(8,128)(2,1)S(1)}, bf16[2,1440,128]{2,1,0:T(8,128)(2,1)}, u32[]{:S(2)}, u32[]{:S(2)}) collective-permute-start(bf16[2,1440,128]{2,1,0:T(8,128)(2,1)S(1)} %bitcast.124), channel_id=1, source_target_pairs={{8,0},{16,8},{24,16},{32,24},{40,32},{48,40},{56,48},{64,56},{72,6... | collective-permute-start | bytes 2211848 | tf_op jit(solution)/shard_map/ppermute | solution.py:23
  26.5 22.5 %multiply_convert_fusion.1 = (bf16[768,1440]{1,0:T(8,128)(2,1)}, bf16[768,1440]{1,0:T(8,128)(2,1)}) fusion(s32[768]{0:T(1024)S(1)} %copy-done.6, f32[768]{0:T(1024)S(1)} %get-tuple-element.98, f32[768]{0:T(1024)S(1)} %get-tuple-element.99), kind=kLoop, calls=%fused_computation.29 | loop fusion | flops 14376960 | bytes 4432896 | tf_op jit(solution)/shard_map/convert.4
  49.0 0.5 broadcast.80
  49.5 0.7 reduce.3
  50.2 1.6 copy.18
  51.8 4.4 %fusion.68 = bf16[6,256,256]{1,2,0:T(8,128)(2,1)S(1)} fusion(bf16[6,256,768]{2,1,0:T(8,128)(2,1)} %bitcast.122, bf16[6,768,256]{2,1,0:T(8,128)(2,1)} %param.8, bf16[6,768]{1,0:T(8,128)(2,1)S(1)} %fusion.89, f32[256]{0:T(256)S(1)} %mul.645, s32[256]{0:T(256)S(1)} %fusion.95), kind=kOutput, calls=%fused_computation.120 | convolution fusion | flops 1211170816 | bytes 5516288 | tf_op jit(solution)/shard_map/slj,sjk->slk/dot_general | solution.py:80
  57.2 1.4 copy.22
  58.6 18.5 %all-to-all-start.2 = ((bf16[6,128,512]{2,0,1:T(8,128)(2,1)}), bf16[6,128,512]{2,0,1:T(8,128)(2,1)S(1)}, u32[]{:S(2)}, u32[]{:S(2)}) async-start(bf16[6,128,512]{2,0,1:T(8,128)(2,1)} %copy.22), calls=%async_computation.2 | async-start | bytes 2097152 | tf_op jit(solution)/shard_map/all_to_all | solution.py:84
  77.2 1.6 pad_maximum_fusion.3
  78.8 1.4 copy-done.2
  80.1 10.6 %concatenate.20 = bf16[6,1444,128]{2,1,0:T(8,128)(2,1)S(1)} concatenate(bf16[6,2,128]{2,1,0:T(2,128)(2,1)S(1)} %get-tuple-element.68, bf16[6,1440,128]{2,1,0:T(8,128)(2,1)} %copy-done.2, bf16[6,2,128]{2,1,0:T(2,128)(2,1)S(1)} %get-tuple-element.67), dimensions={1} | concatenate | bytes 4435968 | tf_op jit(solution)/shard_map/concatenate | solution.py:43
  90.8 2.3 %convert_element_type.41 = f32[6,1444,128]{2,1,0:T(8,128)} convert(bf16[6,1444,128]{2,1,0:T(8,128)(2,1)S(1)} %concatenate.20) | non-fusion elementwise | flops 1108992 | bytes 6653952 | tf_op jit(solution)/shard_map/convert_element_type | solution.py:67
  93.1 1.7 all-to-all-done.2
  95.3 1.1 fusion.103
  96.3 0.6 copy-done.3
  96.9 4.2 %fusion.5 = f32[2880,256]{1,0:T(8,128)S(1)} fusion(bf16[768,1440]{1,0:T(8,128)(2,1)} %get-tuple-element.97, bf16[768,1440]{1,0:T(8,128)(2,1)S(1)} %copy-done.3, bf16[768,1,256]{2,1,0:T(2,128)(2,1)S(1)} %get-tuple-element.70), kind=kOutput, calls=%fused_computation.35 | convolution fusion | flops 1141309440 | bytes 7766016 | tf_op jit(solution)/shard_map/sq,sn->qn/dot_general | solution.py:91
  101.2 2.4 %fusion.6 = f32[2880,256]{1,0:T(8,128)S(1)} fusion(bf16[768,1440]{1,0:T(8,128)(2,1)S(1)} %copy-done.4, bf16[768,1440]{1,0:T(8,128)(2,1)S(1)} %copy-done.3, bf16[768,1,256]{2,1,0:T(2,128)(2,1)S(1)} %get-tuple-element.69), kind=kOutput, calls=%fused_computation.36 | convolution fusion | flops 1141309440 | bytes 7766016 | tf_op jit(solution)/shard_map/sq,sn->qn/dot_general | solution.py:91
  103.8 1.5 fusion.38
  105.3 2.1 %collective-permute-start.3 = (bf16[2,1440,128]{2,1,0:T(8,128)(2,1)S(1)}, bf16[2,1440,128]{2,1,0:T(8,128)(2,1)S(1)}, u32[]{:S(2)}, u32[]{:S(2)}) collective-permute-start(bf16[2,1440,128]{2,1,0:T(8,128)(2,1)S(1)} %get-tuple-element.100), channel_id=1, source_target_pairs={{0,8},{8,16},{16,24},{24,32},{32,40},{40,48},{48,56},{56,64},{64,7... | collective-permute-start | bytes 2211848 | tf_op jit(solution)/shard_map/ppermute | solution.py:22
  107.4 3.7 %collective-permute-start.4 = (bf16[2,1440,128]{2,1,0:T(8,128)(2,1)S(1)}, bf16[2,1440,128]{2,1,0:T(8,128)(2,1)S(1)}, u32[]{:S(2)}, u32[]{:S(2)}) collective-permute-start(bf16[2,1440,128]{2,1,0:T(8,128)(2,1)S(1)} %get-tuple-element.100), channel_id=1, source_target_pairs={{8,0},{16,8},{24,16},{32,24},{40,32},{48,40},{56,48},{64,56},{72,6... | collective-permute-start | bytes 2211848 | tf_op jit(solution)/shard_map/ppermute | solution.py:23
  111.1 5.3 %convolution_bitcast_fusion = f32[128,128]{0,1:T(8,128)S(1)} fusion(f32[6,1444,128]{2,1,0:T(8,128)S(1)} %bitcast.117, f32[128]{0:T(128)S(1)} %get-tuple-element.94, f32[128]{0:T(128)S(1)} %get-tuple-element.95, f32[128]{0:T(128)S(1)} %get-tuple-element.72, f32[128]{0:T(128)S(1)} %get-tuple-element.73, f32[128]{0:T(128)S(1)} %get-tuple-element.74, ...), kind=kOutput, calls=%fused_computation.122 | convolution fusion | flops 113172480 | bytes 37679616 | tf_op jit(solution)/shard_map/rqc,rqd->cd/dot_general | solution.py:106
  116.4 3.3 %fusion.39 = (f32[128]{0:T(128)S(1)}, f32[128]{0:T(128)S(1)}, f32[128]{0:T(128)S(1)}, f32[128]{0:T(128)S(1)}, f32[128]{0:T(128)S(1)}, /*index=5*/f32[128]{0:T(12...) fusion(bf16[2,1440,128]{2,1,0:T(8,128)(2,1)S(1)} %get-tuple-ele, ...), kind=kLoop, calls=%fused_computation.69 | loop fusion | flops 13637376 | bytes 27288576 | tf_op jit(solution)/shard_map/reduce_sum | solution.py:112
  119.9 1.3 collective-permute-done.2
  121.2 4.8 %collective-permute-done.3 = bf16[2,1440,128]{2,1,0:T(8,128)(2,1)S(1)} collective-permute-done((bf16[2,1440,128]{2,1,0:T(8,128)(2,1)S(1)}, bf16[2,1440,128]{2,1,0:T(8,128)(2,1)S(1)}, u32[]{:S(2)}, u32[]{:S(2)}) %collective-permute-start.3) | collective-permute-done | bytes 737312 | tf_op jit(solution)/shard_map/ppermute | solution.py:22
  126.3 1.4 copy-done.1
  127.6 10.6 %concatenate.24 = bf16[6,1444,128]{2,1,0:T(8,128)(2,1)S(1)} concatenate(bf16[6,2,128]{2,1,0:T(2,128)(2,1)S(1)} %get-tuple-element.66, bf16[6,1440,128]{2,1,0:T(8,128)(2,1)} %copy-done.1, bf16[6,2,128]{2,1,0:T(2,128)(2,1)S(1)} %get-tuple-element.65), dimensions={1} | concatenate | bytes 4435968 | tf_op jit(solution)/shard_map/concatenate | solution.py:43
  138.6 0.5 fusion.62
  139.1 1.6 collective-permute-start.5
  140.7 0.7 fusion.58
  141.5 3.7 %collective-permute-done.5 = f32[128,153]{0,1:T(8,128)S(1)} collective-permute-done((f32[128,153]{0,1:T(8,128)S(1)}, f32[128,153]{0,1:T(8,128)S(1)}, u32[]{:S(2)}, u32[]{:S(2)}) %collective-permute-start.5) | collective-permute-done | bytes 78368 | tf_op jit(solution)/shard_map/ppermute | solution.py:33
  145.1 0.9 collective-permute-start.6
  146.5 3.1 %collective-permute-done.6 = f32[128,153]{0,1:T(8,128)S(1)} collective-permute-done((f32[128,153]{0,1:T(8,128)S(1)}, f32[128,153]{0,1:T(8,128)S(1)}, u32[]{:S(2)}, u32[]{:S(2)}) %collective-permute-start.6) | collective-permute-done | bytes 78368 | tf_op jit(solution)/shard_map/ppermute | solution.py:33
  149.7 1.9 %collective-permute-start.7 = (f32[128,153]{0,1:T(8,128)S(1)}, f32[128,153]{0,1:T(8,128)S(1)}, u32[]{:S(2)}, u32[]{:S(2)}) collective-permute-start(f32[128,153]{0,1:T(8,128)S(1)} %add.240), channel_id=1, source_target_pairs={{0,4},{1,5},{2,6},{3,7},{4,0},{5,1},{6,2},{7,3},{8,12},{9,13},{10,... | collective-permute-start | bytes 235016 | tf_op jit(solution)/shard_map/ppermute | solution.py:33
  151.6 0.8 fusion.51
  152.3 3.4 %collective-permute-done.7 = f32[128,153]{0,1:T(8,128)S(1)} collective-permute-done((f32[128,153]{0,1:T(8,128)S(1)}, f32[128,153]{0,1:T(8,128)S(1)}, u32[]{:S(2)}, u32[]{:S(2)}) %collective-permute-start.7) | collective-permute-done | bytes 78368 | tf_op jit(solution)/shard_map/ppermute | solution.py:33
  156.6 3.9 %collective-permute-done.8 = f32[128,153]{0,1:T(8,128)S(1)} collective-permute-done((f32[128,153]{0,1:T(8,128)S(1)}, f32[128,153]{0,1:T(8,128)S(1)}, u32[]{:S(2)}, u32[]{:S(2)}) %collective-permute-start.8) | collective-permute-done | bytes 78368 | tf_op jit(solution)/shard_map/ppermute | solution.py:33
  160.5 0.9 collective-permute-start.9
  161.4 0.7 fusion.44
  162.1 3.8 %collective-permute-done.9 = f32[128,153]{0,1:T(8,128)S(1)} collective-permute-done((f32[128,153]{0,1:T(8,128)S(1)}, f32[128,153]{0,1:T(8,128)S(1)}, u32[]{:S(2)}, u32[]{:S(2)}) %collective-permute-start.9) | collective-permute-done | bytes 78368 | tf_op jit(solution)/shard_map/ppermute | solution.py:33
  165.9 1.3 collective-permute-start.10
  167.2 1.6 fusion.40
  168.8 3.1 %collective-permute-done.10 = f32[128,153]{0,1:T(8,128)S(1)} collective-permute-done((f32[128,153]{0,1:T(8,128)S(1)}, f32[128,153]{0,1:T(8,128)S(1)}, u32[]{:S(2)}, u32[]{:S(2)}) %collective-permute-start.10) | collective-permute-done | bytes 78368 | tf_op jit(solution)/shard_map/ppermute | solution.py:33
  172.0 0.6 slice.459
  172.6 0.7 copy.23
  (54 shorter events, 4.0 us)
Async XLA Ops:
  0.6 103.1 %copy-start = (bf16[128,128]{1,0:T(8,128)(2,1)S(1)}, bf16[128,128]{1,0:T(8,128)(2,1)}, u32[]{:S(2)}) copy-start(bf16[128,128]{1,0:T(8,128)(2,1)} %param.15) | copy-start | bytes 98308
  14.1 6.6 %copy-start.5 = (bf16[2,128,1440]{1,2,0:T(8,128)(2,1)S(1)}, bf16[2,128,1440]{1,2,0:T(8,128)(2,1)}, u32[]{:S(2)}) copy-start(bf16[2,128,1440]{1,2,0:T(8,128)(2,1)} %param.13) | copy-start | bytes 2211844
  14.1 12.2 %copy-start.8 = (s32[48]{0:T(128)S(1)}, s32[48]{0:T(128)}, u32[]{:S(2)}) copy-start(s32[48]{0:T(128)} %param.12) | copy-start | bytes 580
  14.1 12.3 %copy-start.6 = (s32[768]{0:T(1024)S(1)}, s32[768]{0:T(1024)}, u32[]{:S(2)}) copy-start(s32[768]{0:T(1024)} %param.11) | copy-start | bytes 9220
  14.1 36.1 %all-to-all-start = ((bf16[48,32,768]{2,1,0:T(8,128)(2,1)}), bf16[48,32,768]{2,1,0:T(8,128)(2,1)S(1)}, u32[]{:S(2)}, u32[]{:S(2)}) async-start(bf16[48,32,768]{2,1,0:T(8,128)(2,1)} %param.9), calls=%async_computation | async-start | bytes 4718592 | tf_op jit(solution)/shard_map/all_to_all | solution.py:69
  20.7 56.4 %collective-permute-start = (bf16[2,1440,128]{2,1,0:T(8,128)(2,1)S(1)}, bf16[2,1440,128]{2,1,0:T(8,128)(2,1)}, u32[]{:S(2)}, u32[]{:S(2)}) collective-permute-start(bf16[2,1440,128]{2,1,0:T(8,128)(2,1)S(1)} %bitcast.123), channel_id=1, source_target_pairs={{0,8},{8,16},{16,24},{24,32},{32,40},{40,48},{48,56},{56,64},{64,7... | collective-permute-start | bytes 2211848 | tf_op jit(solution)/shard_map/ppermute | solution.py:22
  22.6 54.5 %collective-permute-start.1 = (bf16[2,1440,128]{2,1,0:T(8,128)(2,1)S(1)}, bf16[2,1440,128]{2,1,0:T(8,128)(2,1)}, u32[]{:S(2)}, u32[]{:S(2)}) collective-permute-start(bf16[2,1440,128]{2,1,0:T(8,128)(2,1)S(1)} %bitcast.124), channel_id=1, source_target_pairs={{8,0},{16,8},{24,16},{32,24},{40,32},{48,40},{56,48},{64,56},{72,6... | collective-permute-start | bytes 2211848 | tf_op jit(solution)/shard_map/ppermute | solution.py:23
  58.6 18.5 %copy-start.7 = (f32[128,25]{0,1:T(8,128)S(1)}, f32[128,25]{0,1:T(8,128)}, u32[]{:S(2)}) copy-start(f32[128,25]{0,1:T(8,128)} %param.14) | copy-start | bytes 38404
  58.6 36.2 %all-to-all-start.2 = ((bf16[6,128,512]{2,0,1:T(8,128)(2,1)}), bf16[6,128,512]{2,0,1:T(8,128)(2,1)S(1)}, u32[]{:S(2)}, u32[]{:S(2)}) async-start(bf16[6,128,512]{2,0,1:T(8,128)(2,1)} %copy.22), calls=%async_computation.2 | async-start | bytes 2097152 | tf_op jit(solution)/shard_map/all_to_all | solution.py:84
  78.8 1.4 copy-start.2
  95.2 1.7 copy-start.3
  96.9 4.2 %copy-start.4 = (bf16[768,1440]{1,0:T(8,128)(2,1)S(1)}, bf16[768,1440]{1,0:T(8,128)(2,1)}, u32[]{:S(2)}) copy-start(bf16[768,1440]{1,0:T(8,128)(2,1)} %get-tuple-element.97) | copy-start | bytes 6635524
  96.9 6.8 %slice-start = ((s8[4448256]{0:T(1024)(128)(4,1)}), s8[4194304]{0:T(1024)(128)(4,1)S(1)}, s32[]{:S(2)}) async-start(s8[4448256]{0:T(1024)(128)(4,1)} %bitcast.116), calls=%async_computation.3 | async-start | bytes 8388608
  101.2 2.6 %slice-start.1 = ((s8[4448256]{0:T(1024)(128)(4,1)}), s8[253952]{0:T(1024)(128)(4,1)S(1)}, s32[]{:S(2)}) async-start(s8[4448256]{0:T(1024)(128)(4,1)} %bitcast.116), calls=%async_computation.4 | async-start | bytes 507904
  105.3 20.7 %collective-permute-start.3 = (bf16[2,1440,128]{2,1,0:T(8,128)(2,1)S(1)}, bf16[2,1440,128]{2,1,0:T(8,128)(2,1)S(1)}, u32[]{:S(2)}, u32[]{:S(2)}) collective-permute-start(bf16[2,1440,128]{2,1,0:T(8,128)(2,1)S(1)} %get-tuple-element.100), channel_id=1, source_target_pairs={{0,8},{8,16},{16,24},{24,32},{32,40},{40,48},{48,56},{56,64},{64,7... | collective-permute-start | bytes 2211848 | tf_op jit(solution)/shard_map/ppermute | solution.py:22
  107.4 18.6 %collective-permute-start.4 = (bf16[2,1440,128]{2,1,0:T(8,128)(2,1)S(1)}, bf16[2,1440,128]{2,1,0:T(8,128)(2,1)S(1)}, u32[]{:S(2)}, u32[]{:S(2)}) collective-permute-start(bf16[2,1440,128]{2,1,0:T(8,128)(2,1)S(1)} %get-tuple-element.100), channel_id=1, source_target_pairs={{8,0},{16,8},{24,16},{32,24},{40,32},{48,40},{56,48},{64,56},{72,6... | collective-permute-start | bytes 2211848 | tf_op jit(solution)/shard_map/ppermute | solution.py:23
  119.8 1.3 collective-permute-start.2
  126.3 1.4 copy-start.1
  139.1 6.0 %collective-permute-start.5 = (f32[128,153]{0,1:T(8,128)S(1)}, f32[128,153]{0,1:T(8,128)S(1)}, u32[]{:S(2)}, u32[]{:S(2)}) collective-permute-start(f32[128,153]{0,1:T(8,128)S(1)} %add.232), channel_id=1, source_target_pairs={{0,1},{1,0},{2,3},{3,2},{4,5},{5,4},{6,7},{7,6},{8,9},{9,8},{10,11... | collective-permute-start | bytes 235016 | tf_op jit(solution)/shard_map/ppermute | solution.py:33
  145.1 4.5 %collective-permute-start.6 = (f32[128,153]{0,1:T(8,128)S(1)}, f32[128,153]{0,1:T(8,128)S(1)}, u32[]{:S(2)}, u32[]{:S(2)}) collective-permute-start(f32[128,153]{0,1:T(8,128)S(1)} %add.235), channel_id=1, source_target_pairs={{0,2},{1,3},{2,0},{3,1},{4,6},{5,7},{6,4},{7,5},{8,10},{9,11},{10,... | collective-permute-start | bytes 235016 | tf_op jit(solution)/shard_map/ppermute | solution.py:33
  149.7 6.0 %collective-permute-start.7 = (f32[128,153]{0,1:T(8,128)S(1)}, f32[128,153]{0,1:T(8,128)S(1)}, u32[]{:S(2)}, u32[]{:S(2)}) collective-permute-start(f32[128,153]{0,1:T(8,128)S(1)} %add.240), channel_id=1, source_target_pairs={{0,4},{1,5},{2,6},{3,7},{4,0},{5,1},{6,2},{7,3},{8,12},{9,13},{10,... | collective-permute-start | bytes 235016 | tf_op jit(solution)/shard_map/ppermute | solution.py:33
  155.7 4.8 %collective-permute-start.8 = (f32[128,153]{0,1:T(8,128)S(1)}, f32[128,153]{0,1:T(8,128)S(1)}, u32[]{:S(2)}, u32[]{:S(2)}) collective-permute-start(f32[128,153]{0,1:T(8,128)S(1)} %add.244), channel_id=1, source_target_pairs={{0,16},{1,17},{2,18},{3,19},{4,20},{5,21},{6,22},{7,23},{8,24},{9,... | collective-permute-start | bytes 235016 | tf_op jit(solution)/shard_map/ppermute | solution.py:33
  160.5 5.4 %collective-permute-start.9 = (f32[128,153]{0,1:T(8,128)S(1)}, f32[128,153]{0,1:T(8,128)S(1)}, u32[]{:S(2)}, u32[]{:S(2)}) collective-permute-start(f32[128,153]{0,1:T(8,128)S(1)} %add.249), channel_id=1, source_target_pairs={{0,32},{1,33},{2,34},{3,35},{4,36},{5,37},{6,38},{7,39},{8,40},{9,... | collective-permute-start | bytes 235016 | tf_op jit(solution)/shard_map/ppermute | solution.py:33
  165.9 6.0 %collective-permute-start.10 = (f32[128,153]{0,1:T(8,128)S(1)}, f32[128,153]{0,1:T(8,128)S(1)}, u32[]{:S(2)}, u32[]{:S(2)}) collective-permute-start(f32[128,153]{0,1:T(8,128)S(1)} %add.253), channel_id=1, source_target_pairs={{0,64},{1,65},{2,66},{3,67},{4,68},{5,69},{6,70},{7,71},{8,72},{9,... | collective-permute-start | bytes 235016 | tf_op jit(solution)/shard_map/ppermute | solution.py:33

commit v5 on v4

--- a/solution.py
+++ b/solution.py
@@ -7,6 +7,7 @@
 
 
 MESH_AXES = ("ord", "lat")
+WRAP = 8
 
 
 def device_of_block(k):
@@ -24,17 +25,39 @@
     return jnp.concatenate([upper, field, lower], axis=0)
 
 
+def group_sum(value, bits):
+    count = lax.axis_size("ord") * lax.axis_size("lat")
+    me = lax.axis_index("ord") * lax.axis_size("lat") + lax.axis_index("lat")
+    size = 1 << len(bits)
+
+    def mask_of(x):
+        return sum(((x >> i) & 1) << bit for i, bit in enumerate(bits))
+
+    held = [value]
+    for x in range(1, size):
+        mask = mask_of(x)
+        held.append(lax.ppermute(value, MESH_AXES, [(d, d ^ mask) for d in range(count)]))
+    held = jnp.stack(held)
+    position = sum(((me >> bit) & 1) << i for i, bit in enumerate(bits))
+    members = [lax.dynamic_index_in_dim(held, position ^ j, keepdims=False) for j in range(size)]
+    while len(members) > 1:
+        members = [members[i] + members[i + 1] for i in range(0, len(members), 2)]
+    return members[0]
+
+
 def butterfly_sum(value, carry, steps):
     count = lax.axis_size("ord") * lax.axis_size("lat")
-    bits = count.bit_length() - 1
-    order = sorted(range(bits), key=lambda b: (b != 3, b))
-    for round_index, bit in enumerate(order):
-        pairs = [(d, d ^ (1 << bit)) for d in range(count)]
-        received = lax.ppermute(value, MESH_AXES, pairs)
+    bits = list(range(count.bit_length() - 1))
+    preferred = [(3, 4), (1, 2), (5, 6), (0,)]
+    rounds = [tuple(b for b in group if b in bits) for group in preferred]
+    rounds = [group for group in rounds if group]
+    left = [b for b in bits if all(b not in group for group in rounds)]
+    rounds += [(b,) for b in left]
+    for round_index, group in enumerate(rounds):
         if round_index < len(steps):
             carry = steps[round_index](carry)
-        value, carry = lax.optimization_barrier((value + received, carry))
-    for step in steps[len(order):]:
+        value, carry = lax.optimization_barrier((group_sum(value, group), carry))
+    for step in steps[len(rounds):]:
         carry = step(carry)
     return value, carry
 
@@ -64,7 +87,7 @@
     lat_index = lax.axis_index("lat")
 
     x_rows = with_rims(conv_input.transpose(0, 2, 1))
-    x_pad = wrap_longitudes(x_rows, 2).astype(jnp.float32)
+    x_pad = wrap_longitudes(x_rows.astype(jnp.float32), WRAP)
 
     leg_rows = lax.all_to_all(legendre, "lat", 0, 1, tiled=True)
     spread = jnp.broadcast_to(quad_weight[None], (n_lat,) + quad_weight.shape)
@@ -96,8 +119,9 @@
     for tap_row in range(5):
         for tap_col in range(5):
             weight_tap = depth_kernel[:, 5 * tap_row + tap_col]
+            start = WRAP - 2 + tap_col
             hidden = hidden + weight_tap * x_pad[
-                tap_row : tap_row + row_count, tap_col : tap_col + longitudes
+                tap_row : tap_row + row_count, start : start + longitudes
             ]
     hidden = hidden.astype(jnp.bfloat16)
     grad_hidden = jnp.einsum(
@@ -108,20 +132,22 @@
     depth_terms = []
     for tap_row in range(5):
         for tap_col in range(5):
-            shifted_x = x_pad[tap_row : tap_row + row_count, tap_col : tap_col + longitudes]
+            start = WRAP - 2 + tap_col
+            shifted_x = x_pad[tap_row : tap_row + row_count, start : start + longitudes]
             depth_terms.append(jnp.sum(hidden_wide * shifted_x, axis=(0, 1)))
     depth_part = jnp.stack(depth_terms, axis=1)
-    grad_pad = wrap_longitudes(with_rims(grad_hidden), 2).astype(jnp.float32)
+    grad_pad = wrap_longitudes(with_rims(grad_hidden).astype(jnp.float32), WRAP)
     taps = [(tap_row, tap_col) for tap_row in range(5) for tap_col in range(5)]
-    rounds = (n_ord * n_lat).bit_length() - 1
+    rounds = 4
     groups = [taps[i * len(taps) // rounds : (i + 1) * len(taps) // rounds] for i in range(rounds)]
 
     def tap_group(group):
         def step(grad_input):
             for tap_row, tap_col in group:
                 weight_tap = depth_kernel[:, 5 * tap_row + tap_col]
+                start = WRAP + 2 - tap_col
                 grad_input = grad_input + weight_tap * grad_pad[
-                    4 - tap_row : 4 - tap_row + row_count, 4 - tap_col : 4 - tap_col + longitudes
+                    4 - tap_row : 4 - tap_row + row_count, start : start + longitudes
                 ]
             return grad_input
 

time: 174 us -> 161 us (0.925)
  the two profiles are of different devices: /device:TPU:24 before, /device:TPU:1 now
where the time goes in v5:
time: 161 us; the launch traced here: 160 us
  starting transfers between devices  41.4 us (26%)
  other arithmetic  37.1 us (23%)
  waiting for transfers between devices  36.1 us (22%)
  matrix products  18.1 us (11%)
  blocking collectives  14.8 us (9%)
  local copies, waits for them, and re-layouts  10.9 us (7%)
    another operation x1, other arithmetic  22.5 us
    all_to_all x1, waiting for transfers between devices, layer(): own_rows = lax.all_to_all(by_device, MESH_AXES, 1, 0, tiled=True)  15.8 us
    all_to_all x1, blocking collectives, layer(): weights = lax.all_to_all(spread, 'lat', 0, 0, tiled=True).reshape(-1)  14.8 us
    ppermute x10, starting transfers between devices, group_sum(): lax.ppermute(value, MESH_AXES, [(d, d ^ mask) for d in range(count)])  13.9 us
    ppermute x10, waiting for transfers between devices, group_sum(): lax.ppermute(value, MESH_AXES, [(d, d ^ mask) for d in range(count)])  13.4 us
    all_to_all x1, starting transfers between devices, layer(): own_rows = lax.all_to_all(by_device, MESH_AXES, 1, 0, tiled=True)  13 us
    all_to_all x1, waiting for transfers between devices, layer(): leg_rows = lax.all_to_all(legendre, 'lat', 0, 1, tiled=True)  6.9 us
    dot_general x2, matrix products, layer(): jnp.einsum('sq,sn->qn', table, per_row[:, row], preferred_element_type=jn...  6.57 us
  transfers between devices with their start and end apart: 16, of which 8 were waited for; matrix products, arithmetic and copies ran while one was open for 31% of the time, Pallas kernels for 0%

profile of v5, /device:TPU:1, one launch (start us, length us, event | category | flops | bytes accessed | tf_op | source)
XLA Modules:
  0.0 159.6 jit_solution(17481123135164350394)
XLA Ops:
  0.6 0.7 broadcast_in_dim.10
  1.3 14.8 %all_to_all.39 = f32[8,1,32]{2,1,0:T(1,128)S(1)} all-to-all(f32[8,1,32]{2,1,0:T(1,128)S(1)} %broadcast_in_dim.10), channel_id=1, replica_groups=mesh['ord'=16,'lat'=8] {'lat'}, dimensions={0} | all-to-all | bytes 2048 | tf_op jit(solution)/shard_map/all_to_all | solution.py:94
  16.1 3.8 %all-to-all-start = ((bf16[48,32,768]{2,1,0:T(8,128)(2,1)}), bf16[48,32,768]{2,1,0:T(8,128)(2,1)S(1)}, u32[]{:S(2)}, u32[]{:S(2)}) async-start(bf16[48,32,768]{2,1,0:T(8,128)(2,1)} %param.9), calls=%async_computation | async-start | bytes 4718592 | tf_op jit(solution)/shard_map/all_to_all | solution.py:92
  19.9 4.3 %collective-permute-start = (bf16[2,1440,128]{2,1,0:T(8,128)(2,1)S(1)}, bf16[2,1440,128]{2,1,0:T(8,128)(2,1)}, u32[]{:S(2)}, u32[]{:S(2)}) collective-permute-start(bf16[2,1440,128]{2,1,0:T(8,128)(2,1)S(1)} %bitcast.145), channel_id=1, source_target_pairs={{0,8},{8,16},{16,24},{24,32},{32,40},{40,48},{48,56},{56,64},{64,7... | collective-permute-start | bytes 2211848 | tf_op jit(solution)/shard_map/ppermute | solution.py:23
  24.2 1.9 %collective-permute-start.1 = (bf16[2,1440,128]{2,1,0:T(8,128)(2,1)S(1)}, bf16[2,1440,128]{2,1,0:T(8,128)(2,1)}, u32[]{:S(2)}, u32[]{:S(2)}) collective-permute-start(bf16[2,1440,128]{2,1,0:T(8,128)(2,1)S(1)} %bitcast.146), channel_id=1, source_target_pairs={{8,0},{16,8},{24,16},{32,24},{40,32},{48,40},{56,48},{64,56},{72,6... | collective-permute-start | bytes 2211848 | tf_op jit(solution)/shard_map/ppermute | solution.py:24
  26.3 22.5 %multiply_convert_fusion.1 = (bf16[768,1440]{1,0:T(8,128)(2,1)}, bf16[768,1440]{1,0:T(8,128)(2,1)}) fusion(s32[768]{0:T(1024)S(1)} %copy-done.5, f32[768]{0:T(1024)S(1)} %get-tuple-element.93, f32[768]{0:T(1024)S(1)} %get-tuple-element.94), kind=kLoop, calls=%fused_computation.65 | loop fusion | flops 14376960 | bytes 4432896 | tf_op jit(solution)/shard_map/convert.4
  48.8 0.5 broadcast.84
  49.3 0.7 reduce.3
  50.1 6.9 %all-to-all-done = bf16[48,32,768]{2,1,0:T(8,128)(2,1)S(1)} async-done(((bf16[48,32,768]{2,1,0:T(8,128)(2,1)}), bf16[48,32,768]{2,1,0:T(8,128)(2,1)S(1)}, u32[]{:S(2)}, u32[]{:S(2)}) %all-to-all-start) | async-done | bytes 2359328 | tf_op jit(solution)/shard_map/all_to_all | solution.py:92
  57.0 1.6 %copy.18 = bf16[8,6,32,768]{3,2,0,1:T(8,128)(2,1)} copy(bf16[8,6,32,768]{3,2,1,0:T(8,128)(2,1)S(1)} %bitcast.140) | data formatting | bytes 4718592 | tf_op jit(solution)/shard_map/all_to_all | solution.py:92
  58.6 4.4 %fusion.124 = bf16[6,256,256]{1,2,0:T(8,128)(2,1)S(1)} fusion(bf16[6,256,768]{2,1,0:T(8,128)(2,1)} %bitcast.144, bf16[6,768,256]{2,1,0:T(8,128)(2,1)} %param.8, bf16[6,768]{1,0:T(8,128)(2,1)S(1)} %fusion.149, f32[256]{0:T(256)S(1)} %mul.651, s32[256]{0:T(256)S(1)} %fusion.155), kind=kOutput, calls=%fused_computation.232 | convolution fusion | flops 1211170816 | bytes 5516288 | tf_op jit(solution)/shard_map/slj,sjk->slk/dot_general | solution.py:103
  63.0 0.3 copy.20
  63.2 0.3 reshape.105
  63.5 0.4 copy.36
  64.0 1.4 copy.22
  65.4 13.0 %all-to-all-start.2 = ((bf16[6,128,512]{2,0,1:T(8,128)(2,1)}), bf16[6,128,512]{2,0,1:T(8,128)(2,1)S(1)}, u32[]{:S(2)}, u32[]{:S(2)}) async-start(bf16[6,128,512]{2,0,1:T(8,128)(2,1)} %copy.22), calls=%async_computation.2 | async-start | bytes 2097152 | tf_op jit(solution)/shard_map/all_to_all | solution.py:107
  78.4 1.7 %maximum_convert_fusion = f32[6,1440,128]{2,1,0:T(8,128)S(1)} fusion(bf16[2,1440,128]{2,1,0:T(8,128)(2,1)} %collective-permute-done.1, bf16[2,1440,128]{2,1,0:T(8,128)(2,1)S(1)} %bitcast.147, bf16[2,1440,128]{2,1,0:T(8,128)(2,1)} %collective-permute-done), kind=kLoop, calls=%fused_computation.114 | loop fusion | flops 3317760 | bytes 6635520 | tf_op jit(solution)/shard_map/convert_element_type | solution.py:90
  80.1 2.0 %copy-done.1 = f32[6,1440,128]{2,1,0:T(8,128)} copy-done((f32[6,1440,128]{2,1,0:T(8,128)}, f32[6,1440,128]{2,1,0:T(8,128)S(1)}, u32[]{:S(2)}) %copy-start.1) | copy-done | bytes 4423704
  82.1 15.8 %all-to-all-done.2 = bf16[6,128,512]{2,0,1:T(8,128)(2,1)S(1)} async-done(((bf16[6,128,512]{2,0,1:T(8,128)(2,1)}), bf16[6,128,512]{2,0,1:T(8,128)(2,1)S(1)}, u32[]{:S(2)}, u32[]{:S(2)}) %all-to-all-start.2) | async-done | bytes 786464 | tf_op jit(solution)/shard_map/all_to_all | solution.py:107
  97.8 0.4 reshape_reshape.3
  98.3 1.1 fusion.181
  99.4 0.6 copy-done.2
  99.9 4.2 %fusion.5 = f32[2880,256]{1,0:T(8,128)S(1)} fusion(bf16[768,1440]{1,0:T(8,128)(2,1)} %get-tuple-element.92, bf16[768,1440]{1,0:T(8,128)(2,1)S(1)} %copy-done.2, bf16[768,1,256]{2,1,0:T(2,128)(2,1)S(1)} %get-tuple-element.65), kind=kOutput, calls=%fused_computation.71 | convolution fusion | flops 1141309440 | bytes 7766016 | tf_op jit(solution)/shard_map/sq,sn->qn/dot_general | solution.py:114
  104.1 2.4 %fusion.6 = f32[2880,256]{1,0:T(8,128)S(1)} fusion(bf16[768,1440]{1,0:T(8,128)(2,1)S(1)} %copy-done.3, bf16[768,1440]{1,0:T(8,128)(2,1)S(1)} %copy-done.2, bf16[768,1,256]{2,1,0:T(2,128)(2,1)S(1)} %get-tuple-element.64), kind=kOutput, calls=%fused_computation.72 | convolution fusion | flops 1141309440 | bytes 7766016 | tf_op jit(solution)/shard_map/sq,sn->qn/dot_general | solution.py:114
  106.7 1.9 %fusion.116 = (f32[128]{0:T(128)S(1)}, f32[128]{0:T(128)S(1)}, f32[128]{0:T(128)S(1)}, f32[128]{0:T(128)S(1)}, f32[128]{0:T(128)S(1)}, /*index=5*/f32[128]{0:T(1...) fusion(f32[6,1440,128]{2,1,0:T(8,128)S(1)} %bitcast.139, ...), kind=kOutput, calls=%fused_computation.218 | convolution fusion | flops 101375104 | bytes 16305664 | tf_op jit(solution)/shard_map/rqd,cd->rqc/dot_general | solution.py:127
  108.6 1.9 %collective-permute-start.5 = (bf16[2,1440,128]{2,1,0:T(8,128)(2,1)S(1)}, bf16[2,1440,128]{2,1,0:T(8,128)(2,1)S(1)}, u32[]{:S(2)}, u32[]{:S(2)}) collective-permute-start(bf16[2,1440,128]{2,1,0:T(8,128)(2,1)S(1)} %get-tuple-element.95), channel_id=1, source_target_pairs={{0,8},{8,16},{16,24},{24,32},{32,40},{40,48},{48,56},{56,64},{64,7... | collective-permute-start | bytes 2211848 | tf_op jit(solution)/shard_map/ppermute | solution.py:23
  110.5 2.7 %collective-permute-start.6 = (bf16[2,1440,128]{2,1,0:T(8,128)(2,1)S(1)}, bf16[2,1440,128]{2,1,0:T(8,128)(2,1)S(1)}, u32[]{:S(2)}, u32[]{:S(2)}) collective-permute-start(bf16[2,1440,128]{2,1,0:T(8,128)(2,1)S(1)} %get-tuple-element.95), channel_id=1, source_target_pairs={{8,0},{16,8},{24,16},{32,24},{40,32},{48,40},{56,48},{64,56},{72,6... | collective-permute-start | bytes 2211848 | tf_op jit(solution)/shard_map/ppermute | solution.py:24
  113.2 3.4 %fusion.115 = (f32[128]{0:T(128)S(1)}, f32[128]{0:T(128)S(1)}, f32[128]{0:T(128)S(1)}, f32[128]{0:T(128)S(1)}, f32[128]{0:T(128)S(1)}, /*index=5*/f32[128]{0:T(1...) fusion(bf16[2,1440,128]{2,1,0:T(8,128)(2,1)S(1)} %get-tuple-element.95, f32[6,8,128]{2,1,0:T(8,128)S(1)} %get-tuple-element.62, ...), kind=kLoop, calls=%fused_computation.217 | loop fusion | flops 10320768 | bytes 5190144 | tf_op jit(solution)/shard_map/reduce_sum | solution.py:137
  116.6 5.3 %convolution_bitcast_fusion = f32[128,128]{0,1:T(8,128)S(1)} fusion(f32[2,1440,128]{2,1,0:T(8,128)S(1)} %get-tuple-element.59, f32[2,1440,128]{2,1,0:T(8,128)S(1)} %get-tuple-element.58, f32[6,1440,128]{2,1,0:T(8,128)S(1)} %bitcast.139, f32[128]{0:T(128)S(1)} %get-tuple-element.89, f32[128]{0:T(128)S(1)} %get-tuple-element.90, ...), kind=kOutput, calls=%fused_computation.234 | convolution fusion | flops 119808000 | bytes 15610368 | tf_op jit(solution)/shard_map/rqc,rqd->cd/dot_general | solution.py:130
  122.0 1.9 %fusion.112 = (f32[128]{0:T(128)S(1)}, f32[128]{0:T(128)S(1)}, f32[128]{0:T(128)S(1)}, f32[128]{0:T(128)S(1)}, f32[128]{0:T(128)S(1)}, /*index=5*/f32[128]{0:T(1...) fusion(bf16[2,1440,128]{2,1,0:T(8,128)(2,1)S(1)} %get-tuple-element.95, f32[6,1440,128]{2,1,0:T(8,128)S(1)} %bitcast.139, ...), kind=kLoop, calls=%fused_computation.214 | loop fusion | flops 10320768 | bytes 5190144 | tf_op jit(solution)/shard_map/reduce_sum | solution.py:137
  124.0 1.3 collective-permute-start.3
  125.3 0.8 collective-permute-start.4
  126.2 2.6 %collective-permute-done.3 = f32[128,153]{0,1:T(8,128)S(1)} collective-permute-done((f32[128,153]{0,1:T(8,128)S(1)}, f32[128,153]{0,1:T(8,128)S(1)}, u32[]{:S(2)}, u32[]{:S(2)}) %collective-permute-start.3) | collective-permute-done | bytes 78368 | tf_op jit(solution)/shard_map/ppermute | solution.py:39
  128.8 1.5 collective-permute-done.4
  130.4 0.3 maximum_convert_fusion.1
  130.8 1.2 fusion.23
  132.0 5.2 %collective-permute-start.7 = (f32[128,153]{0,1:T(8,128)S(1)}, f32[128,153]{0,1:T(8,128)S(1)}, u32[]{:S(2)}, u32[]{:S(2)}) collective-permute-start(f32[128,153]{0,1:T(8,128)S(1)} %add_bitcast_fusion.2), channel_id=1, source_target_pairs={{0,2},{1,3},{2,0},{3,1},{4,6},{5,7},{6,4},{7,5},{8,10},{9,11},{10,... | collective-permute-start | bytes 235016 | tf_op jit(solution)/shard_map/ppermute | solution.py:39
  137.1 2.4 %collective-permute-start.8 = (f32[128,153]{0,1:T(8,128)S(1)}, f32[128,153]{0,1:T(8,128)S(1)}, u32[]{:S(2)}, u32[]{:S(2)}) collective-permute-start(f32[128,153]{0,1:T(8,128)S(1)} %add_bitcast_fusion.2), channel_id=1, source_target_pairs={{0,4},{1,5},{2,6},{3,7},{4,0},{5,1},{6,2},{7,3},{8,12},{9,13},{10,... | collective-permute-start | bytes 235016 | tf_op jit(solution)/shard_map/ppermute | solution.py:39
  139.6 1.3 fusion.31
  140.9 2.8 %collective-permute-done.8 = f32[128,153]{0,1:T(8,128)S(1)} collective-permute-done((f32[128,153]{0,1:T(8,128)S(1)}, f32[128,153]{0,1:T(8,128)S(1)}, u32[]{:S(2)}, u32[]{:S(2)}) %collective-permute-start.8) | collective-permute-done | bytes 78368 | tf_op jit(solution)/shard_map/ppermute | solution.py:39
  143.7 2.0 %collective-permute-done.9 = f32[128,153]{0,1:T(8,128)S(1)} collective-permute-done((f32[128,153]{0,1:T(8,128)S(1)}, f32[128,153]{0,1:T(8,128)S(1)}, u32[]{:S(2)}, u32[]{:S(2)}) %collective-permute-start.9) | collective-permute-done | bytes 78368 | tf_op jit(solution)/shard_map/ppermute | solution.py:39
  146.0 3.8 %collective-permute-start.12 = (f32[128,153]{0,1:T(8,128)S(1)}, f32[128,153]{0,1:T(8,128)S(1)}, u32[]{:S(2)}, u32[]{:S(2)}) collective-permute-start(f32[128,153]{0,1:T(8,128)S(1)} %add_bitcast_fusion.1), channel_id=1, source_target_pairs={{0,96},{1,97},{2,98},{3,99},{4,100},{5,101},{6,102},{7,103},{8,104... | collective-permute-start | bytes 235016 | tf_op jit(solution)/shard_map/ppermute | solution.py:39
  149.8 1.1 fusion.40
  150.9 2.3 %collective-permute-done.12 = f32[128,153]{0,1:T(8,128)S(1)} collective-permute-done((f32[128,153]{0,1:T(8,128)S(1)}, f32[128,153]{0,1:T(8,128)S(1)}, u32[]{:S(2)}, u32[]{:S(2)}) %collective-permute-start.12) | collective-permute-done | bytes 78368 | tf_op jit(solution)/shard_map/ppermute | solution.py:39
  153.4 2.6 %fusion.18 = bf16[2,1440,128]{2,1,0:T(8,128)(2,1)} fusion(f32[6,1440,128]{2,1,0:T(8,128)S(1)} %maximum_convert_fusion.1, f32[2,1440,128]{2,1,0:T(8,128)S(1)} %fusion.40, f32[6,8,128]{2,1,0:T(8,128)S(1)} %get-tuple-element.61, f32[6,8,128]{2,1,0:T(8,128)S(1)} %get-tuple-element.60, f32[128]{0:T(128)S(1)} %get-tuple-element.89, f32[128]{0:T(128)S(1)} %get-tuple-element.90, ...), kind=kLoop, calls=%fused_computation.120 | loop fusion | flops 7741440 | bytes 8162816 | tf_op jit(solution)/shard_map/add | solution.py:149
  156.0 2.1 %collective-permute-done.13 = f32[128,153]{0,1:T(8,128)S(1)} collective-permute-done((f32[128,153]{0,1:T(8,128)S(1)}, f32[128,153]{0,1:T(8,128)S(1)}, u32[]{:S(2)}, u32[]{:S(2)}) %collective-permute-start.13) | collective-permute-done | bytes 78368 | tf_op jit(solution)/shard_map/ppermute | solution.py:39
  158.2 0.6 slice.531
  158.8 0.7 copy.23
  (52 shorter events, 1.2 us)
Async XLA Ops:
  0.6 106.1 %copy-start = (bf16[128,128]{1,0:T(8,128)(2,1)S(1)}, bf16[128,128]{1,0:T(8,128)(2,1)}, u32[]{:S(2)}) copy-start(bf16[128,128]{1,0:T(8,128)(2,1)} %param.15) | copy-start | bytes 98308
  16.1 3.8 %copy-start.4 = (bf16[2,128,1440]{1,2,0:T(8,128)(2,1)S(1)}, bf16[2,128,1440]{1,2,0:T(8,128)(2,1)}, u32[]{:S(2)}) copy-start(bf16[2,128,1440]{1,2,0:T(8,128)(2,1)} %param.13) | copy-start | bytes 2211844
  16.1 10.0 %copy-start.7 = (s32[48]{0:T(128)S(1)}, s32[48]{0:T(128)}, u32[]{:S(2)}) copy-start(s32[48]{0:T(128)} %param.12) | copy-start | bytes 580
  16.1 10.1 %copy-start.5 = (s32[768]{0:T(1024)S(1)}, s32[768]{0:T(1024)}, u32[]{:S(2)}) copy-start(s32[768]{0:T(1024)} %param.11) | copy-start | bytes 9220
  16.1 10.2 %copy-start.6 = (f32[128,25]{0,1:T(8,128)S(1)}, f32[128,25]{0,1:T(8,128)}, u32[]{:S(2)}) copy-start(f32[128,25]{0,1:T(8,128)} %param.14) | copy-start | bytes 38404
  16.1 40.8 %all-to-all-start = ((bf16[48,32,768]{2,1,0:T(8,128)(2,1)}), bf16[48,32,768]{2,1,0:T(8,128)(2,1)S(1)}, u32[]{:S(2)}, u32[]{:S(2)}) async-start(bf16[48,32,768]{2,1,0:T(8,128)(2,1)} %param.9), calls=%async_computation | async-start | bytes 4718592 | tf_op jit(solution)/shard_map/all_to_all | solution.py:92
  19.9 58.5 %collective-permute-start = (bf16[2,1440,128]{2,1,0:T(8,128)(2,1)S(1)}, bf16[2,1440,128]{2,1,0:T(8,128)(2,1)}, u32[]{:S(2)}, u32[]{:S(2)}) collective-permute-start(bf16[2,1440,128]{2,1,0:T(8,128)(2,1)S(1)} %bitcast.145), channel_id=1, source_target_pairs={{0,8},{8,16},{16,24},{24,32},{32,40},{40,48},{48,56},{56,64},{64,7... | collective-permute-start | bytes 2211848 | tf_op jit(solution)/shard_map/ppermute | solution.py:23
  24.2 54.2 %collective-permute-start.1 = (bf16[2,1440,128]{2,1,0:T(8,128)(2,1)S(1)}, bf16[2,1440,128]{2,1,0:T(8,128)(2,1)}, u32[]{:S(2)}, u32[]{:S(2)}) collective-permute-start(bf16[2,1440,128]{2,1,0:T(8,128)(2,1)S(1)} %bitcast.146), channel_id=1, source_target_pairs={{8,0},{16,8},{24,16},{32,24},{40,32},{48,40},{56,48},{64,56},{72,6... | collective-permute-start | bytes 2211848 | tf_op jit(solution)/shard_map/ppermute | solution.py:24
  65.4 32.4 %all-to-all-start.2 = ((bf16[6,128,512]{2,0,1:T(8,128)(2,1)}), bf16[6,128,512]{2,0,1:T(8,128)(2,1)S(1)}, u32[]{:S(2)}, u32[]{:S(2)}) async-start(bf16[6,128,512]{2,0,1:T(8,128)(2,1)} %copy.22), calls=%async_computation.2 | async-start | bytes 2097152 | tf_op jit(solution)/shard_map/all_to_all | solution.py:107
  80.0 2.0 %copy-start.1 = (f32[6,1440,128]{2,1,0:T(8,128)}, f32[6,1440,128]{2,1,0:T(8,128)S(1)}, u32[]{:S(2)}) copy-start(f32[6,1440,128]{2,1,0:T(8,128)S(1)} %maximum_convert_fusion) | copy-start | bytes 13271044
  98.3 1.7 %copy-start.2 = (bf16[768,1440]{1,0:T(8,128)(2,1)S(1)}, bf16[768,1440]{1,0:T(8,128)(2,1)}, u32[]{:S(2)}) copy-start(bf16[768,1440]{1,0:T(8,128)(2,1)} %get-tuple-element.91) | copy-start | bytes 6635524
  99.9 4.2 %copy-start.3 = (bf16[768,1440]{1,0:T(8,128)(2,1)S(1)}, bf16[768,1440]{1,0:T(8,128)(2,1)}, u32[]{:S(2)}) copy-start(bf16[768,1440]{1,0:T(8,128)(2,1)} %get-tuple-element.92) | copy-start | bytes 6635524
  99.9 6.8 %slice-start = ((s8[4423680]{0:T(1024)(128)(4,1)}), s8[4194304]{0:T(1024)(128)(4,1)S(1)}, s32[]{:S(2)}) async-start(s8[4423680]{0:T(1024)(128)(4,1)} %bitcast.138), calls=%async_computation.3 | async-start | bytes 8388608
  104.1 2.6 %slice-start.1 = ((s8[4423680]{0:T(1024)(128)(4,1)}), s8[229376]{0:T(1024)(128)(4,1)S(1)}, s32[]{:S(2)}) async-start(s8[4423680]{0:T(1024)(128)(4,1)} %bitcast.138), calls=%async_computation.4 | async-start | bytes 458752
  108.6 21.8 %collective-permute-start.5 = (bf16[2,1440,128]{2,1,0:T(8,128)(2,1)S(1)}, bf16[2,1440,128]{2,1,0:T(8,128)(2,1)S(1)}, u32[]{:S(2)}, u32[]{:S(2)}) collective-permute-start(bf16[2,1440,128]{2,1,0:T(8,128)(2,1)S(1)} %get-tuple-element.95), channel_id=1, source_target_pairs={{0,8},{8,16},{16,24},{24,32},{32,40},{40,48},{48,56},{56,64},{64,7... | collective-permute-start | bytes 2211848 | tf_op jit(solution)/shard_map/ppermute | solution.py:23
  110.5 19.9 %collective-permute-start.6 = (bf16[2,1440,128]{2,1,0:T(8,128)(2,1)S(1)}, bf16[2,1440,128]{2,1,0:T(8,128)(2,1)S(1)}, u32[]{:S(2)}, u32[]{:S(2)}) collective-permute-start(bf16[2,1440,128]{2,1,0:T(8,128)(2,1)S(1)} %get-tuple-element.95), channel_id=1, source_target_pairs={{8,0},{16,8},{24,16},{32,24},{40,32},{48,40},{56,48},{64,56},{72,6... | collective-permute-start | bytes 2211848 | tf_op jit(solution)/shard_map/ppermute | solution.py:24
  124.0 2.2 %collective-permute-start.2 = (f32[128,153]{0,1:T(8,128)S(1)}, f32[128,153]{0,1:T(8,128)S(1)}, u32[]{:S(2)}, u32[]{:S(2)}) collective-permute-start(f32[128,153]{0,1:T(8,128)S(1)} %concatenate.67), channel_id=1, source_target_pairs={{0,8},{1,9},{2,10},{3,11},{4,12},{5,13},{6,14},{7,15},{8,0},{9,1},... | collective-permute-start | bytes 235016 | tf_op jit(solution)/shard_map/ppermute | solution.py:39
  124.0 4.8 %collective-permute-start.3 = (f32[128,153]{0,1:T(8,128)S(1)}, f32[128,153]{0,1:T(8,128)S(1)}, u32[]{:S(2)}, u32[]{:S(2)}) collective-permute-start(f32[128,153]{0,1:T(8,128)S(1)} %concatenate.67), channel_id=1, source_target_pairs={{0,16},{1,17},{2,18},{3,19},{4,20},{5,21},{6,22},{7,23},{8,24},{9,... | collective-permute-start | bytes 235016 | tf_op jit(solution)/shard_map/ppermute | solution.py:39
  125.3 5.0 %collective-permute-start.4 = (f32[128,153]{0,1:T(8,128)S(1)}, f32[128,153]{0,1:T(8,128)S(1)}, u32[]{:S(2)}, u32[]{:S(2)}) collective-permute-start(f32[128,153]{0,1:T(8,128)S(1)} %concatenate.67), channel_id=1, source_target_pairs={{0,24},{1,25},{2,26},{3,27},{4,28},{5,29},{6,30},{7,31},{8,16},{9,... | collective-permute-start | bytes 235016 | tf_op jit(solution)/shard_map/ppermute | solution.py:39
  132.0 8.9 %collective-permute-start.7 = (f32[128,153]{0,1:T(8,128)S(1)}, f32[128,153]{0,1:T(8,128)S(1)}, u32[]{:S(2)}, u32[]{:S(2)}) collective-permute-start(f32[128,153]{0,1:T(8,128)S(1)} %add_bitcast_fusion.2), channel_id=1, source_target_pairs={{0,2},{1,3},{2,0},{3,1},{4,6},{5,7},{6,4},{7,5},{8,10},{9,11},{10,... | collective-permute-start | bytes 235016 | tf_op jit(solution)/shard_map/ppermute | solution.py:39
  137.1 6.6 %collective-permute-start.8 = (f32[128,153]{0,1:T(8,128)S(1)}, f32[128,153]{0,1:T(8,128)S(1)}, u32[]{:S(2)}, u32[]{:S(2)}) collective-permute-start(f32[128,153]{0,1:T(8,128)S(1)} %add_bitcast_fusion.2), channel_id=1, source_target_pairs={{0,4},{1,5},{2,6},{3,7},{4,0},{5,1},{6,2},{7,3},{8,12},{9,13},{10,... | collective-permute-start | bytes 235016 | tf_op jit(solution)/shard_map/ppermute | solution.py:39
  139.6 6.2 %collective-permute-start.9 = (f32[128,153]{0,1:T(8,128)S(1)}, f32[128,153]{0,1:T(8,128)S(1)}, u32[]{:S(2)}, u32[]{:S(2)}) collective-permute-start(f32[128,153]{0,1:T(8,128)S(1)} %add_bitcast_fusion.2), channel_id=1, source_target_pairs={{0,6},{1,7},{2,4},{3,5},{4,2},{5,3},{6,0},{7,1},{8,14},{9,15},{10,... | collective-permute-start | bytes 235016 | tf_op jit(solution)/shard_map/ppermute | solution.py:39
  145.8 5.1 %collective-permute-start.10 = (f32[128,153]{0,1:T(8,128)S(1)}, f32[128,153]{0,1:T(8,128)S(1)}, u32[]{:S(2)}, u32[]{:S(2)}) collective-permute-start(f32[128,153]{0,1:T(8,128)S(1)} %add_bitcast_fusion.1), channel_id=1, source_target_pairs={{0,32},{1,33},{2,34},{3,35},{4,36},{5,37},{6,38},{7,39},{8,40},{9,... | collective-permute-start | bytes 235016 | tf_op jit(solution)/shard_map/ppermute | solution.py:39
  145.9 5.0 %collective-permute-start.11 = (f32[128,153]{0,1:T(8,128)S(1)}, f32[128,153]{0,1:T(8,128)S(1)}, u32[]{:S(2)}, u32[]{:S(2)}) collective-permute-start(f32[128,153]{0,1:T(8,128)S(1)} %add_bitcast_fusion.1), channel_id=1, source_target_pairs={{0,64},{1,65},{2,66},{3,67},{4,68},{5,69},{6,70},{7,71},{8,72},{9,... | collective-permute-start | bytes 235016 | tf_op jit(solution)/shard_map/ppermute | solution.py:39
  146.0 7.2 %collective-permute-start.12 = (f32[128,153]{0,1:T(8,128)S(1)}, f32[128,153]{0,1:T(8,128)S(1)}, u32[]{:S(2)}, u32[]{:S(2)}) collective-permute-start(f32[128,153]{0,1:T(8,128)S(1)} %add_bitcast_fusion.1), channel_id=1, source_target_pairs={{0,96},{1,97},{2,98},{3,99},{4,100},{5,101},{6,102},{7,103},{8,104... | collective-permute-start | bytes 235016 | tf_op jit(solution)/shard_map/ppermute | solution.py:39
  153.3 4.9 %collective-permute-start.13 = (f32[128,153]{0,1:T(8,128)S(1)}, f32[128,153]{0,1:T(8,128)S(1)}, u32[]{:S(2)}, u32[]{:S(2)}) collective-permute-start(f32[128,153]{0,1:T(8,128)S(1)} %add_bitcast_fusion), channel_id=1, source_target_pairs={{0,1},{1,0},{2,3},{3,2},{4,5},{5,4},{6,7},{7,6},{8,9},{9,8},{10,11... | collective-permute-start | bytes 235016 | tf_op jit(solution)/shard_map/ppermute | solution.py:39
